TPU v7x, 256 devices: a whole 4x4x8 slice. The times are simulated.
256 devices in a mesh: grp: 8 (over x, core), cell: 32 (over y, z).
Axes of the slice: x: 4, y: 4, z: 8, core: 2. Of those that a mesh axis runs over, the one named last changes fastest.
Arguments:
- rhs: float32 [128, 2, 128, 16, 128], P('grp', None, 'cell'), may hold values from -8 to 8
- log_perm: float32 [128, 128, 16, 128], P('grp', 'cell'), may hold values from -1.5 to 1.5
- porosity: float32 [128, 128, 16, 128], P('grp', 'cell'), may hold values from 0.1 to 0.3
- saturation: float32 [128, 128, 16, 128], P('grp', 'cell'), may hold values from 0.2 to 0.8
- pressure: float32 [128, 128, 16, 128], P('grp', 'cell'), may hold values from -6 to 6
- obs_values: float32 [256], replicated, may hold values from -6 to 6
- obs_error: float32 [256], replicated, may hold values from 0.1 to 1
- noise: float32 [128, 256], replicated, may hold values from -6 to 6
- well_cell: int32 [128], replicated, may hold values from 0 to 262143
- obs_well: int32 [256], replicated, may hold values from 0 to 127
Outputs:
- increment: float32 [128, 2, 128, 16, 128], P('grp', None, 'cell')
- log_perm_post: float32 [128, 128, 16, 128], P('grp', 'cell')
- porosity_post: float32 [128, 128, 16, 128], P('grp', 'cell')
All inputs are finite; a program needn't handle non-finite values.
Results may differ from a plain program's by a relative error of at most 0.0003.
Values sent between devices are 32-bit elements; how exact they have to be, the bound alone decides.
No kernel may reach another device: no remote copies, remote signals or barrier semaphores. Data moves between devices by JAX's collectives and lax.ppermute only.
A program may use at most 128 MiB of HBM per device.

v0:
```python
import math

import jax
import jax.numpy as jnp
from jax import lax
from jax.sharding import PartitionSpec as P

KRYLOV = 4


epsilon = 1e-06
time_step = 0.1
compress = 0.5
inflation = 4.0


def with_halo(block, sides, width):
    for axis, dim in sides:
        count = lax.axis_size(axis)
        forward = [(i, i + 1) for i in range(count - 1)]
        backward = [(target, source) for source, target in forward]
        low = lax.ppermute(
            lax.slice_in_dim(block, block.shape[dim] - width, None, axis=dim), axis, forward
        )
        high = lax.ppermute(lax.slice_in_dim(block, 0, width, axis=dim), axis, backward)
        block = jnp.concatenate([low, block, high], axis=dim)
    return block


def mobility(sat_field):
    return sat_field * sat_field + 0.5 * (1.0 - sat_field) * (1.0 - sat_field)


def face_pair(perm_low, perm_high, sat_low, sat_high):
    trans = (
        2.0
        * perm_low
        * perm_high
        / (perm_low + perm_high)
        * (0.5 * (mobility(sat_low) + mobility(sat_high)))
    )
    return (trans, trans * (0.5 * (sat_low + sat_high)))


def plane_faces(perm, sat_field):
    plane_rows = perm.shape[-2]
    plane_cols = perm.shape[-1]
    keep_rows = (
        lax.broadcasted_iota(jnp.int32, (plane_rows, plane_cols), 0) < plane_rows - 1
    ).astype(jnp.float32)
    keep_cols = (
        lax.broadcasted_iota(jnp.int32, (plane_rows, plane_cols), 1) < plane_cols - 1
    ).astype(jnp.float32)
    trans_y, frac_y = face_pair(
        perm, jnp.roll(perm, -1, -2), sat_field, jnp.roll(sat_field, -1, -2)
    )
    trans_z, frac_z = face_pair(
        perm, jnp.roll(perm, -1, -1), sat_field, jnp.roll(sat_field, -1, -1)
    )
    return (trans_y * keep_rows, frac_y * keep_rows, trans_z * keep_cols, frac_z * keep_cols)


def operator(padded, second, coeffs):
    accum, trans_x, frac_x, trans_y, frac_y, trans_z, frac_z = coeffs
    first = padded[..., 1:-1, :, :]
    diff_x = padded[..., 1:, :, :] - padded[..., :-1, :, :]
    diff_y = jnp.roll(first, -1, -2) - first
    diff_z = jnp.roll(first, -1, -1) - first

    def net(coef_x, coef_y, coef_z):
        flow_x = coef_x * diff_x
        flow_y = coef_y * diff_y
        flow_z = coef_z * diff_z
        return (
            flow_x[..., :-1, :, :]
            - flow_x[..., 1:, :, :]
            + (jnp.roll(flow_y, 1, -2) - flow_y)
            + (jnp.roll(flow_z, 1, -1) - flow_z)
        )

    out_pressure = accum * (compress * first + 0.5 * second) + net(trans_x, trans_y, trans_z)
    out_water = accum * second + net(frac_x, frac_y, frac_z)
    return (out_pressure, out_water)


def least_squares(columns, beta):
    rows = [list(column) for column in columns]
    cosines = []
    sines = []
    target = [beta] + [jnp.zeros_like(beta) for column in columns]
    for jdx in range(len(rows)):
        column = rows[jdx]
        for idx in range(jdx):
            upper = cosines[idx] * column[idx] + sines[idx] * column[idx + 1]
            column[idx + 1] = -sines[idx] * column[idx] + cosines[idx] * column[idx + 1]
            column[idx] = upper
        radius = jnp.sqrt(column[jdx] * column[jdx] + column[jdx + 1] * column[jdx + 1])
        cosines.append(column[jdx] / radius)
        sines.append(column[jdx + 1] / radius)
        column[jdx] = radius
        target[jdx + 1] = -sines[jdx] * target[jdx]
        target[jdx] = cosines[jdx] * target[jdx]
    count = len(rows)
    solved = [None] * count
    for jdx in reversed(range(count)):
        partial_sum = target[jdx]
        for idx in range(jdx + 1, count):
            partial_sum = partial_sum - rows[idx][jdx] * solved[idx]
        solved[jdx] = partial_sum / rows[jdx][jdx]
    return solved


def ensemble_weights(predicted, obs_values, obs_error, noise):
    members = predicted.shape[0]
    sigma = math.sqrt(inflation) * obs_error
    center = jnp.mean(predicted, axis=0)
    spread = (predicted - center) / (math.sqrt(members - 1.0) * sigma)
    innov = (obs_values + sigma * noise - predicted) / sigma
    gram = jnp.eye(members, dtype=jnp.float32) + jnp.dot(
        spread, spread.T, precision=lax.Precision.HIGHEST, preferred_element_type=jnp.float32
    )
    cross = jnp.dot(
        spread, innov.T, precision=lax.Precision.HIGHEST, preferred_element_type=jnp.float32
    )
    factor = jnp.linalg.cholesky(gram)
    return jax.scipy.linalg.cho_solve((factor, True), cross)


def expand(values):
    return values[:, None, None, None, None]


def inner(left, right):
    return jnp.sum(left * right, axis=(1, 2, 3, 4))


def local(
    rhs, log_perm, porosity, saturation, pressure, obs_values, obs_error, noise, well_cell, obs_well
):
    local_members, slab_x, plane_rows, plane_cols = log_perm.shape
    members = noise.shape[0]
    plane = plane_rows * plane_cols
    cells_dev = slab_x * plane
    slab_index = lax.axis_index("cell")
    slab_count = lax.axis_size("cell")
    stacked = jnp.stack([log_perm, saturation], axis=1)
    rimmed = with_halo(stacked, (("cell", 2),), 1)
    perm_pad = jnp.exp(rimmed[:, 0])
    sat_pad = rimmed[:, 1]
    trans_x, frac_x = face_pair(perm_pad[:, :-1], perm_pad[:, 1:], sat_pad[:, :-1], sat_pad[:, 1:])
    face_pos = lax.broadcasted_iota(jnp.int32, (slab_x + 1, 1, 1), 0)
    keep_face = jnp.where(
        face_pos == 0,
        slab_index > 0,
        jnp.where(face_pos == slab_x, slab_index < slab_count - 1, True),
    ).astype(jnp.float32)
    trans_x = trans_x * keep_face
    frac_x = frac_x * keep_face
    trans_y, frac_y, trans_z, frac_z = plane_faces(perm_pad[:, 1:-1], saturation)
    coeffs = (porosity / time_step, trans_x, frac_x, trans_y, frac_y, trans_z, frac_z)
    columns = []
    beta = jnp.sqrt(lax.psum(inner(rhs, rhs), "cell") + epsilon)
    basis = [rhs / expand(beta)]
    for jdx in range(KRYLOV):
        vector = basis[jdx]
        padded = with_halo(vector[:, 0], (("cell", 1),), 1)
        out_pressure, out_water = operator(padded, vector[:, 1], coeffs)
        image = jnp.stack([out_pressure, out_water], 1)
        local_dots = jnp.stack([inner(basis[idx], image) for idx in range(jdx + 1)], 0)
        projected = lax.psum(local_dots, "cell")
        for idx in range(jdx + 1):
            image = image - expand(projected[idx]) * basis[idx]
        height = jnp.sqrt(lax.psum(inner(image, image), "cell") + epsilon)
        columns.append([projected[idx] for idx in range(jdx + 1)] + [height])
        basis.append(image / expand(height))
    solved = least_squares(columns, beta)
    increment = expand(solved[0]) * basis[0]
    for jdx in range(1, KRYLOV):
        increment = increment + expand(solved[jdx]) * basis[jdx]
    flat = jnp.stack([pressure + increment[:, 0], saturation + increment[:, 1]], 1).reshape(
        local_members, 2 * cells_dev
    )
    cells = jnp.take(well_cell, obs_well)
    wells = well_cell.shape[0]
    component = (jnp.arange(obs_well.shape[0], dtype=jnp.int32) >= wells).astype(jnp.int32)
    slab_row = cells // plane - slab_index * slab_x
    inside = (slab_row >= 0) & (slab_row < slab_x)
    local_cell = jnp.where(inside, slab_row * plane + cells % plane, 0)
    picked = jnp.take(flat, component * cells_dev + local_cell, axis=1) * inside.astype(jnp.float32)
    slab_pred = lax.psum(picked, "cell")
    predicted = lax.all_gather(slab_pred, "grp", axis=0, tiled=True)
    weights = ensemble_weights(predicted, obs_values, obs_error, noise)
    params = jnp.stack([log_perm, porosity], 1).reshape(local_members, 2 * cells_dev)
    offset = lax.axis_index("grp") * local_members
    scale_factor = 1.0 / math.sqrt(members - 1.0)
    scaled = params * scale_factor
    own_columns = lax.dynamic_slice_in_dim(weights, offset, local_members, 1)
    update = jnp.dot(
        own_columns.T,
        lax.all_gather(scaled, "grp", axis=0, tiled=True),
        precision=lax.Precision.HIGHEST,
        preferred_element_type=jnp.float32,
    )
    posterior = params + update
    posterior = posterior.reshape(local_members, 2, slab_x, plane_rows, plane_cols)
    return (increment, posterior[:, 0], posterior[:, 1])


def solution(mesh):
    in_specs = (
        P("grp", None, "cell", None, None),
        P("grp", "cell", None, None),
        P("grp", "cell", None, None),
        P("grp", "cell", None, None),
        P("grp", "cell", None, None),
        P(),
        P(),
        P(),
        P(),
        P(),
    )
    out_specs = (
        P("grp", None, "cell", None, None),
        P("grp", "cell", None, None),
        P("grp", "cell", None, None),
    )
    return jax.shard_map(local, mesh=mesh, in_specs=in_specs, out_specs=out_specs, check_vma=False)
```

profile of v0, /device:TPU:1, one launch (start us, length us, event | category | flops | bytes accessed | tf_op | source)
XLA Modules:
  0.0 937.8 jit_solution(11814738720340162796)
XLA Ops:
  7.2 2.0 fusion.61
  9.3 4.5 collective-permute-start
  14.0 1.3 collective-permute-start.1
  15.3 64.8 %psum.70 = f32[16]{0:T(128)S(1)} all-reduce(f32[16]{0:T(128)S(1)} %multiply_reduce_fusion.14), channel_id=1, replica_groups=mesh['grp'=8,'cell'=32] {'cell'}, use_global_device_ids=true, to_apply=%region_1.2 | all-reduce | flops 16 | bytes 128 | tf_op jit(solution)/shard_map/psum | solution.py:162
  81.0 1.3 collective-permute-start.2
  82.3 4.7 collective-permute-start.3
  87.1 1.0 copy-done.22
  88.1 1.7 bitcast_multiply_fusion
  89.9 1.9 gather_fusion
  91.9 0.8 slice.516
  92.7 1.0 slice.522
  93.7 0.9 slice.402
  94.6 1.0 slice.410
  95.7 1.1 pad_maximum_fusion
  98.5 1.1 multiply_multiply_fusion.11
  99.6 1.6 fusion.100
  101.7 2.7 fusion.60
  106.6 55.7 %psum.71 = f32[16]{0:T(128)S(1)} all-reduce(f32[16]{0:T(128)S(1)} %multiply_reduce_fusion.13), channel_id=1, replica_groups=mesh['grp'=8,'cell'=32] {'cell'}, use_global_device_ids=true, to_apply=%region_3.4 | all-reduce | flops 16 | bytes 128 | tf_op jit(solution)/shard_map/psum | solution.py:170
  162.3 1.6 multiply_reduce_fusion.12
  163.9 57.9 %psum.72 = f32[16]{0:T(128)S(1)} all-reduce(f32[16]{0:T(128)S(1)} %get-tuple-element.23), channel_id=1, replica_groups=mesh['grp'=8,'cell'=32] {'cell'}, use_global_device_ids=true, to_apply=%region_5.6 | all-reduce | flops 16 | bytes 128 | tf_op jit(solution)/shard_map/psum | solution.py:173
  222.3 1.4 collective-permute-start.4
  223.7 4.0 collective-permute-start.5
  228.8 0.8 collective-permute-done.5
  232.0 57.7 %psum.73 = f32[2,16]{1,0:T(2,128)S(1)} all-reduce(f32[2,16]{1,0:T(2,128)S(1)} %pad_maximum_fusion.14), channel_id=1, replica_groups=mesh['grp'=8,'cell'=32] {'cell'}, use_global_device_ids=true, to_apply=%region_8.9 | all-reduce | flops 32 | bytes 256 | tf_op jit(solution)/shard_map/psum | solution.py:170
  289.7 1.7 multiply_reduce_fusion.9
  291.4 55.7 %psum.74 = f32[16]{0:T(128)S(1)} all-reduce(f32[16]{0:T(128)S(1)} %get-tuple-element.21), channel_id=1, replica_groups=mesh['grp'=8,'cell'=32] {'cell'}, use_global_device_ids=true, to_apply=%region_10.11 | all-reduce | flops 16 | bytes 128 | tf_op jit(solution)/shard_map/psum | solution.py:173
  347.6 1.4 collective-permute-start.6
  349.0 4.2 collective-permute-start.7
  357.6 57.3 %psum.75 = f32[3,16]{1,0:T(4,128)S(1)} all-reduce(f32[3,16]{1,0:T(4,128)S(1)} %pad_maximum_fusion.12), channel_id=1, replica_groups=mesh['grp'=8,'cell'=32] {'cell'}, use_global_device_ids=true, to_apply=%region_14.15 | all-reduce | flops 48 | bytes 384 | tf_op jit(solution)/shard_map/psum | solution.py:170
  414.9 2.7 multiply_reduce_fusion.5
  417.6 56.2 %psum.76 = f32[16]{0:T(128)S(1)} all-reduce(f32[16]{0:T(128)S(1)} %get-tuple-element.19), channel_id=1, replica_groups=mesh['grp'=8,'cell'=32] {'cell'}, use_global_device_ids=true, to_apply=%region_16.17 | all-reduce | flops 16 | bytes 128 | tf_op jit(solution)/shard_map/psum | solution.py:173
  473.8 1.4 copy_divide_fusion
  475.6 1.4 collective-permute-start.8
  477.0 4.1 collective-permute-start.9
  482.3 0.8 collective-permute-done.9
  486.2 57.4 %psum.77 = f32[4,16]{1,0:T(4,128)S(1)} all-reduce(f32[4,16]{1,0:T(4,128)S(1)} %pad_maximum_fusion.13), channel_id=1, replica_groups=mesh['grp'=8,'cell'=32] {'cell'}, use_global_device_ids=true, to_apply=%region_21.22 | all-reduce | flops 64 | bytes 512 | tf_op jit(solution)/shard_map/psum | solution.py:170
  543.6 2.2 multiply_reduce_fusion
  545.8 56.0 %psum.78 = f32[16]{0:T(128)S(1)} all-reduce(f32[16]{0:T(128)S(1)} %multiply_reduce_fusion), channel_id=1, replica_groups=mesh['grp'=8,'cell'=32] {'cell'}, use_global_device_ids=true, to_apply=%region_23.24 | all-reduce | flops 16 | bytes 128 | tf_op jit(solution)/shard_map/psum | solution.py:173
  602.0 1.8 multiply_add_fusion
  604.0 0.8 copy-done.43
  604.9 4.6 copy.101
  609.5 4.1 gather_fusion.1
  613.8 111.5 %psum.79 = f32[16,256]{0,1:T(8,128)S(1)} all-reduce(f32[16,256]{0,1:T(8,128)S(1)} %multiply_bitcast_fusion), channel_id=1, replica_groups=mesh['grp'=8,'cell'=32] {'cell'}, use_global_device_ids=true, to_apply=%region_24.25 | all-reduce | flops 4096 | bytes 32768 | tf_op jit(solution)/shard_map/psum | solution.py:190
  725.3 173.0 %all_gather.6 = f32[128,256]{1,0:T(8,128)S(1)} all-gather(f32[16,256]{1,0:T(8,128)S(1)} %copy.102), channel_id=1, replica_groups=mesh['grp'=8,'cell'=32] {'grp'}, dimensions={0}, use_global_device_ids=true | all-gather | bytes 147456 | tf_op jit(solution)/shard_map/all_gather | solution.py:191
  898.8 11.7 %cholesky.17 = f32[128,128]{1,0:T(8,128)S(1)} custom-call(f32[128,128]{1,0:T(8,128)S(1)} %fusion.78), custom_call_target="Cholesky" | custom-call | tf_op jit(solution)/shard_map/jit(cholesky)/cholesky | solution.py:125
  911.8 9.8 %custom-call.10 = f32[1,128,128]{1,2,0:T(8,128)S(1)} custom-call(f32[1,128,128]{2,1,0:T(8,128)S(1)} %fusion.72), custom_call_target="InvertDiagBlocksLowerTriangular" | custom-call | tf_op jit(solution)/shard_map/jit(_cho_solve)/triangular_solve | solution.py:126
  922.6 7.1 fusion
  929.9 1.1 slice_bitcast_fusion.1
  (204 shorter events, 22.2 us)
Async XLA Ops:
  7.2 82.7 %copy-start = (s32[128]{0:T(128)S(1)}, s32[128]{0:T(128)}, u32[]{:S(2)}) copy-start(s32[128]{0:T(128)} %param.18) | copy-start | bytes 1540
  7.2 6.6 copy-start.2
  7.2 915.4 %all-gather.2.cloned.1.call-start = ((), (), s32[]{:S(2)}) async-start(), calls=%async_computation | async-start | bytes 9437184 | tf_op jit(solution)/shard_map/all_gather | solution.py:200
  9.3 77.7 %copy-start.5 = (f32[16,4,16,128]{3,2,1,0:T(8,128)S(1)}, f32[16,4,16,128]{3,2,1,0:T(8,128)}, u32[]{:S(2)}) copy-start(f32[16,4,16,128]{3,2,1,0:T(8,128)} %param.12) | copy-start | bytes 1572868
  9.3 77.7 %copy-start.37 = (f32[16,4,16,128]{3,2,1,0:T(8,128)S(1)}, f32[16,4,16,128]{3,2,1,0:T(8,128)}, u32[]{:S(2)}) copy-start(f32[16,4,16,128]{3,2,1,0:T(8,128)} %param.11) | copy-start | bytes 1572868
  9.3 86.4 %collective-permute-start = (f32[16,2,1,16,128]{4,3,2,0,1:T(8,128)}, f32[16,2,1,16,128]{4,3,2,0,1:T(8,128)S(1)}, u32[]{:S(2)}, u32[]{:S(2)}) collective-permute-start(f32[16,2,1,16,128]{4,3,2,0,1:T(8,128)} %get-tuple-element.67), channel_id=1, source_target_pairs={{0,1},{1,2},{2,3},{3,4},{4,5},{5,6},{6,7},{7,8},{8,9},{9,10},{10,1... | collective-permute-start | bytes 786440 | tf_op jit(solution)/shard_map/ppermute | solution.py:22
  14.0 81.7 %collective-permute-start.1 = (f32[16,2,1,16,128]{4,3,2,0,1:T(8,128)}, f32[16,2,1,16,128]{4,3,2,0,1:T(8,128)}, u32[]{:S(2)}, u32[]{:S(2)}) collective-permute-start(f32[16,2,1,16,128]{4,3,2,0,1:T(8,128)} %get-tuple-element.68), channel_id=1, source_target_pairs={{1,0},{2,1},{3,2},{4,3},{5,4},{6,5},{7,6},{8,7},{9,8},{10,9},{11,1... | collective-permute-start | bytes 786440 | tf_op jit(solution)/shard_map/ppermute | solution.py:25
  81.0 20.7 %collective-permute-start.2 = (f32[16,1,16,128]{3,2,1,0:T(8,128)}, f32[16,1,16,128]{3,2,1,0:T(8,128)}, u32[]{:S(2)}, u32[]{:S(2)}) collective-permute-start(f32[16,1,16,128]{3,2,1,0:T(8,128)} %get-tuple-element.81), channel_id=1, source_target_pairs={{1,0},{2,1},{3,2},{4,3},{5,4},{6,5},{7,6},{8,7},{9,8},{10,9},{11,1... | collective-permute-start | bytes 393224 | tf_op jit(solution)/shard_map/ppermute | solution.py:25
  82.3 19.4 %collective-permute-start.3 = (f32[16,1,16,128]{3,2,1,0:T(8,128)}, f32[16,1,16,128]{3,2,1,0:T(8,128)}, u32[]{:S(2)}, u32[]{:S(2)}) collective-permute-start(f32[16,1,16,128]{3,2,1,0:T(8,128)} %get-tuple-element.82), channel_id=1, source_target_pairs={{0,1},{1,2},{2,3},{3,4},{4,5},{5,6},{6,7},{7,8},{8,9},{9,10},{10,1... | collective-permute-start | bytes 393224 | tf_op jit(solution)/shard_map/ppermute | solution.py:22
  88.1 1.8 copy-start.45
  89.9 3.8 copy-start.3
  92.7 2.9 copy-start.46
  96.9 1.2 copy-start.32
  97.0 1.3 copy-start.33
  97.0 1.5 copy-start.34
  99.6 1.6 copy-start.12
  99.6 128.1 %copy-start.9 = (f32[16,4,16,128]{3,2,1,0:T(8,128)}, f32[16,4,16,128]{3,2,1,0:T(8,128)S(1)}, u32[]{:S(2)}) copy-start(f32[16,4,16,128]{3,2,1,0:T(8,128)S(1)} %get-tuple-element.26) | copy-start | bytes 1572868
  221.9 5.8 copy-start.13
  222.0 5.8 copy-start.24
  222.0 5.8 copy-start.27
  222.3 6.5 collective-permute-start.4
  223.7 5.9 collective-permute-start.5
  228.3 1.3 copy-start.16
  228.3 1.3 copy-start.19
  347.2 6.0 copy-start.10
  347.2 6.0 copy-start.14
  347.2 6.0 copy-start.25
  347.2 6.0 copy-start.28
  347.6 6.8 collective-permute-start.6
  349.0 6.0 collective-permute-start.7
  353.9 1.3 copy-start.20
  354.4 1.1 copy-start.6
  475.3 5.9 copy-start.11
  475.3 5.9 copy-start.15
  475.3 5.9 copy-start.26
  475.3 5.9 copy-start.29
  475.6 6.7 collective-permute-start.8
  477.0 6.1 collective-permute-start.9
  481.8 1.3 copy-start.18
  481.8 1.3 copy-start.21
  482.3 1.1 copy-start.7
  484.0 1.4 copy-start.8
  601.9 1.8 copy-start.4
  601.9 1.8 copy-start.44
  609.5 312.2 %copy-start.47 = (f32[128,256]{1,0:T(8,128)S(1)}, f32[128,256]{1,0:T(8,128)}, u32[]{:S(2)}) copy-start(f32[128,256]{1,0:T(8,128)} %param.17) | copy-start | bytes 393220
  609.5 312.2 %copy-start.48 = (f32[256]{0:T(256)S(1)}, f32[256]{0:T(256)}, u32[]{:S(2)}) copy-start(f32[256]{0:T(256)} %param.15) | copy-start | bytes 3076
  613.8 308.8 %copy-start.23 = (f32[16,2,4,16,128]{4,3,2,1,0:T(8,128)S(1)}, f32[16,2,4,16,128]{4,3,2,1,0:T(8,128)}, u32[]{:S(2)}) copy-start(f32[16,2,4,16,128]{4,3,2,1,0:T(8,128)} %copy-done.22) | copy-start | bytes 3145732
  929.7 1.3 copy-start.1
  (12 other events, 10.5 us)
Sparse Core Ops, SparseCore 0:
  89.9 61.6 all-gather.1
where the time goes:
time: 939 us; the launch traced here: 938 us
  blocking collectives  803 us (86%)
  other arithmetic  54.4 us (6%)
  starting transfers between devices  28.3 us (3%)
  local copies, waits for them, and re-layouts  26.2 us (3%)
  between operations  15.2 us (2%)
    psum x4, blocking collectives, local(): projected = lax.psum(local_dots, 'cell')  228 us
    psum x4, blocking collectives, local(): height = jnp.sqrt(lax.psum(inner(image, image), 'cell') + epsilon)  226 us
    all_gather x1, blocking collectives, local(): predicted = lax.all_gather(slab_pred, 'grp', axis=0, tiled=True)  173 us
    psum x1, blocking collectives, local(): slab_pred = lax.psum(picked, 'cell')  111 us
    psum x1, blocking collectives, local(): beta = jnp.sqrt(lax.psum(inner(rhs, rhs), 'cell') + epsilon)  64.8 us
    ppermute x5, starting transfers between devices, with_halo(): lax.ppermute(lax.slice_in_dim(block, block.shape[dim] - width, None, axis...  21.5 us
  transfers between devices with their start and end apart: 11, of which 3 were waited for; matrix products, arithmetic and copies ran while one was open for 8% of the time, Pallas kernels for 0%

commit v1 on v0

--- a/solution.py
+++ b/solution.py
@@ -3,6 +3,7 @@
 import jax
 import jax.numpy as jnp
 from jax import lax
+from jax.sharding import Mesh
 from jax.sharding import PartitionSpec as P
 
 KRYLOV = 4
@@ -14,9 +15,16 @@
 inflation = 4.0
 
 
+CELL = ("cy", "cz")
+
+
+def cell_sum(values):
+    return lax.psum(lax.psum(values, "cz"), "cy")
+
+
 def with_halo(block, sides, width):
     for axis, dim in sides:
-        count = lax.axis_size(axis)
+        count = lax.axis_size(axis[0]) * lax.axis_size(axis[1])
         forward = [(i, i + 1) for i in range(count - 1)]
         backward = [(target, source) for source, target in forward]
         low = lax.ppermute(
@@ -141,10 +149,10 @@
     members = noise.shape[0]
     plane = plane_rows * plane_cols
     cells_dev = slab_x * plane
-    slab_index = lax.axis_index("cell")
-    slab_count = lax.axis_size("cell")
+    slab_index = lax.axis_index("cy") * lax.axis_size("cz") + lax.axis_index("cz")
+    slab_count = lax.axis_size("cy") * lax.axis_size("cz")
     stacked = jnp.stack([log_perm, saturation], axis=1)
-    rimmed = with_halo(stacked, (("cell", 2),), 1)
+    rimmed = with_halo(stacked, ((CELL, 2),), 1)
     perm_pad = jnp.exp(rimmed[:, 0])
     sat_pad = rimmed[:, 1]
     trans_x, frac_x = face_pair(perm_pad[:, :-1], perm_pad[:, 1:], sat_pad[:, :-1], sat_pad[:, 1:])
@@ -159,18 +167,18 @@
     trans_y, frac_y, trans_z, frac_z = plane_faces(perm_pad[:, 1:-1], saturation)
     coeffs = (porosity / time_step, trans_x, frac_x, trans_y, frac_y, trans_z, frac_z)
     columns = []
-    beta = jnp.sqrt(lax.psum(inner(rhs, rhs), "cell") + epsilon)
+    beta = jnp.sqrt(cell_sum(inner(rhs, rhs)) + epsilon)
     basis = [rhs / expand(beta)]
     for jdx in range(KRYLOV):
         vector = basis[jdx]
-        padded = with_halo(vector[:, 0], (("cell", 1),), 1)
+        padded = with_halo(vector[:, 0], ((CELL, 1),), 1)
         out_pressure, out_water = operator(padded, vector[:, 1], coeffs)
         image = jnp.stack([out_pressure, out_water], 1)
         local_dots = jnp.stack([inner(basis[idx], image) for idx in range(jdx + 1)], 0)
-        projected = lax.psum(local_dots, "cell")
+        projected = cell_sum(local_dots)
         for idx in range(jdx + 1):
             image = image - expand(projected[idx]) * basis[idx]
-        height = jnp.sqrt(lax.psum(inner(image, image), "cell") + epsilon)
+        height = jnp.sqrt(cell_sum(inner(image, image)) + epsilon)
         columns.append([projected[idx] for idx in range(jdx + 1)] + [height])
         basis.append(image / expand(height))
     solved = least_squares(columns, beta)
@@ -187,7 +195,7 @@
     inside = (slab_row >= 0) & (slab_row < slab_x)
     local_cell = jnp.where(inside, slab_row * plane + cells % plane, 0)
     picked = jnp.take(flat, component * cells_dev + local_cell, axis=1) * inside.astype(jnp.float32)
-    slab_pred = lax.psum(picked, "cell")
+    slab_pred = cell_sum(picked)
     predicted = lax.all_gather(slab_pred, "grp", axis=0, tiled=True)
     weights = ensemble_weights(predicted, obs_values, obs_error, noise)
     params = jnp.stack([log_perm, porosity], 1).reshape(local_members, 2 * cells_dev)
@@ -206,13 +214,21 @@
     return (increment, posterior[:, 0], posterior[:, 1])
 
 
+def split_mesh(mesh):
+    devices = mesh.devices
+    groups, slabs = devices.shape
+    along_z = len({device.coords[2] for device in devices[0]})
+    return Mesh(devices.reshape(groups, slabs // along_z, along_z), ("grp", "cy", "cz"))
+
+
 def solution(mesh):
+    mesh = split_mesh(mesh)
     in_specs = (
-        P("grp", None, "cell", None, None),
-        P("grp", "cell", None, None),
-        P("grp", "cell", None, None),
-        P("grp", "cell", None, None),
-        P("grp", "cell", None, None),
+        P("grp", None, CELL, None, None),
+        P("grp", CELL, None, None),
+        P("grp", CELL, None, None),
+        P("grp", CELL, None, None),
+        P("grp", CELL, None, None),
         P(),
         P(),
         P(),
@@ -220,8 +236,8 @@
         P(),
     )
     out_specs = (
-        P("grp", None, "cell", None, None),
-        P("grp", "cell", None, None),
-        P("grp", "cell", None, None),
+        P("grp", None, CELL, None, None),
+        P("grp", CELL, None, None),
+        P("grp", CELL, None, None),
     )
     return jax.shard_map(local, mesh=mesh, in_specs=in_specs, out_specs=out_specs, check_vma=False)

time: 939 us -> 432 us (0.46)
  blocking collectives: 803 us -> 297 us
    psum x10 -> x20, blocking collectives: 630 us -> 222 us  [cell_sum(): return lax.psum(lax.psum(values, 'cz'), 'cy')]
    all_gather x1, blocking collectives: 173 us -> 74.9 us  [local(): predicted = lax.all_gather(slab_pred, 'grp', axis=0, tiled=True)]
  transfers between devices with their start and end apart: 11 -> 11, of which waited for: 3 -> 3; matrix products, arithmetic and copies ran while one was open for 8% -> 17% of each run, Pallas kernels for 0% -> 0%
where the time goes in v1:
time: 432 us; the launch traced here: 431 us
  blocking collectives  297 us (69%)
  other arithmetic  54.5 us (13%)
  starting transfers between devices  28 us (6%)
  local copies, waits for them, and re-layouts  26.1 us (6%)
  between operations  15.2 us (4%)
  matrix products  8.24 us (2%)
    psum x20, blocking collectives, cell_sum(): return lax.psum(lax.psum(values, 'cz'), 'cy')  222 us
    all_gather x1, blocking collectives, local(): predicted = lax.all_gather(slab_pred, 'grp', axis=0, tiled=True)  74.9 us
    ppermute x5, starting transfers between devices, with_halo(): lax.ppermute(lax.slice_in_dim(block, block.shape[dim] - width, None, axis...  21 us
    another operation x3, other arithmetic, ensemble_weights(): factor = jnp.linalg.cholesky(gram)  12.4 us
    reduce_sum x9, other arithmetic, inner(): return jnp.sum(left * right, axis=(1, 2, 3, 4))  10.5 us
    another operation x2, other arithmetic, ensemble_weights(): return jax.scipy.linalg.cho_solve((factor, True), cross)  10.5 us
  transfers between devices with their start and end apart: 11, of which 3 were waited for; matrix products, arithmetic and copies ran while one was open for 17% of the time, Pallas kernels for 0%

profile of v1, /device:TPU:1, one launch (start us, length us, event | category | flops | bytes accessed | tf_op | source)
XLA Modules:
  0.0 430.9 jit_solution(3549934632958953070)
XLA Ops:
  7.2 2.1 fusion.61
  9.3 4.4 %collective-permute-start = (f32[16,2,1,16,128]{4,3,2,0,1:T(8,128)}, f32[16,2,1,16,128]{4,3,2,0,1:T(8,128)S(1)}, u32[]{:S(2)}, u32[]{:S(2)}) collective-permute-start(f32[16,2,1,16,128]{4,3,2,0,1:T(8,128)} %get-tuple-element.67), channel_id=1, source_target_pairs={{0,1},{1,2},{2,3},{3,4},{4,5},{5,6},{6,7},{7,8},{8,9},{9,10},{10,1... | collective-permute-start | bytes 786440 | tf_op jit(solution)/shard_map/ppermute | solution.py:30
  13.7 1.4 collective-permute-start.1
  15.4 17.1 %psum.140 = f32[16]{0:T(128)S(1)} all-reduce(f32[16]{0:T(128)S(1)} %multiply_reduce_fusion.14), channel_id=1, replica_groups=mesh['grp'=8,'cy'=4,'cz'=8] {'cz'}, use_global_device_ids=true, to_apply=%region_1.2 | all-reduce | flops 16 | bytes 128 | tf_op jit(solution)/shard_map/psum | solution.py:22
  32.4 10.2 %psum.141 = f32[16]{0:T(128)S(1)} all-reduce(f32[16]{0:T(128)S(1)} %psum.140), channel_id=1, replica_groups=mesh['grp'=8,'cy'=4,'cz'=8] {'cy'}, use_global_device_ids=true, to_apply=%region_2.3 | all-reduce | flops 16 | bytes 128 | tf_op jit(solution)/shard_map/psum | solution.py:22
  43.6 1.3 collective-permute-start.2
  44.8 4.6 %collective-permute-start.3 = (f32[16,1,16,128]{3,2,1,0:T(8,128)}, f32[16,1,16,128]{3,2,1,0:T(8,128)}, u32[]{:S(2)}, u32[]{:S(2)}) collective-permute-start(f32[16,1,16,128]{3,2,1,0:T(8,128)} %get-tuple-element.82), channel_id=1, source_target_pairs={{0,1},{1,2},{2,3},{3,4},{4,5},{5,6},{6,7},{7,8},{8,9},{9,10},{10,1... | collective-permute-start | bytes 393224 | tf_op jit(solution)/shard_map/ppermute | solution.py:30
  50.7 1.7 bitcast_multiply_fusion
  52.5 1.9 gather_fusion
  61.1 1.1 multiply_multiply_fusion.11
  62.2 1.6 fusion.100
  64.3 2.7 fusion.60
  69.2 13.1 %psum.142 = f32[1,16]{1,0:T(1,128)S(1)} all-reduce(f32[1,16]{1,0:T(1,128)S(1)} %bitcast.361), channel_id=1, replica_groups=mesh['grp'=8,'cy'=4,'cz'=8] {'cz'}, use_global_device_ids=true, to_apply=%region_4.5 | all-reduce | flops 16 | bytes 128 | tf_op jit(solution)/shard_map/psum | solution.py:22
  82.2 6.8 %psum.143 = f32[16]{0:T(128)S(1)} all-reduce(f32[16]{0:T(128)S(1)} %bitcast.362), channel_id=1, replica_groups=mesh['grp'=8,'cy'=4,'cz'=8] {'cy'}, use_global_device_ids=true, to_apply=%region_5.6 | all-reduce | flops 16 | bytes 128 | tf_op jit(solution)/shard_map/psum | solution.py:22
  89.0 1.6 multiply_reduce_fusion.12
  90.6 13.0 %psum.144 = f32[16]{0:T(128)S(1)} all-reduce(f32[16]{0:T(128)S(1)} %get-tuple-element.23), channel_id=1, replica_groups=mesh['grp'=8,'cy'=4,'cz'=8] {'cz'}, use_global_device_ids=true, to_apply=%region_7.8 | all-reduce | flops 16 | bytes 128 | tf_op jit(solution)/shard_map/psum | solution.py:22
  103.6 7.5 %psum.145 = f32[16]{0:T(128)S(1)} all-reduce(f32[16]{0:T(128)S(1)} %psum.144), channel_id=1, replica_groups=mesh['grp'=8,'cy'=4,'cz'=8] {'cy'}, use_global_device_ids=true, to_apply=%region_8.9 | all-reduce | flops 16 | bytes 128 | tf_op jit(solution)/shard_map/psum | solution.py:22
  111.5 1.4 collective-permute-start.4
  113.0 4.0 collective-permute-start.5
  121.2 14.2 %psum.146 = f32[2,16]{1,0:T(2,128)S(1)} all-reduce(f32[2,16]{1,0:T(2,128)S(1)} %pad_maximum_fusion.14), channel_id=1, replica_groups=mesh['grp'=8,'cy'=4,'cz'=8] {'cz'}, use_global_device_ids=true, to_apply=%region_11.12 | all-reduce | flops 32 | bytes 256 | tf_op jit(solution)/shard_map/psum | solution.py:22
  135.4 7.4 %psum.147 = f32[2,16]{1,0:T(2,128)S(1)} all-reduce(f32[2,16]{1,0:T(2,128)S(1)} %psum.146), channel_id=1, replica_groups=mesh['grp'=8,'cy'=4,'cz'=8] {'cy'}, use_global_device_ids=true, to_apply=%region_12.13 | all-reduce | flops 32 | bytes 256 | tf_op jit(solution)/shard_map/psum | solution.py:22
  142.8 1.7 multiply_reduce_fusion.9
  144.5 12.6 %psum.148 = f32[16]{0:T(128)S(1)} all-reduce(f32[16]{0:T(128)S(1)} %get-tuple-element.21), channel_id=1, replica_groups=mesh['grp'=8,'cy'=4,'cz'=8] {'cz'}, use_global_device_ids=true, to_apply=%region_14.15 | all-reduce | flops 16 | bytes 128 | tf_op jit(solution)/shard_map/psum | solution.py:22
  157.1 6.5 %psum.149 = f32[16]{0:T(128)S(1)} all-reduce(f32[16]{0:T(128)S(1)} %psum.148), channel_id=1, replica_groups=mesh['grp'=8,'cy'=4,'cz'=8] {'cy'}, use_global_device_ids=true, to_apply=%region_15.16 | all-reduce | flops 16 | bytes 128 | tf_op jit(solution)/shard_map/psum | solution.py:22
  164.1 1.4 collective-permute-start.6
  165.5 4.0 collective-permute-start.7
  173.9 12.7 %psum.150 = f32[3,16]{1,0:T(4,128)S(1)} all-reduce(f32[3,16]{1,0:T(4,128)S(1)} %pad_maximum_fusion.12), channel_id=1, replica_groups=mesh['grp'=8,'cy'=4,'cz'=8] {'cz'}, use_global_device_ids=true, to_apply=%region_19.20 | all-reduce | flops 48 | bytes 384 | tf_op jit(solution)/shard_map/psum | solution.py:22
  186.7 7.7 %psum.151 = f32[3,16]{1,0:T(4,128)S(1)} all-reduce(f32[3,16]{1,0:T(4,128)S(1)} %psum.150), channel_id=1, replica_groups=mesh['grp'=8,'cy'=4,'cz'=8] {'cy'}, use_global_device_ids=true, to_apply=%region_20.21 | all-reduce | flops 48 | bytes 384 | tf_op jit(solution)/shard_map/psum | solution.py:22
  194.4 2.7 multiply_reduce_fusion.5
  197.0 11.9 %psum.152 = f32[16]{0:T(128)S(1)} all-reduce(f32[16]{0:T(128)S(1)} %get-tuple-element.19), channel_id=1, replica_groups=mesh['grp'=8,'cy'=4,'cz'=8] {'cz'}, use_global_device_ids=true, to_apply=%region_22.23 | all-reduce | flops 16 | bytes 128 | tf_op jit(solution)/shard_map/psum | solution.py:22
  208.9 6.5 %psum.153 = f32[16]{0:T(128)S(1)} all-reduce(f32[16]{0:T(128)S(1)} %psum.152), channel_id=1, replica_groups=mesh['grp'=8,'cy'=4,'cz'=8] {'cy'}, use_global_device_ids=true, to_apply=%region_23.24 | all-reduce | flops 16 | bytes 128 | tf_op jit(solution)/shard_map/psum | solution.py:22
  215.5 1.4 copy_divide_fusion
  217.3 1.4 collective-permute-start.8
  218.7 4.0 collective-permute-start.9
  227.8 13.1 %psum.154 = f32[4,16]{1,0:T(4,128)S(1)} all-reduce(f32[4,16]{1,0:T(4,128)S(1)} %pad_maximum_fusion.13), channel_id=1, replica_groups=mesh['grp'=8,'cy'=4,'cz'=8] {'cz'}, use_global_device_ids=true, to_apply=%region_28.29 | all-reduce | flops 64 | bytes 512 | tf_op jit(solution)/shard_map/psum | solution.py:22
  240.9 7.6 %psum.155 = f32[4,16]{1,0:T(4,128)S(1)} all-reduce(f32[4,16]{1,0:T(4,128)S(1)} %psum.154), channel_id=1, replica_groups=mesh['grp'=8,'cy'=4,'cz'=8] {'cy'}, use_global_device_ids=true, to_apply=%region_29.30 | all-reduce | flops 64 | bytes 512 | tf_op jit(solution)/shard_map/psum | solution.py:22
  248.5 2.2 multiply_reduce_fusion
  250.7 12.5 %psum.156 = f32[16]{0:T(128)S(1)} all-reduce(f32[16]{0:T(128)S(1)} %multiply_reduce_fusion), channel_id=1, replica_groups=mesh['grp'=8,'cy'=4,'cz'=8] {'cz'}, use_global_device_ids=true, to_apply=%region_31.32 | all-reduce | flops 16 | bytes 128 | tf_op jit(solution)/shard_map/psum | solution.py:22
  263.2 6.2 %psum.157 = f32[16]{0:T(128)S(1)} all-reduce(f32[16]{0:T(128)S(1)} %psum.156), channel_id=1, replica_groups=mesh['grp'=8,'cy'=4,'cz'=8] {'cy'}, use_global_device_ids=true, to_apply=%region_32.33 | all-reduce | flops 16 | bytes 128 | tf_op jit(solution)/shard_map/psum | solution.py:22
  269.5 1.8 multiply_add_fusion
  272.4 4.7 %copy.101 = f32[16,2,4,16,128]{0,4,3,2,1:T(8,128)} copy(f32[16,2,4,16,128]{4,3,2,0,1:T(8,128)S(1)} %pad_maximum_fusion.6) | data formatting | bytes 2097152 | tf_op jit(solution)/shard_map/stack | solution.py:188
  277.1 4.1 gather_fusion.1
  281.4 21.4 %psum.158 = f32[16,256]{0,1:T(8,128)S(1)} all-reduce(f32[16,256]{0,1:T(8,128)S(1)} %multiply_bitcast_fusion), channel_id=1, replica_groups=mesh['grp'=8,'cy'=4,'cz'=8] {'cz'}, use_global_device_ids=true, to_apply=%region_33.34 | all-reduce | flops 4096 | bytes 32768 | tf_op jit(solution)/shard_map/psum | solution.py:22
  302.8 13.6 %psum.159 = f32[16,256]{0,1:T(8,128)S(1)} all-reduce(f32[16,256]{0,1:T(8,128)S(1)} %psum.158), channel_id=1, replica_groups=mesh['grp'=8,'cy'=4,'cz'=8] {'cy'}, use_global_device_ids=true, to_apply=%region_34.35 | all-reduce | flops 4096 | bytes 32768 | tf_op jit(solution)/shard_map/psum | solution.py:22
  316.5 74.9 %all_gather.6 = f32[128,256]{1,0:T(8,128)S(1)} all-gather(f32[16,256]{1,0:T(8,128)S(1)} %copy.102), channel_id=1, replica_groups=mesh['grp'=8,'cy'=4,'cz'=8] {'grp'}, dimensions={0}, use_global_device_ids=true | all-gather | bytes 147456 | tf_op jit(solution)/shard_map/all_gather | solution.py:199
  391.9 11.7 %cholesky.17 = f32[128,128]{1,0:T(8,128)S(1)} custom-call(f32[128,128]{1,0:T(8,128)S(1)} %fusion.78), custom_call_target="Cholesky" | custom-call | tf_op jit(solution)/shard_map/jit(cholesky)/cholesky | solution.py:133
  404.9 9.8 %custom-call.10 = f32[1,128,128]{1,2,0:T(8,128)S(1)} custom-call(f32[1,128,128]{2,1,0:T(8,128)S(1)} %fusion.72), custom_call_target="InvertDiagBlocksLowerTriangular" | custom-call | tf_op jit(solution)/shard_map/jit(_cho_solve)/triangular_solve | solution.py:134
  415.7 7.1 %fusion = f32[2,8,128,128]{3,1,2,0:T(8,128)S(1)} fusion(f32[128,16384]{1,0:T(8,128)} %all-gather.2.cloned.1.call-done, f32[2,8,128,128]{3,2,1,0:T(8,128)S(1)} %bitcast.330, f32[128,128]{0,1:T(8,128)S(1)} %fusion.73, s32[]{:T(128)S(6)} %select_n.96), kind=kOutput, calls=%fused_computation.4 | convolution fusion | flops 402915328 | bytes 10493956 | tf_op jit(solution)/shard_map/dot_general | solution.py:206
  (214 shorter events, 31.4 us)
Async XLA Ops:
  7.2 45.3 %copy-start = (s32[128]{0:T(128)S(1)}, s32[128]{0:T(128)}, u32[]{:S(2)}) copy-start(s32[128]{0:T(128)} %param.18) | copy-start | bytes 1540
  7.2 8.0 %copy-start.2 = (f32[16,2,4,16,128]{4,3,2,1,0:T(8,128)S(1)}, f32[16,2,4,16,128]{4,3,2,1,0:T(8,128)}, u32[]{:S(2)}) copy-start(f32[16,2,4,16,128]{4,3,2,1,0:T(8,128)} %param.10) | copy-start | bytes 3145732
  7.2 408.5 %all-gather.2.cloned.1.call-start = ((), (), s32[]{:S(2)}) async-start(), calls=%async_computation | async-start | bytes 9437184 | tf_op jit(solution)/shard_map/all_gather | solution.py:208
  9.3 48.9 %collective-permute-start = (f32[16,2,1,16,128]{4,3,2,0,1:T(8,128)}, f32[16,2,1,16,128]{4,3,2,0,1:T(8,128)S(1)}, u32[]{:S(2)}, u32[]{:S(2)}) collective-permute-start(f32[16,2,1,16,128]{4,3,2,0,1:T(8,128)} %get-tuple-element.67), channel_id=1, source_target_pairs={{0,1},{1,2},{2,3},{3,4},{4,5},{5,6},{6,7},{7,8},{8,9},{9,10},{10,1... | collective-permute-start | bytes 786440 | tf_op jit(solution)/shard_map/ppermute | solution.py:30
  13.7 35.8 %copy-start.5 = (f32[16,4,16,128]{3,2,1,0:T(8,128)S(1)}, f32[16,4,16,128]{3,2,1,0:T(8,128)}, u32[]{:S(2)}) copy-start(f32[16,4,16,128]{3,2,1,0:T(8,128)} %param.12) | copy-start | bytes 1572868
  13.7 35.8 %copy-start.37 = (f32[16,4,16,128]{3,2,1,0:T(8,128)S(1)}, f32[16,4,16,128]{3,2,1,0:T(8,128)}, u32[]{:S(2)}) copy-start(f32[16,4,16,128]{3,2,1,0:T(8,128)} %param.11) | copy-start | bytes 1572868
  13.7 44.6 %collective-permute-start.1 = (f32[16,2,1,16,128]{4,3,2,0,1:T(8,128)}, f32[16,2,1,16,128]{4,3,2,0,1:T(8,128)}, u32[]{:S(2)}, u32[]{:S(2)}) collective-permute-start(f32[16,2,1,16,128]{4,3,2,0,1:T(8,128)} %get-tuple-element.68), channel_id=1, source_target_pairs={{1,0},{2,1},{3,2},{4,3},{5,4},{6,5},{7,6},{8,7},{9,8},{10,9},{11,1... | collective-permute-start | bytes 786440 | tf_op jit(solution)/shard_map/ppermute | solution.py:33
  43.6 20.7 %collective-permute-start.2 = (f32[16,1,16,128]{3,2,1,0:T(8,128)}, f32[16,1,16,128]{3,2,1,0:T(8,128)}, u32[]{:S(2)}, u32[]{:S(2)}) collective-permute-start(f32[16,1,16,128]{3,2,1,0:T(8,128)} %get-tuple-element.81), channel_id=1, source_target_pairs={{1,0},{2,1},{3,2},{4,3},{5,4},{6,5},{7,6},{8,7},{9,8},{10,9},{11,1... | collective-permute-start | bytes 393224 | tf_op jit(solution)/shard_map/ppermute | solution.py:33
  44.8 19.4 %collective-permute-start.3 = (f32[16,1,16,128]{3,2,1,0:T(8,128)}, f32[16,1,16,128]{3,2,1,0:T(8,128)}, u32[]{:S(2)}, u32[]{:S(2)}) collective-permute-start(f32[16,1,16,128]{3,2,1,0:T(8,128)} %get-tuple-element.82), channel_id=1, source_target_pairs={{0,1},{1,2},{2,3},{3,4},{4,5},{5,6},{6,7},{7,8},{8,9},{9,10},{10,1... | collective-permute-start | bytes 393224 | tf_op jit(solution)/shard_map/ppermute | solution.py:30
  50.7 1.8 copy-start.45
  52.5 3.8 copy-start.3
  55.3 3.0 copy-start.46
  59.5 1.2 copy-start.32
  59.6 1.3 copy-start.33
  59.6 1.5 copy-start.34
  62.2 1.6 copy-start.12
  62.2 54.8 %copy-start.9 = (f32[16,4,16,128]{3,2,1,0:T(8,128)}, f32[16,4,16,128]{3,2,1,0:T(8,128)S(1)}, u32[]{:S(2)}) copy-start(f32[16,4,16,128]{3,2,1,0:T(8,128)S(1)} %get-tuple-element.26) | copy-start | bytes 1572868
  111.2 5.8 %copy-start.13 = (f32[16,4,16,128]{3,2,1,0:T(8,128)S(1)}, f32[16,4,16,128]{3,2,1,0:T(8,128)}, u32[]{:S(2)}) copy-start(f32[16,4,16,128]{3,2,1,0:T(8,128)} %copy-done.12) | copy-start | bytes 1572868
  111.2 5.8 %copy-start.24 = (f32[16,4,16,128]{3,2,1,0:T(8,128)S(1)}, f32[16,4,16,128]{3,2,1,0:T(8,128)}, u32[]{:S(2)}) copy-start(f32[16,4,16,128]{3,2,1,0:T(8,128)} %get-tuple-element.32) | copy-start | bytes 1572868
  111.2 5.8 %copy-start.27 = (f32[16,4,16,128]{3,2,1,0:T(8,128)S(1)}, f32[16,4,16,128]{3,2,1,0:T(8,128)}, u32[]{:S(2)}) copy-start(f32[16,4,16,128]{3,2,1,0:T(8,128)} %get-tuple-element.54) | copy-start | bytes 1572868
  111.5 6.5 %collective-permute-start.4 = (f32[16,1,16,128]{3,2,1,0:T(8,128)S(1)}, f32[16,1,16,128]{3,2,1,0:T(8,128)S(1)}, u32[]{:S(2)}, u32[]{:S(2)}) collective-permute-start(f32[16,1,16,128]{3,2,1,0:T(8,128)S(1)} %get-tuple-element.79), channel_id=1, source_target_pairs={{1,0},{2,1},{3,2},{4,3},{5,4},{6,5},{7,6},{8,7},{9,8},{10,9},{11,1... | collective-permute-start | bytes 393224 | tf_op jit(solution)/shard_map/ppermute | solution.py:33
  113.0 5.9 %collective-permute-start.5 = (f32[16,1,16,128]{3,2,1,0:T(8,128)S(1)}, f32[16,1,16,128]{3,2,1,0:T(8,128)S(1)}, u32[]{:S(2)}, u32[]{:S(2)}) collective-permute-start(f32[16,1,16,128]{3,2,1,0:T(8,128)S(1)} %get-tuple-element.80), channel_id=1, source_target_pairs={{0,1},{1,2},{2,3},{3,4},{4,5},{5,6},{6,7},{7,8},{8,9},{9,10},{10,1... | collective-permute-start | bytes 393224 | tf_op jit(solution)/shard_map/ppermute | solution.py:30
  117.6 1.3 copy-start.16
  117.6 1.3 copy-start.19
  163.8 5.8 %copy-start.10 = (f32[16,4,16,128]{3,2,1,0:T(8,128)S(1)}, f32[16,4,16,128]{3,2,1,0:T(8,128)}, u32[]{:S(2)}) copy-start(f32[16,4,16,128]{3,2,1,0:T(8,128)} %copy-done.9) | copy-start | bytes 1572868
  163.8 5.8 %copy-start.14 = (f32[16,4,16,128]{3,2,1,0:T(8,128)S(1)}, f32[16,4,16,128]{3,2,1,0:T(8,128)}, u32[]{:S(2)}) copy-start(f32[16,4,16,128]{3,2,1,0:T(8,128)} %copy-done.12) | copy-start | bytes 1572868
  163.8 5.8 %copy-start.25 = (f32[16,4,16,128]{3,2,1,0:T(8,128)S(1)}, f32[16,4,16,128]{3,2,1,0:T(8,128)}, u32[]{:S(2)}) copy-start(f32[16,4,16,128]{3,2,1,0:T(8,128)} %get-tuple-element.32) | copy-start | bytes 1572868
  163.8 5.8 %copy-start.28 = (f32[16,4,16,128]{3,2,1,0:T(8,128)S(1)}, f32[16,4,16,128]{3,2,1,0:T(8,128)}, u32[]{:S(2)}) copy-start(f32[16,4,16,128]{3,2,1,0:T(8,128)} %get-tuple-element.54) | copy-start | bytes 1572868
  164.1 6.6 %collective-permute-start.6 = (f32[16,1,16,128]{3,2,1,0:T(8,128)S(1)}, f32[16,1,16,128]{3,2,1,0:T(8,128)S(1)}, u32[]{:S(2)}, u32[]{:S(2)}) collective-permute-start(f32[16,1,16,128]{3,2,1,0:T(8,128)S(1)} %get-tuple-element.77), channel_id=1, source_target_pairs={{1,0},{2,1},{3,2},{4,3},{5,4},{6,5},{7,6},{8,7},{9,8},{10,9},{11,1... | collective-permute-start | bytes 393224 | tf_op jit(solution)/shard_map/ppermute | solution.py:33
  165.5 5.9 %collective-permute-start.7 = (f32[16,1,16,128]{3,2,1,0:T(8,128)S(1)}, f32[16,1,16,128]{3,2,1,0:T(8,128)S(1)}, u32[]{:S(2)}, u32[]{:S(2)}) collective-permute-start(f32[16,1,16,128]{3,2,1,0:T(8,128)S(1)} %get-tuple-element.78), channel_id=1, source_target_pairs={{0,1},{1,2},{2,3},{3,4},{4,5},{5,6},{6,7},{7,8},{8,9},{9,10},{10,1... | collective-permute-start | bytes 393224 | tf_op jit(solution)/shard_map/ppermute | solution.py:30
  170.2 1.3 copy-start.17
  170.2 1.3 copy-start.20
  170.7 1.1 copy-start.6
  216.9 5.8 %copy-start.11 = (f32[16,4,16,128]{3,2,1,0:T(8,128)S(1)}, f32[16,4,16,128]{3,2,1,0:T(8,128)}, u32[]{:S(2)}) copy-start(f32[16,4,16,128]{3,2,1,0:T(8,128)} %copy-done.9) | copy-start | bytes 1572868
  216.9 5.8 %copy-start.15 = (f32[16,4,16,128]{3,2,1,0:T(8,128)S(1)}, f32[16,4,16,128]{3,2,1,0:T(8,128)}, u32[]{:S(2)}) copy-start(f32[16,4,16,128]{3,2,1,0:T(8,128)} %copy-done.12) | copy-start | bytes 1572868
  217.0 5.8 %copy-start.26 = (f32[16,4,16,128]{3,2,1,0:T(8,128)S(1)}, f32[16,4,16,128]{3,2,1,0:T(8,128)}, u32[]{:S(2)}) copy-start(f32[16,4,16,128]{3,2,1,0:T(8,128)} %get-tuple-element.32) | copy-start | bytes 1572868
  217.0 5.8 %copy-start.29 = (f32[16,4,16,128]{3,2,1,0:T(8,128)S(1)}, f32[16,4,16,128]{3,2,1,0:T(8,128)}, u32[]{:S(2)}) copy-start(f32[16,4,16,128]{3,2,1,0:T(8,128)} %get-tuple-element.54) | copy-start | bytes 1572868
  217.3 6.6 %collective-permute-start.8 = (f32[16,1,16,128]{3,2,1,0:T(8,128)S(1)}, f32[16,1,16,128]{3,2,1,0:T(8,128)S(1)}, u32[]{:S(2)}, u32[]{:S(2)}) collective-permute-start(f32[16,1,16,128]{3,2,1,0:T(8,128)S(1)} %get-tuple-element.75), channel_id=1, source_target_pairs={{1,0},{2,1},{3,2},{4,3},{5,4},{6,5},{7,6},{8,7},{9,8},{10,9},{11,1... | collective-permute-start | bytes 393224 | tf_op jit(solution)/shard_map/ppermute | solution.py:33
  218.7 5.9 %collective-permute-start.9 = (f32[16,1,16,128]{3,2,1,0:T(8,128)S(1)}, f32[16,1,16,128]{3,2,1,0:T(8,128)S(1)}, u32[]{:S(2)}, u32[]{:S(2)}) collective-permute-start(f32[16,1,16,128]{3,2,1,0:T(8,128)S(1)} %get-tuple-element.76), channel_id=1, source_target_pairs={{0,1},{1,2},{2,3},{3,4},{4,5},{5,6},{6,7},{7,8},{8,9},{9,10},{10,1... | collective-permute-start | bytes 393224 | tf_op jit(solution)/shard_map/ppermute | solution.py:30
  223.4 1.3 copy-start.18
  223.4 1.3 copy-start.21
  225.6 1.4 copy-start.8
  269.5 1.8 copy-start.4
  269.5 1.8 copy-start.44
  277.1 137.6 %copy-start.47 = (f32[128,256]{1,0:T(8,128)S(1)}, f32[128,256]{1,0:T(8,128)}, u32[]{:S(2)}) copy-start(f32[128,256]{1,0:T(8,128)} %param.17) | copy-start | bytes 393220
  277.1 137.6 %copy-start.48 = (f32[256]{0:T(256)S(1)}, f32[256]{0:T(256)}, u32[]{:S(2)}) copy-start(f32[256]{0:T(256)} %param.15) | copy-start | bytes 3076
  302.8 112.9 %copy-start.23 = (f32[16,2,4,16,128]{4,3,2,1,0:T(8,128)S(1)}, f32[16,2,4,16,128]{4,3,2,1,0:T(8,128)}, u32[]{:S(2)}) copy-start(f32[16,2,4,16,128]{4,3,2,1,0:T(8,128)} %copy-done.22) | copy-start | bytes 3145732
  422.8 1.3 copy-start.1
  (12 other events, 10.5 us)
Sparse Core Ops, SparseCore 0:
  52.5 55.9 all-gather.1

commit v2 on v1

--- a/solution.py
+++ b/solution.py
@@ -166,21 +166,62 @@
     frac_x = frac_x * keep_face
     trans_y, frac_y, trans_z, frac_z = plane_faces(perm_pad[:, 1:-1], saturation)
     coeffs = (porosity / time_step, trans_x, frac_x, trans_y, frac_y, trans_z, frac_z)
+    count = slab_count
+    forward = [(i, i + 1) for i in range(count - 1)]
+    backward = [(target, source) for source, target in forward]
+
+    def planes(field):
+        low = lax.ppermute(field[:, -1:], CELL, forward)
+        high = lax.ppermute(field[:, :1], CELL, backward)
+        return (low, high)
+
+    def apply(vector, ghosts):
+        padded = jnp.concatenate([ghosts[0], vector[:, 0], ghosts[1]], axis=1)
+        out_pressure, out_water = operator(padded, vector[:, 1], coeffs)
+        return jnp.stack([out_pressure, out_water], 1)
+
+    def scale_planes(ghosts, scale):
+        factor = scale[:, None, None, None]
+        return (ghosts[0] / factor, ghosts[1] / factor)
+
+    rhs_planes = planes(rhs[:, 0])
+    image = apply(rhs, rhs_planes)
+    image_planes = planes(image[:, 0])
+    reduced = cell_sum(jnp.stack([inner(rhs, rhs), inner(rhs, image)], 0))
+    beta = jnp.sqrt(reduced[0] + epsilon)
+    basis = [rhs / expand(beta)]
+    basis_planes = [scale_planes(rhs_planes, beta)]
+    image = image / expand(beta)
+    image_planes = scale_planes(image_planes, beta)
+    projected = [reduced[1] / (beta * beta)]
     columns = []
-    beta = jnp.sqrt(cell_sum(inner(rhs, rhs)) + epsilon)
-    basis = [rhs / expand(beta)]
     for jdx in range(KRYLOV):
-        vector = basis[jdx]
-        padded = with_halo(vector[:, 0], ((CELL, 1),), 1)
-        out_pressure, out_water = operator(padded, vector[:, 1], coeffs)
-        image = jnp.stack([out_pressure, out_water], 1)
-        local_dots = jnp.stack([inner(basis[idx], image) for idx in range(jdx + 1)], 0)
-        projected = cell_sum(local_dots)
+        ortho = image
+        ortho_low, ortho_high = image_planes
         for idx in range(jdx + 1):
-            image = image - expand(projected[idx]) * basis[idx]
-        height = jnp.sqrt(cell_sum(inner(image, image)) + epsilon)
-        columns.append([projected[idx] for idx in range(jdx + 1)] + [height])
-        basis.append(image / expand(height))
+            ortho = ortho - expand(projected[idx]) * basis[idx]
+            factor = projected[idx][:, None, None, None]
+            ortho_low = ortho_low - factor * basis_planes[idx][0]
+            ortho_high = ortho_high - factor * basis_planes[idx][1]
+        ortho_planes = (ortho_low, ortho_high)
+        if jdx == KRYLOV - 1:
+            height = jnp.sqrt(cell_sum(inner(ortho, ortho)) + epsilon)
+            columns.append(projected + [height])
+            break
+        image = apply(ortho, ortho_planes)
+        image_planes = planes(image[:, 0])
+        parts = [inner(ortho, ortho)]
+        parts += [inner(basis[idx], image) for idx in range(jdx + 1)]
+        parts.append(inner(ortho, image))
+        reduced = cell_sum(jnp.stack(parts, 0))
+        height = jnp.sqrt(reduced[0] + epsilon)
+        columns.append(projected + [height])
+        basis.append(ortho / expand(height))
+        basis_planes.append(scale_planes(ortho_planes, height))
+        image = image / expand(height)
+        image_planes = scale_planes(image_planes, height)
+        projected = [reduced[1 + idx] / height for idx in range(jdx + 1)]
+        projected.append(reduced[jdx + 2] / (height * height))
     solved = least_squares(columns, beta)
     increment = expand(solved[0]) * basis[0]
     for jdx in range(1, KRYLOV):

time: 432 us -> 343 us (0.79)
  blocking collectives: 297 us -> 201 us
    psum x20 -> x12, blocking collectives: 222 us -> 145 us  [cell_sum(): return lax.psum(lax.psum(values, 'cz'), 'cy')]
    ppermute x0 -> x8, starting transfers between devices: none -> 22.1 us  [the longest x4 16.8 us: planes(): low = lax.ppermute(field[:, -1:], CELL, forward)]
    all_gather x1, blocking collectives: 74.9 us -> 56.2 us  [local(): predicted = lax.all_gather(slab_pred, 'grp', axis=0, tiled=True)]
    ppermute x5 -> x1, starting transfers between devices: 21 us -> 5.07 us  [with_halo(): lax.ppermute(lax.slice_in_dim(block, block.shape[dim] - width, None, axis...]
    ppermute x5 -> x1, starting transfers between devices: 6.97 us -> 1.28 us  [with_halo(): lax.ppermute(lax.slice_in_dim(block, 0, width, axis=dim), axis, backward)]
    reduce_sum x9 -> x6, other arithmetic: 10.5 us -> 4.87 us  [inner(): return jnp.sum(left * right, axis=(1, 2, 3, 4))]
    sub x0 -> x6, other arithmetic: none -> 5.52 us  [the longest x3 5.05 us: local(): ortho = ortho - expand(projected[idx]) * basis[idx]]
    unnamed x99 -> x161, local copies, waits for them, and re-layouts: 6.36 us -> 10.6 us
  transfers between devices with their start and end apart: 11 -> 11, of which waited for: 3 -> 2; matrix products, arithmetic and copies ran while one was open for 17% -> 22% of each run, Pallas kernels for 0% -> 0%
where the time goes in v2:
time: 343 us; the launch traced here: 342 us
  blocking collectives  201 us (59%)
  other arithmetic  57.2 us (17%)
  local copies, waits for them, and re-layouts  29.7 us (9%)
  starting transfers between devices  28.5 us (8%)
  between operations  15.6 us (5%)
  matrix products  8.23 us (2%)
    psum x12, blocking collectives, cell_sum(): return lax.psum(lax.psum(values, 'cz'), 'cy')  145 us
    all_gather x1, blocking collectives, local(): predicted = lax.all_gather(slab_pred, 'grp', axis=0, tiled=True)  56.2 us
    ppermute x4, starting transfers between devices, planes(): low = lax.ppermute(field[:, -1:], CELL, forward)  16.8 us
    another operation x3, other arithmetic, ensemble_weights(): factor = jnp.linalg.cholesky(gram)  12.4 us
    unnamed x161, local copies, waits for them, and re-layouts  10.6 us
    another operation x2, other arithmetic, ensemble_weights(): return jax.scipy.linalg.cho_solve((factor, True), cross)  10.5 us
    dot_general x1, matrix products, local(): jnp.dot(own_columns.T, lax.all_gather(scaled, 'grp', axis=0, tiled=True),...  7.08 us
  transfers between devices with their start and end apart: 11, of which 2 were waited for; matrix products, arithmetic and copies ran while one was open for 22% of the time, Pallas kernels for 0%

profile of v2, /device:TPU:1, one launch (start us, length us, event | category | flops | bytes accessed | tf_op | source)
XLA Modules:
  0.0 342.0 jit_solution(13493309787634116779)
XLA Ops:
  7.3 2.1 fusion.58
  9.4 5.1 %collective-permute-start = (f32[16,2,1,16,128]{4,3,2,0,1:T(8,128)}, f32[16,2,1,16,128]{4,3,2,0,1:T(8,128)}, u32[]{:S(2)}, u32[]{:S(2)}) collective-permute-start(f32[16,2,1,16,128]{4,3,2,0,1:T(8,128)} %get-tuple-element.64), channel_id=1, source_target_pairs={{0,1},{1,2},{2,3},{3,4},{4,5},{5,6},{6,7},{7,8},{8,9},{9,10},{10,1... | collective-permute-start | bytes 786440 | tf_op jit(solution)/shard_map/ppermute | solution.py:30
  14.5 1.3 collective-permute-start.1
  16.5 1.3 collective-permute-start.2
  17.8 4.6 %collective-permute-start.3 = (f32[16,1,16,128]{3,2,1,0:T(8,128)}, f32[16,1,16,128]{3,2,1,0:T(8,128)S(1)}, u32[]{:S(2)}, u32[]{:S(2)}) collective-permute-start(f32[16,1,16,128]{3,2,1,0:T(8,128)} %get-tuple-element.79), channel_id=1, source_target_pairs={{0,1},{1,2},{2,3},{3,4},{4,5},{5,6},{6,7},{7,8},{8,9},{9,10},{10,1... | collective-permute-start | bytes 393224 | tf_op jit(solution)/shard_map/ppermute | solution.py:174
  22.7 1.0 copy-done.27
  23.7 1.6 bitcast_multiply_fusion
  26.0 1.9 gather_fusion
  29.8 1.0 slice.534
  31.6 1.0 slice.417
  33.3 1.3 pad_maximum_fusion
  36.1 1.0 multiply_multiply_fusion.11
  37.1 1.6 fusion.98
  39.3 1.6 fusion.57
  42.2 19.1 %psum.84 = f32[2,16]{1,0:T(2,128)S(1)} all-reduce(f32[2,16]{1,0:T(2,128)S(1)} %pad_maximum_fusion.14), channel_id=1, replica_groups=mesh['grp'=8,'cy'=4,'cz'=8] {'cz'}, use_global_device_ids=true, to_apply=%region_2.3 | all-reduce | flops 32 | bytes 256 | tf_op jit(solution)/shard_map/psum | solution.py:22
  61.2 8.1 %psum.85 = f32[2,16]{1,0:T(2,128)S(1)} all-reduce(f32[2,16]{1,0:T(2,128)S(1)} %psum.84), channel_id=1, replica_groups=mesh['grp'=8,'cy'=4,'cz'=8] {'cy'}, use_global_device_ids=true, to_apply=%region_3.4 | all-reduce | flops 32 | bytes 256 | tf_op jit(solution)/shard_map/psum | solution.py:22
  70.3 1.4 collective-permute-start.4
  71.7 4.0 %collective-permute-start.5 = (f32[16,1,16,128]{3,2,1,0:T(8,128)S(1)}, f32[16,1,16,128]{3,2,1,0:T(8,128)S(1)}, u32[]{:S(2)}, u32[]{:S(2)}) collective-permute-start(f32[16,1,16,128]{3,2,1,0:T(8,128)S(1)} %get-tuple-element.77), channel_id=1, source_target_pairs={{0,1},{1,2},{2,3},{3,4},{4,5},{5,6},{6,7},{7,8},{8,9},{9,10},{10,1... | collective-permute-start | bytes 393224 | tf_op jit(solution)/shard_map/ppermute | solution.py:174
  76.4 1.2 broadcast_divide_fusion
  81.1 12.7 %psum.86 = f32[3,16]{1,0:T(4,128)S(1)} all-reduce(f32[3,16]{1,0:T(4,128)S(1)} %pad_maximum_fusion.12), channel_id=1, replica_groups=mesh['grp'=8,'cy'=4,'cz'=8] {'cz'}, use_global_device_ids=true, to_apply=%region_7.8 | all-reduce | flops 48 | bytes 384 | tf_op jit(solution)/shard_map/psum | solution.py:22
  93.8 7.1 %psum.87 = f32[3,16]{1,0:T(4,128)S(1)} all-reduce(f32[3,16]{1,0:T(4,128)S(1)} %psum.86), channel_id=1, replica_groups=mesh['grp'=8,'cy'=4,'cz'=8] {'cy'}, use_global_device_ids=true, to_apply=%region_8.9 | all-reduce | flops 48 | bytes 384 | tf_op jit(solution)/shard_map/psum | solution.py:22
  101.5 2.5 multiply_subtract_fusion.1
  105.0 1.3 collective-permute-start.6
  106.3 4.2 %collective-permute-start.7 = (f32[16,1,16,128]{3,2,1,0:T(8,128)S(1)}, f32[16,1,16,128]{3,2,1,0:T(8,128)S(1)}, u32[]{:S(2)}, u32[]{:S(2)}) collective-permute-start(f32[16,1,16,128]{3,2,1,0:T(8,128)S(1)} %get-tuple-element.75), channel_id=1, source_target_pairs={{0,1},{1,2},{2,3},{3,4},{4,5},{5,6},{6,7},{7,8},{8,9},{9,10},{10,1... | collective-permute-start | bytes 393224 | tf_op jit(solution)/shard_map/ppermute | solution.py:174
  116.6 14.8 %psum.88 = f32[4,16]{1,0:T(4,128)} all-reduce(f32[4,16]{1,0:T(4,128)S(1)} %pad_maximum_fusion.13), channel_id=1, replica_groups=mesh['grp'=8,'cy'=4,'cz'=8] {'cz'}, use_global_device_ids=true, to_apply=%region_13.14 | all-reduce | flops 64 | bytes 512 | tf_op jit(solution)/shard_map/psum | solution.py:22
  131.4 8.5 %psum.89 = f32[4,16]{1,0:T(4,128)} all-reduce(f32[4,16]{1,0:T(4,128)} %psum.88), channel_id=1, replica_groups=mesh['grp'=8,'cy'=4,'cz'=8] {'cy'}, use_global_device_ids=true, to_apply=%region_14.15 | all-reduce | flops 64 | bytes 512 | tf_op jit(solution)/shard_map/psum | solution.py:22
  141.5 2.3 copy_subtract_fusion
  144.2 1.0 copy-done.38
  145.3 1.3 collective-permute-start.8
  146.6 4.0 %collective-permute-start.9 = (f32[16,1,16,128]{3,2,1,0:T(8,128)S(1)}, f32[16,1,16,128]{3,2,1,0:T(8,128)S(1)}, u32[]{:S(2)}, u32[]{:S(2)}) collective-permute-start(f32[16,1,16,128]{3,2,1,0:T(8,128)S(1)} %get-tuple-element.73), channel_id=1, source_target_pairs={{0,1},{1,2},{2,3},{3,4},{4,5},{5,6},{6,7},{7,8},{8,9},{9,10},{10,1... | collective-permute-start | bytes 393224 | tf_op jit(solution)/shard_map/ppermute | solution.py:174
  151.7 0.8 collective-permute-done.9
  152.9 0.9 copy-done.10
  155.6 0.9 multiply_reduce_fusion.1
  156.5 14.0 %psum.90 = f32[5,16]{1,0:T(8,128)S(1)} all-reduce(f32[5,16]{1,0:T(8,128)S(1)} %stack.147), channel_id=1, replica_groups=mesh['grp'=8,'cy'=4,'cz'=8] {'cz'}, use_global_device_ids=true, to_apply=%region_20.21 | all-reduce | flops 80 | bytes 640 | tf_op jit(solution)/shard_map/psum | solution.py:22
  170.4 7.9 %psum.91 = f32[5,16]{1,0:T(8,128)S(1)} all-reduce(f32[5,16]{1,0:T(8,128)S(1)} %psum.90), channel_id=1, replica_groups=mesh['grp'=8,'cy'=4,'cz'=8] {'cy'}, use_global_device_ids=true, to_apply=%region_21.22 | all-reduce | flops 80 | bytes 640 | tf_op jit(solution)/shard_map/psum | solution.py:22
  178.4 2.3 multiply_reduce_fusion
  180.7 12.1 %psum.92 = f32[16]{0:T(128)S(1)} all-reduce(f32[16]{0:T(128)S(1)} %multiply_reduce_fusion), channel_id=1, replica_groups=mesh['grp'=8,'cy'=4,'cz'=8] {'cz'}, use_global_device_ids=true, to_apply=%region_23.24 | all-reduce | flops 16 | bytes 128 | tf_op jit(solution)/shard_map/psum | solution.py:22
  192.9 6.2 %psum.93 = f32[16]{0:T(128)S(1)} all-reduce(f32[16]{0:T(128)S(1)} %psum.92), channel_id=1, replica_groups=mesh['grp'=8,'cy'=4,'cz'=8] {'cy'}, use_global_device_ids=true, to_apply=%region_24.25 | all-reduce | flops 16 | bytes 128 | tf_op jit(solution)/shard_map/psum | solution.py:22
  199.2 2.1 multiply_add_fusion
  202.4 4.6 %copy.89 = f32[16,2,4,16,128]{0,4,3,2,1:T(8,128)} copy(f32[16,2,4,16,128]{4,3,2,0,1:T(8,128)S(1)} %pad_maximum_fusion.6) | data formatting | bytes 2097152 | tf_op jit(solution)/shard_map/stack | solution.py:229
  207.1 4.3 %gather_fusion.1 = f32[256,16]{1,0:T(8,128)S(1)} fusion(f32[16,16384]{0,1:T(8,128)} %bitcast.447, s32[1024]{0:T(1024)} %pad_clamp_fusion), kind=kCustom, calls=%fused_computation.1 | custom fusion | bytes 33792 | tf_op jit(solution)/shard_map/jit(_take)/gather | solution.py:238
  211.5 21.6 %psum.94 = f32[16,256]{0,1:T(8,128)S(1)} all-reduce(f32[16,256]{0,1:T(8,128)S(1)} %multiply_bitcast_fusion), channel_id=1, replica_groups=mesh['grp'=8,'cy'=4,'cz'=8] {'cz'}, use_global_device_ids=true, to_apply=%region_25.26 | all-reduce | flops 4096 | bytes 32768 | tf_op jit(solution)/shard_map/psum | solution.py:22
  233.1 13.2 %psum.95 = f32[16,256]{0,1:T(8,128)S(1)} all-reduce(f32[16,256]{0,1:T(8,128)S(1)} %psum.94), channel_id=1, replica_groups=mesh['grp'=8,'cy'=4,'cz'=8] {'cy'}, use_global_device_ids=true, to_apply=%region_26.27 | all-reduce | flops 4096 | bytes 32768 | tf_op jit(solution)/shard_map/psum | solution.py:22
  246.3 56.2 %all_gather.6 = f32[128,256]{1,0:T(8,128)S(1)} all-gather(f32[16,256]{1,0:T(8,128)S(1)} %copy.90), channel_id=1, replica_groups=mesh['grp'=8,'cy'=4,'cz'=8] {'grp'}, dimensions={0}, use_global_device_ids=true | all-gather | bytes 147456 | tf_op jit(solution)/shard_map/all_gather | solution.py:240
  303.0 11.7 %cholesky.17 = f32[128,128]{1,0:T(8,128)S(1)} custom-call(f32[128,128]{1,0:T(8,128)S(1)} %fusion.75), custom_call_target="Cholesky" | custom-call | tf_op jit(solution)/shard_map/jit(cholesky)/cholesky | solution.py:133
  316.0 9.8 %custom-call.10 = f32[1,128,128]{1,2,0:T(8,128)S(1)} custom-call(f32[1,128,128]{2,1,0:T(8,128)S(1)} %fusion.69), custom_call_target="InvertDiagBlocksLowerTriangular" | custom-call | tf_op jit(solution)/shard_map/jit(_cho_solve)/triangular_solve | solution.py:134
  326.8 7.1 %fusion = f32[2,8,128,128]{3,1,2,0:T(8,128)S(1)} fusion(f32[128,16384]{1,0:T(8,128)} %all-gather.2.cloned.1.call-done, f32[2,8,128,128]{3,2,1,0:T(8,128)S(1)} %bitcast.446, f32[128,128]{0,1:T(8,128)S(1)} %fusion.70, s32[]{:T(128)S(6)} %select_n.96), kind=kOutput, calls=%fused_computation.4 | convolution fusion | flops 402915328 | bytes 10493956 | tf_op jit(solution)/shard_map/dot_general | solution.py:247
  334.1 1.1 slice_bitcast_fusion.1
  (273 shorter events, 29.8 us)
Async XLA Ops:
  7.2 18.8 %copy-start = (s32[128]{0:T(128)S(1)}, s32[128]{0:T(128)}, u32[]{:S(2)}) copy-start(s32[128]{0:T(128)} %param.18) | copy-start | bytes 1540
  7.2 8.6 %copy-start.2 = (f32[16,2,4,16,128]{4,3,2,1,0:T(8,128)S(1)}, f32[16,2,4,16,128]{4,3,2,1,0:T(8,128)}, u32[]{:S(2)}) copy-start(f32[16,2,4,16,128]{4,3,2,1,0:T(8,128)} %param.10) | copy-start | bytes 3145732
  7.2 319.6 %all-gather.2.cloned.1.call-start = ((), (), s32[]{:S(2)}) async-start(), calls=%async_computation | async-start | bytes 9437184 | tf_op jit(solution)/shard_map/all_gather | solution.py:249
  7.2 15.2 %copy-start.8 = (f32[16,4,16,128]{3,2,1,0:T(8,128)S(1)}, f32[16,4,16,128]{3,2,1,0:T(8,128)}, u32[]{:S(2)}) copy-start(f32[16,4,16,128]{3,2,1,0:T(8,128)} %param.12) | copy-start | bytes 1572868
  7.2 15.2 %copy-start.43 = (f32[16,4,16,128]{3,2,1,0:T(8,128)S(1)}, f32[16,4,16,128]{3,2,1,0:T(8,128)}, u32[]{:S(2)}) copy-start(f32[16,4,16,128]{3,2,1,0:T(8,128)} %param.11) | copy-start | bytes 1572868
  9.4 23.8 %collective-permute-start = (f32[16,2,1,16,128]{4,3,2,0,1:T(8,128)}, f32[16,2,1,16,128]{4,3,2,0,1:T(8,128)}, u32[]{:S(2)}, u32[]{:S(2)}) collective-permute-start(f32[16,2,1,16,128]{4,3,2,0,1:T(8,128)} %get-tuple-element.64), channel_id=1, source_target_pairs={{0,1},{1,2},{2,3},{3,4},{4,5},{5,6},{6,7},{7,8},{8,9},{9,10},{10,1... | collective-permute-start | bytes 786440 | tf_op jit(solution)/shard_map/ppermute | solution.py:30
  14.5 18.8 %collective-permute-start.1 = (f32[16,2,1,16,128]{4,3,2,0,1:T(8,128)}, f32[16,2,1,16,128]{4,3,2,0,1:T(8,128)}, u32[]{:S(2)}, u32[]{:S(2)}) collective-permute-start(f32[16,2,1,16,128]{4,3,2,0,1:T(8,128)} %get-tuple-element.65), channel_id=1, source_target_pairs={{1,0},{2,1},{3,2},{4,3},{5,4},{6,5},{7,6},{8,7},{9,8},{10,9},{11,1... | collective-permute-start | bytes 786440 | tf_op jit(solution)/shard_map/ppermute | solution.py:33
  16.5 22.7 %collective-permute-start.2 = (f32[16,1,16,128]{3,2,1,0:T(8,128)}, f32[16,1,16,128]{3,2,1,0:T(8,128)S(1)}, u32[]{:S(2)}, u32[]{:S(2)}) collective-permute-start(f32[16,1,16,128]{3,2,1,0:T(8,128)} %get-tuple-element.78), channel_id=1, source_target_pairs={{1,0},{2,1},{3,2},{4,3},{5,4},{6,5},{7,6},{8,7},{9,8},{10,9},{11,1... | collective-permute-start | bytes 393224 | tf_op jit(solution)/shard_map/ppermute | solution.py:175
  17.8 21.4 %collective-permute-start.3 = (f32[16,1,16,128]{3,2,1,0:T(8,128)}, f32[16,1,16,128]{3,2,1,0:T(8,128)S(1)}, u32[]{:S(2)}, u32[]{:S(2)}) collective-permute-start(f32[16,1,16,128]{3,2,1,0:T(8,128)} %get-tuple-element.79), channel_id=1, source_target_pairs={{0,1},{1,2},{2,3},{3,4},{4,5},{5,6},{6,7},{7,8},{8,9},{9,10},{10,1... | collective-permute-start | bytes 393224 | tf_op jit(solution)/shard_map/ppermute | solution.py:174
  25.3 85.2 %copy-start.57 = (f32[128]{0:T(128)}, f32[128]{0:T(128)S(1)}, u32[]{:S(2)}) copy-start(f32[128]{0:T(128)S(1)} %compare_convert_fusion) | copy-start | bytes 1540
  25.4 50.4 %copy-start.59 = (f32[16]{0:T(128)}, f32[16]{0:T(128)S(1)}, u32[]{:S(2)}) copy-start(f32[16]{0:T(128)S(1)} %compare_convert_fusion.1) | copy-start | bytes 196
  41.9 38.2 %copy-start.5 = (f32[16,1,4,16,128]{4,3,2,0,1:T(8,128)}, f32[16,1,4,16,128]{4,3,2,0,1:T(8,128)S(1)}, u32[]{:S(2)}) copy-start(f32[16,1,4,16,128]{4,3,2,0,1:T(8,128)S(1)} %fusion.46) | copy-start | bytes 1572868
  69.9 9.7 %copy-start.12 = (f32[16,2,4,16,128]{4,3,2,0,1:T(8,128)}, f32[16,2,4,16,128]{4,3,2,0,1:T(8,128)S(1)}, u32[]{:S(2)}) copy-start(f32[16,2,4,16,128]{4,3,2,0,1:T(8,128)S(1)} %multiply_subtract_fusion.2) | copy-start | bytes 3145732
  70.0 5.8 %copy-start.14 = (f32[16,4,16,128]{3,2,1,0:T(8,128)S(1)}, f32[16,4,16,128]{3,2,1,0:T(8,128)}, u32[]{:S(2)}) copy-start(f32[16,4,16,128]{3,2,1,0:T(8,128)} %copy-done.13) | copy-start | bytes 1572868
  70.3 7.7 %collective-permute-start.4 = (f32[16,1,16,128]{3,2,1,0:T(8,128)S(1)}, f32[16,1,16,128]{3,2,1,0:T(8,128)S(1)}, u32[]{:S(2)}, u32[]{:S(2)}) collective-permute-start(f32[16,1,16,128]{3,2,1,0:T(8,128)S(1)} %get-tuple-element.76), channel_id=1, source_target_pairs={{1,0},{2,1},{3,2},{4,3},{5,4},{6,5},{7,6},{8,7},{9,8},{10,9},{11,1... | collective-permute-start | bytes 393224 | tf_op jit(solution)/shard_map/ppermute | solution.py:175
  71.7 6.3 %collective-permute-start.5 = (f32[16,1,16,128]{3,2,1,0:T(8,128)S(1)}, f32[16,1,16,128]{3,2,1,0:T(8,128)S(1)}, u32[]{:S(2)}, u32[]{:S(2)}) collective-permute-start(f32[16,1,16,128]{3,2,1,0:T(8,128)S(1)} %get-tuple-element.77), channel_id=1, source_target_pairs={{0,1},{1,2},{2,3},{3,4},{4,5},{5,6},{6,7},{7,8},{8,9},{9,10},{10,1... | collective-permute-start | bytes 393224 | tf_op jit(solution)/shard_map/ppermute | solution.py:174
  80.5 20.4 %copy-start.65 = (f32[2,16]{1,0:T(2,128)S(1)}, f32[2,16]{1,0:T(2,128)}, u32[]{:S(2)}) copy-start(f32[2,16]{1,0:T(2,128)} %copy-done.64) | copy-start | bytes 388
  101.5 10.8 %copy-start.69 = (f32[16]{0:T(128)}, f32[16]{0:T(128)S(1)}, u32[]{:S(2)}) copy-start(f32[16]{0:T(128)S(1)} %get-tuple-element.93) | copy-start | bytes 196
  104.0 6.5 %copy-start.15 = (f32[16,4,16,128]{3,2,1,0:T(8,128)S(1)}, f32[16,4,16,128]{3,2,1,0:T(8,128)}, u32[]{:S(2)}) copy-start(f32[16,4,16,128]{3,2,1,0:T(8,128)} %copy-done.13) | copy-start | bytes 1572868
  104.0 6.5 %copy-start.19 = (f32[16,4,16,128]{3,2,1,0:T(8,128)S(1)}, f32[16,4,16,128]{3,2,1,0:T(8,128)}, u32[]{:S(2)}) copy-start(f32[16,4,16,128]{3,2,1,0:T(8,128)} %copy-done.17) | copy-start | bytes 1572868
  104.0 6.5 %copy-start.30 = (f32[16,4,16,128]{3,2,1,0:T(8,128)S(1)}, f32[16,4,16,128]{3,2,1,0:T(8,128)}, u32[]{:S(2)}) copy-start(f32[16,4,16,128]{3,2,1,0:T(8,128)} %get-tuple-element.29) | copy-start | bytes 1572868
  104.1 6.5 %copy-start.33 = (f32[16,4,16,128]{3,2,1,0:T(8,128)S(1)}, f32[16,4,16,128]{3,2,1,0:T(8,128)}, u32[]{:S(2)}) copy-start(f32[16,4,16,128]{3,2,1,0:T(8,128)} %get-tuple-element.51) | copy-start | bytes 1572868
  104.1 6.5 %copy-start.60 = (f32[16]{0:T(128)S(1)}, f32[16]{0:T(128)}, u32[]{:S(2)}) copy-start(f32[16]{0:T(128)} %copy-done.59) | copy-start | bytes 196
  105.0 6.6 %collective-permute-start.6 = (f32[16,1,16,128]{3,2,1,0:T(8,128)S(1)}, f32[16,1,16,128]{3,2,1,0:T(8,128)S(1)}, u32[]{:S(2)}, u32[]{:S(2)}) collective-permute-start(f32[16,1,16,128]{3,2,1,0:T(8,128)S(1)} %get-tuple-element.74), channel_id=1, source_target_pairs={{1,0},{2,1},{3,2},{4,3},{5,4},{6,5},{7,6},{8,7},{9,8},{10,9},{11,1... | collective-permute-start | bytes 393224 | tf_op jit(solution)/shard_map/ppermute | solution.py:175
  106.3 5.9 %collective-permute-start.7 = (f32[16,1,16,128]{3,2,1,0:T(8,128)S(1)}, f32[16,1,16,128]{3,2,1,0:T(8,128)S(1)}, u32[]{:S(2)}, u32[]{:S(2)}) collective-permute-start(f32[16,1,16,128]{3,2,1,0:T(8,128)S(1)} %get-tuple-element.75), channel_id=1, source_target_pairs={{0,1},{1,2},{2,3},{3,4},{4,5},{5,6},{6,7},{7,8},{8,9},{9,10},{10,1... | collective-permute-start | bytes 393224 | tf_op jit(solution)/shard_map/ppermute | solution.py:174
  141.5 11.0 %copy-start.67 = (f32[16]{0:T(128)}, f32[16]{0:T(128)S(1)}, u32[]{:S(2)}) copy-start(f32[16]{0:T(128)S(1)} %get-tuple-element.86) | copy-start | bytes 196
  143.8 11.0 %copy-start.3 = (f32[16,2,4,16,128]{4,3,2,1,0:T(8,128)}, f32[16,2,4,16,128]{4,3,2,1,0:T(8,128)S(1)}, u32[]{:S(2)}) copy-start(f32[16,2,4,16,128]{4,3,2,1,0:T(8,128)S(1)} %copy_subtract_fusion) | copy-start | bytes 3145732
  143.9 6.7 %copy-start.16 = (f32[16,4,16,128]{3,2,1,0:T(8,128)S(1)}, f32[16,4,16,128]{3,2,1,0:T(8,128)}, u32[]{:S(2)}) copy-start(f32[16,4,16,128]{3,2,1,0:T(8,128)} %copy-done.13) | copy-start | bytes 1572868
  143.9 6.7 %copy-start.20 = (f32[16,4,16,128]{3,2,1,0:T(8,128)S(1)}, f32[16,4,16,128]{3,2,1,0:T(8,128)}, u32[]{:S(2)}) copy-start(f32[16,4,16,128]{3,2,1,0:T(8,128)} %copy-done.17) | copy-start | bytes 1572868
  143.9 6.7 %copy-start.31 = (f32[16,4,16,128]{3,2,1,0:T(8,128)S(1)}, f32[16,4,16,128]{3,2,1,0:T(8,128)}, u32[]{:S(2)}) copy-start(f32[16,4,16,128]{3,2,1,0:T(8,128)} %get-tuple-element.29) | copy-start | bytes 1572868
  143.9 6.7 %copy-start.34 = (f32[16,4,16,128]{3,2,1,0:T(8,128)S(1)}, f32[16,4,16,128]{3,2,1,0:T(8,128)}, u32[]{:S(2)}) copy-start(f32[16,4,16,128]{3,2,1,0:T(8,128)} %get-tuple-element.51) | copy-start | bytes 1572868
  143.9 6.7 %copy-start.58 = (f32[128]{0:T(128)S(1)}, f32[128]{0:T(128)}, u32[]{:S(2)}) copy-start(f32[128]{0:T(128)} %copy-done.57) | copy-start | bytes 1540
  144.0 6.7 %copy-start.61 = (f32[16]{0:T(128)S(1)}, f32[16]{0:T(128)}, u32[]{:S(2)}) copy-start(f32[16]{0:T(128)} %copy-done.59) | copy-start | bytes 196
  145.3 6.4 %collective-permute-start.8 = (f32[16,1,16,128]{3,2,1,0:T(8,128)S(1)}, f32[16,1,16,128]{3,2,1,0:T(8,128)S(1)}, u32[]{:S(2)}, u32[]{:S(2)}) collective-permute-start(f32[16,1,16,128]{3,2,1,0:T(8,128)S(1)} %get-tuple-element.72), channel_id=1, source_target_pairs={{1,0},{2,1},{3,2},{4,3},{5,4},{6,5},{7,6},{8,7},{9,8},{10,9},{11,1... | collective-permute-start | bytes 393224 | tf_op jit(solution)/shard_map/ppermute | solution.py:175
  146.6 5.9 %collective-permute-start.9 = (f32[16,1,16,128]{3,2,1,0:T(8,128)S(1)}, f32[16,1,16,128]{3,2,1,0:T(8,128)S(1)}, u32[]{:S(2)}, u32[]{:S(2)}) collective-permute-start(f32[16,1,16,128]{3,2,1,0:T(8,128)S(1)} %get-tuple-element.73), channel_id=1, source_target_pairs={{0,1},{1,2},{2,3},{3,4},{4,5},{5,6},{6,7},{7,8},{8,9},{9,10},{10,1... | collective-permute-start | bytes 393224 | tf_op jit(solution)/shard_map/ppermute | solution.py:174
  178.4 20.7 %copy-start.56 = (f32[4,16]{1,0:T(4,128)S(1)}, f32[4,16]{1,0:T(4,128)}, u32[]{:S(2)}) copy-start(f32[4,16]{1,0:T(4,128)} %psum.89) | copy-start | bytes 772
  178.4 20.7 %copy-start.63 = (f32[3,16]{1,0:T(4,128)S(1)}, f32[3,16]{1,0:T(4,128)}, u32[]{:S(2)}) copy-start(f32[3,16]{1,0:T(4,128)} %copy-done.62) | copy-start | bytes 580
  178.4 20.7 %copy-start.66 = (f32[2,16]{1,0:T(2,128)S(1)}, f32[2,16]{1,0:T(2,128)}, u32[]{:S(2)}) copy-start(f32[2,16]{1,0:T(2,128)} %copy-done.64) | copy-start | bytes 388
  178.4 20.7 %copy-start.68 = (f32[16]{0:T(128)S(1)}, f32[16]{0:T(128)}, u32[]{:S(2)}) copy-start(f32[16]{0:T(128)} %copy-done.67) | copy-start | bytes 196
  178.4 20.7 %copy-start.70 = (f32[16]{0:T(128)S(1)}, f32[16]{0:T(128)}, u32[]{:S(2)}) copy-start(f32[16]{0:T(128)} %copy-done.69) | copy-start | bytes 196
  178.4 20.7 %copy-start.74 = (f32[16]{0:T(128)S(1)}, f32[16]{0:T(128)}, u32[]{:S(2)}) copy-start(f32[16]{0:T(128)} %get-tuple-element.92) | copy-start | bytes 196
  202.4 8.9 %copy-start.71 = (f32[256]{0:T(256)S(1)}, f32[256]{0:T(256)}, u32[]{:S(2)}) copy-start(f32[256]{0:T(256)} %fusion.88) | copy-start | bytes 3076
  202.4 8.9 %copy-start.73 = (pred[256]{0:T(512)(128)(4,1)S(1)}, pred[256]{0:T(512)(128)(4,1)}, u32[]{:S(2)}) copy-start(pred[256]{0:T(512)(128)(4,1)} %get-tuple-element.15) | copy-start | bytes 772
  202.4 100.1 %copy-start.76 = (f32[256]{0:T(256)S(1)}, f32[256]{0:T(256)}, u32[]{:S(2)}) copy-start(f32[256]{0:T(256)} %get-tuple-element.94) | copy-start | bytes 3076
  207.1 118.8 %copy-start.77 = (f32[256]{0:T(256)S(1)}, f32[256]{0:T(256)}, u32[]{:S(2)}) copy-start(f32[256]{0:T(256)} %get-tuple-element.95) | copy-start | bytes 3076
  207.1 118.8 %copy-start.78 = (f32[128,256]{1,0:T(8,128)S(1)}, f32[128,256]{1,0:T(8,128)}, u32[]{:S(2)}) copy-start(f32[128,256]{1,0:T(8,128)} %param.17) | copy-start | bytes 393220
  207.1 118.8 %copy-start.79 = (f32[256]{0:T(256)S(1)}, f32[256]{0:T(256)}, u32[]{:S(2)}) copy-start(f32[256]{0:T(256)} %param.15) | copy-start | bytes 3076
  233.1 93.7 %copy-start.28 = (f32[16,2,4,16,128]{4,3,2,1,0:T(8,128)S(1)}, f32[16,2,4,16,128]{4,3,2,1,0:T(8,128)}, u32[]{:S(2)}) copy-start(f32[16,2,4,16,128]{4,3,2,1,0:T(8,128)} %copy-done.27) | copy-start | bytes 3145732
  (43 other events, 70.0 us)
Sparse Core Ops, SparseCore 0:
  25.5 56.9 all-gather.1

commit v3 on v2

--- a/solution.py
+++ b/solution.py
@@ -18,8 +18,17 @@
 CELL = ("cy", "cz")
 
 
-def cell_sum(values):
-    return lax.psum(lax.psum(values, "cz"), "cy")
+def cell_sum(values, doubling=False):
+    for axis in ("cz", "cy"):
+        size = lax.axis_size(axis)
+        if not doubling or size & (size - 1):
+            values = lax.psum(values, axis)
+            continue
+        step = 1
+        while step < size:
+            values = values + lax.ppermute(values, axis, [(i, i ^ step) for i in range(size)])
+            step *= 2
+    return values
 
 
 def with_halo(block, sides, width):
@@ -226,17 +235,21 @@
     increment = expand(solved[0]) * basis[0]
     for jdx in range(1, KRYLOV):
         increment = increment + expand(solved[jdx]) * basis[jdx]
-    flat = jnp.stack([pressure + increment[:, 0], saturation + increment[:, 1]], 1).reshape(
-        local_members, 2 * cells_dev
-    )
     cells = jnp.take(well_cell, obs_well)
     wells = well_cell.shape[0]
     component = (jnp.arange(obs_well.shape[0], dtype=jnp.int32) >= wells).astype(jnp.int32)
     slab_row = cells // plane - slab_index * slab_x
     inside = (slab_row >= 0) & (slab_row < slab_x)
-    local_cell = jnp.where(inside, slab_row * plane + cells % plane, 0)
-    picked = jnp.take(flat, component * cells_dev + local_cell, axis=1) * inside.astype(jnp.float32)
-    slab_pred = cell_sum(picked)
+    row = jnp.where(inside, slab_row, 0)
+    col_y = (cells % plane) // plane_cols
+    col_z = cells % plane_cols
+    state = jnp.where(
+        component[None, :] > 0,
+        saturation[:, row, col_y, col_z],
+        pressure[:, row, col_y, col_z],
+    )
+    picked = (state + increment[:, component, row, col_y, col_z]) * inside.astype(jnp.float32)
+    slab_pred = cell_sum(picked, doubling=True)
     predicted = lax.all_gather(slab_pred, "grp", axis=0, tiled=True)
     weights = ensemble_weights(predicted, obs_values, obs_error, noise)
     params = jnp.stack([log_perm, porosity], 1).reshape(local_members, 2 * cells_dev)

time: 343 us -> 353 us (1.029)
  blocking collectives: 201 us -> 171 us
  waiting for transfers between devices: 1.48 us -> 22.6 us
  local copies, waits for them, and re-layouts: 29.7 us -> 36.8 us
  starting transfers between devices: 28.5 us -> 33.4 us
  other arithmetic: 57.2 us -> 61.7 us
    psum x12 -> x10, blocking collectives: 145 us -> 121 us  [cell_sum(): values = lax.psum(values, axis)]
    ppermute x0 -> x5, waiting for transfers between devices: none -> 21.8 us  [cell_sum(): lax.ppermute(values, axis, [(i, i ^ step) for i in range(size)])]
    add x0 -> x2, local copies, waits for them, and re-layouts: none -> 6.14 us  [the longest x1 6.08 us: local(): increment = increment + expand(solved[jdx]) * basis[jdx]]
    all_gather x1, blocking collectives: 56.2 us -> 50.2 us  [local(): predicted = lax.all_gather(slab_pred, 'grp', axis=0, tiled=True)]
    gather x1 -> x3, local copies, waits for them, and re-layouts: 4.27 us -> 9.81 us  [the longest x1 3.51 us: local(): increment[:, component, row, col_y, col_z]]
    ppermute x0 -> x5, starting transfers between devices: none -> 4.9 us  [cell_sum(): lax.ppermute(values, axis, [(i, i ^ step) for i in range(size)])]
    mul x5, other arithmetic: 4.24 us -> 9.13 us  [net(): flow_z = coef_z * diff_z]
    another operation x2 -> x0, local copies, waits for them, and re-layouts: 4.73 us -> none  [the longest x1 4.63 us: local(): jnp.stack([pressure + increment[:, 0], saturation + increment[:, 1]], 1)]
  transfers between devices with their start and end apart: 11 -> 16, of which waited for: 2 -> 6; matrix products, arithmetic and copies ran while one was open for 22% -> 27% of each run, Pallas kernels for 0% -> 0%
where the time goes in v3:
time: 353 us; the launch traced here: 349 us
  blocking collectives  171 us (48%)
  other arithmetic  61.7 us (17%)
  local copies, waits for them, and re-layouts  36.8 us (10%)
  starting transfers between devices  33.4 us (9%)
  waiting for transfers between devices  22.6 us (6%)
  between operations  15.7 us (4%)
  matrix products  8.23 us (2%)
    psum x10, blocking collectives, cell_sum(): values = lax.psum(values, axis)  121 us
    all_gather x1, blocking collectives, local(): predicted = lax.all_gather(slab_pred, 'grp', axis=0, tiled=True)  50.2 us
    ppermute x5, waiting for transfers between devices, cell_sum(): lax.ppermute(values, axis, [(i, i ^ step) for i in range(size)])  21.8 us
    ppermute x4, starting transfers between devices, planes(): low = lax.ppermute(field[:, -1:], CELL, forward)  16.9 us
    another operation x3, other arithmetic, ensemble_weights(): factor = jnp.linalg.cholesky(gram)  12.4 us
    another operation x2, other arithmetic, ensemble_weights(): return jax.scipy.linalg.cho_solve((factor, True), cross)  10.5 us
    mul x5, other arithmetic, net(): flow_z = coef_z * diff_z  9.13 us
    unnamed x138, local copies, waits for them, and re-layouts  8.98 us
  transfers between devices with their start and end apart: 16, of which 6 were waited for; matrix products, arithmetic and copies ran while one was open for 27% of the time, Pallas kernels for 0%

profile of v3, /device:TPU:1, one launch (start us, length us, event | category | flops | bytes accessed | tf_op | source)
XLA Modules:
  0.0 349.5 jit_solution(8500601149866048120)
XLA Ops:
  7.2 2.0 fusion.55
  9.3 5.2 %collective-permute-start = (f32[16,2,1,16,128]{4,3,2,1,0:T(8,128)}, f32[16,2,1,16,128]{4,3,2,1,0:T(8,128)}, u32[]{:S(2)}, u32[]{:S(2)}) collective-permute-start(f32[16,2,1,16,128]{4,3,2,1,0:T(8,128)} %get-tuple-element.81), channel_id=1, source_target_pairs={{0,1},{1,2},{2,3},{3,4},{4,5},{5,6},{6,7},{7,8},{8,9},{9,10},{10,1... | collective-permute-start | bytes 786440 | tf_op jit(solution)/shard_map/ppermute | solution.py:39
  18.9 4.6 %collective-permute-start.3 = (f32[16,1,16,128]{3,2,1,0:T(8,128)}, f32[16,1,16,128]{3,2,1,0:T(8,128)S(1)}, u32[]{:S(2)}, u32[]{:S(2)}) collective-permute-start(f32[16,1,16,128]{3,2,1,0:T(8,128)} %get-tuple-element.96), channel_id=1, source_target_pairs={{0,1},{1,2},{2,3},{3,4},{4,5},{5,6},{6,7},{7,8},{8,9},{9,10},{10,1... | collective-permute-start | bytes 393224 | tf_op jit(solution)/shard_map/ppermute | solution.py:183
  23.5 1.3 pad_maximum_fusion.1
  24.8 1.6 bitcast_multiply_fusion
  27.4 1.9 gather_fusion
  33.6 2.6 copy.346
  36.3 3.6 %copy.347 = f32[16,4,16,128]{0,3,2,1:T(8,128)} copy(f32[16,4,16,128]{3,2,1,0:T(8,128)} %param.14) | data formatting | bytes 1048576 | tf_op args[4]
  39.8 3.0 gather_fusion.1
  42.9 3.3 gather_fusion.2
  47.9 2.7 multiply_multiply_fusion.11
  50.6 1.6 fusion.101
  52.8 1.7 fusion.54
  55.8 19.4 %psum.70 = f32[2,16]{1,0:T(2,128)S(1)} all-reduce(f32[2,16]{1,0:T(2,128)S(1)} %pad_maximum_fusion.13), channel_id=1, replica_groups=mesh['grp'=8,'cy'=4,'cz'=8] {'cz'}, use_global_device_ids=true, to_apply=%region_2.3 | all-reduce | flops 32 | bytes 256 | tf_op jit(solution)/shard_map/psum | solution.py:25
  75.1 7.7 %psum.71 = f32[2,16]{1,0:T(2,128)S(1)} all-reduce(f32[2,16]{1,0:T(2,128)S(1)} %psum.70), channel_id=1, replica_groups=mesh['grp'=8,'cy'=4,'cz'=8] {'cy'}, use_global_device_ids=true, to_apply=%region_3.4 | all-reduce | flops 32 | bytes 256 | tf_op jit(solution)/shard_map/psum | solution.py:25
  83.5 1.3 collective-permute-start.4
  84.8 4.3 %collective-permute-start.5 = (f32[16,1,16,128]{3,2,1,0:T(8,128)S(1)}, f32[16,1,16,128]{3,2,1,0:T(8,128)S(1)}, u32[]{:S(2)}, u32[]{:S(2)}) collective-permute-start(f32[16,1,16,128]{3,2,1,0:T(8,128)S(1)} %get-tuple-element.94), channel_id=1, source_target_pairs={{0,1},{1,2},{2,3},{3,4},{4,5},{5,6},{6,7},{7,8},{8,9},{9,10},{10,1... | collective-permute-start | bytes 393224 | tf_op jit(solution)/shard_map/ppermute | solution.py:183
  89.1 2.1 multiply_multiply_fusion.10
  94.3 13.0 %psum.72 = f32[3,16]{1,0:T(4,128)S(1)} all-reduce(f32[3,16]{1,0:T(4,128)S(1)} %pad_maximum_fusion.11), channel_id=1, replica_groups=mesh['grp'=8,'cy'=4,'cz'=8] {'cz'}, use_global_device_ids=true, to_apply=%region_7.8 | all-reduce | flops 48 | bytes 384 | tf_op jit(solution)/shard_map/psum | solution.py:25
  107.4 6.6 %psum.73 = f32[3,16]{1,0:T(4,128)S(1)} all-reduce(f32[3,16]{1,0:T(4,128)S(1)} %psum.72), channel_id=1, replica_groups=mesh['grp'=8,'cy'=4,'cz'=8] {'cy'}, use_global_device_ids=true, to_apply=%region_8.9 | all-reduce | flops 48 | bytes 384 | tf_op jit(solution)/shard_map/psum | solution.py:25
  114.0 1.4 bitcast_multiply_fusion.6
  115.3 1.7 multiply_subtract_fusion.1
  118.7 4.0 %collective-permute-start.7 = (f32[16,1,16,128]{3,2,1,0:T(8,128)S(1)}, f32[16,1,16,128]{3,2,1,0:T(8,128)S(1)}, u32[]{:S(2)}, u32[]{:S(2)}) collective-permute-start(f32[16,1,16,128]{3,2,1,0:T(8,128)S(1)} %get-tuple-element.92), channel_id=1, source_target_pairs={{0,1},{1,2},{2,3},{3,4},{4,5},{5,6},{6,7},{7,8},{8,9},{9,10},{10,1... | collective-permute-start | bytes 393224 | tf_op jit(solution)/shard_map/ppermute | solution.py:183
  122.8 2.1 multiply_multiply_fusion.9
  128.7 15.0 %psum.74 = f32[4,16]{1,0:T(4,128)} all-reduce(f32[4,16]{1,0:T(4,128)} %pad_maximum_fusion.12), channel_id=1, replica_groups=mesh['grp'=8,'cy'=4,'cz'=8] {'cz'}, use_global_device_ids=true, to_apply=%region_13.14 | all-reduce | flops 64 | bytes 512 | tf_op jit(solution)/shard_map/psum | solution.py:25
  143.7 7.8 %psum.75 = f32[4,16]{1,0:T(4,128)} all-reduce(f32[4,16]{1,0:T(4,128)} %psum.74), channel_id=1, replica_groups=mesh['grp'=8,'cy'=4,'cz'=8] {'cy'}, use_global_device_ids=true, to_apply=%region_14.15 | all-reduce | flops 64 | bytes 512 | tf_op jit(solution)/shard_map/psum | solution.py:25
  153.0 2.1 multiply_subtract_fusion
  155.5 1.3 collective-permute-start.8
  156.8 4.0 %collective-permute-start.9 = (f32[16,1,16,128]{3,2,1,0:T(8,128)S(1)}, f32[16,1,16,128]{3,2,1,0:T(8,128)S(1)}, u32[]{:S(2)}, u32[]{:S(2)}) collective-permute-start(f32[16,1,16,128]{3,2,1,0:T(8,128)S(1)} %get-tuple-element.90), channel_id=1, source_target_pairs={{0,1},{1,2},{2,3},{3,4},{4,5},{5,6},{6,7},{7,8},{8,9},{9,10},{10,1... | collective-permute-start | bytes 393224 | tf_op jit(solution)/shard_map/ppermute | solution.py:183
  165.1 13.9 %psum.76 = f32[5,16]{1,0:T(8,128)S(1)} all-reduce(f32[5,16]{1,0:T(8,128)S(1)} %stack.138), channel_id=1, replica_groups=mesh['grp'=8,'cy'=4,'cz'=8] {'cz'}, use_global_device_ids=true, to_apply=%region_20.21 | all-reduce | flops 80 | bytes 640 | tf_op jit(solution)/shard_map/psum | solution.py:25
  179.0 7.6 %psum.77 = f32[5,16]{1,0:T(8,128)S(1)} all-reduce(f32[5,16]{1,0:T(8,128)S(1)} %psum.76), channel_id=1, replica_groups=mesh['grp'=8,'cy'=4,'cz'=8] {'cy'}, use_global_device_ids=true, to_apply=%region_21.22 | all-reduce | flops 80 | bytes 640 | tf_op jit(solution)/shard_map/psum | solution.py:25
  186.7 2.4 multiply_reduce_fusion
  189.0 23.7 %psum.78 = f32[16]{0:T(128)S(1)} all-reduce(f32[16]{0:T(128)S(1)} %multiply_reduce_fusion), channel_id=1, replica_groups=mesh['grp'=8,'cy'=4,'cz'=8] {'cz'}, use_global_device_ids=true, to_apply=%region_23.24 | all-reduce | flops 16 | bytes 128 | tf_op jit(solution)/shard_map/psum | solution.py:25
  212.8 6.0 %psum.79 = f32[16]{0:T(128)S(1)} all-reduce(f32[16]{0:T(128)S(1)} %psum.78), channel_id=1, replica_groups=mesh['grp'=8,'cy'=4,'cz'=8] {'cy'}, use_global_device_ids=true, to_apply=%region_24.25 | all-reduce | flops 16 | bytes 128 | tf_op jit(solution)/shard_map/psum | solution.py:25
  218.9 2.9 multiply_add_fusion
  221.8 6.1 %copy.348 = f32[16,2,4,16,128]{0,4,3,2,1:T(8,128)} copy(f32[16,2,4,16,128]{4,3,2,0,1:T(8,128)} %multiply_add_fusion) | data formatting | bytes 2097152 | tf_op jit(solution)/shard_map/add | solution.py:237
  227.9 3.5 %gather_fusion.3 = f32[256,16]{1,0:T(8,128)S(1)} fusion(f32[16,2,4,16,128]{0,4,3,2,1:T(8,128)} %copy.348, s32[256]{0:T(256)S(1)} %bitcast.430), kind=kCustom, calls=%fused_computation.3 | custom fusion | bytes 36864 | tf_op jit(solution)/shard_map/gather | solution.py:251
  231.7 4.1 %collective-permute-done.10 = f32[16,256]{0,1:T(8,128)S(1)} collective-permute-done((f32[16,256]{0,1:T(8,128)S(1)}, f32[16,256]{0,1:T(8,128)S(1)}, u32[]{:S(2)}, u32[]{:S(2)}) %collective-permute-start.10) | collective-permute-done | bytes 16416 | tf_op jit(solution)/shard_map/ppermute | solution.py:29
  236.0 5.7 %collective-permute-done.11 = f32[16,256]{0,1:T(8,128)S(1)} collective-permute-done((f32[16,256]{0,1:T(8,128)S(1)}, f32[16,256]{0,1:T(8,128)S(1)}, u32[]{:S(2)}, u32[]{:S(2)}) %collective-permute-start.11) | collective-permute-done | bytes 16416 | tf_op jit(solution)/shard_map/ppermute | solution.py:29
  241.7 2.1 collective-permute-start.12
  243.8 6.3 %collective-permute-done.12 = f32[16,256]{0,1:T(8,128)S(1)} collective-permute-done((f32[16,256]{0,1:T(8,128)S(1)}, f32[16,256]{0,1:T(8,128)S(1)}, u32[]{:S(2)}, u32[]{:S(2)}) %collective-permute-start.12) | collective-permute-done | bytes 16416 | tf_op jit(solution)/shard_map/ppermute | solution.py:29
  250.2 1.4 collective-permute-start.13
  251.6 2.5 collective-permute-done.13
  256.3 3.2 collective-permute-done.14
  259.6 50.2 %all_gather.6 = f32[128,256]{1,0:T(8,128)S(1)} all-gather(f32[16,256]{1,0:T(8,128)S(1)} %copy.349), channel_id=1, replica_groups=mesh['grp'=8,'cy'=4,'cz'=8] {'grp'}, dimensions={0}, use_global_device_ids=true | all-gather | bytes 147456 | tf_op jit(solution)/shard_map/all_gather | solution.py:253
  310.2 11.7 %cholesky.17 = f32[128,128]{1,0:T(8,128)S(1)} custom-call(f32[128,128]{1,0:T(8,128)S(1)} %fusion.72), custom_call_target="Cholesky" | custom-call | tf_op jit(solution)/shard_map/jit(cholesky)/cholesky | solution.py:142
  323.3 9.8 %custom-call.10 = f32[1,128,128]{1,2,0:T(8,128)S(1)} custom-call(f32[1,128,128]{2,1,0:T(8,128)S(1)} %fusion.66), custom_call_target="InvertDiagBlocksLowerTriangular" | custom-call | tf_op jit(solution)/shard_map/jit(_cho_solve)/triangular_solve | solution.py:143
  334.1 7.1 %fusion = f32[2,8,128,128]{3,1,2,0:T(8,128)S(1)} fusion(f32[128,16384]{1,0:T(8,128)} %all-gather.2.cloned.1.call-done, f32[2,8,128,128]{3,2,1,0:T(8,128)S(1)} %bitcast.435, f32[128,128]{0,1:T(8,128)S(1)} %fusion.67, s32[]{:T(128)S(6)} %select_n.135), kind=kOutput, calls=%fused_computation.6 | convolution fusion | flops 402915328 | bytes 10493956 | tf_op jit(solution)/shard_map/dot_general | solution.py:260
  (264 shorter events, 34.6 us)
Async XLA Ops:
  7.2 20.2 %copy-start = (s32[128]{0:T(128)S(1)}, s32[128]{0:T(128)}, u32[]{:S(2)}) copy-start(s32[128]{0:T(128)} %param.18) | copy-start | bytes 1540
  7.2 326.9 %all-gather.2.cloned.1.call-start = ((), (), s32[]{:S(2)}) async-start(), calls=%async_computation | async-start | bytes 9437184 | tf_op jit(solution)/shard_map/all_gather | solution.py:262
  7.2 19.3 %copy-start.2 = (f32[16,2,4,16,128]{4,3,2,1,0:T(8,128)S(1)}, f32[16,2,4,16,128]{4,3,2,1,0:T(8,128)}, u32[]{:S(2)}) copy-start(f32[16,2,4,16,128]{4,3,2,1,0:T(8,128)} %param.10) | copy-start | bytes 3145732
  9.3 18.1 %copy-start.61 = (s32[256]{0:T(256)S(1)}, s32[256]{0:T(256)}, u32[]{:S(2)}) copy-start(s32[256]{0:T(256)} %param.19) | copy-start | bytes 3076
  9.3 36.9 %collective-permute-start = (f32[16,2,1,16,128]{4,3,2,1,0:T(8,128)}, f32[16,2,1,16,128]{4,3,2,1,0:T(8,128)}, u32[]{:S(2)}, u32[]{:S(2)}) collective-permute-start(f32[16,2,1,16,128]{4,3,2,1,0:T(8,128)} %get-tuple-element.81), channel_id=1, source_target_pairs={{0,1},{1,2},{2,3},{3,4},{4,5},{5,6},{6,7},{7,8},{8,9},{9,10},{10,1... | collective-permute-start | bytes 786440 | tf_op jit(solution)/shard_map/ppermute | solution.py:39
  14.5 31.7 %collective-permute-start.1 = (f32[16,2,1,16,128]{4,3,2,1,0:T(8,128)}, f32[16,2,1,16,128]{4,3,2,1,0:T(8,128)}, u32[]{:S(2)}, u32[]{:S(2)}) collective-permute-start(f32[16,2,1,16,128]{4,3,2,1,0:T(8,128)} %get-tuple-element.82), channel_id=1, source_target_pairs={{1,0},{2,1},{3,2},{4,3},{5,4},{6,5},{7,6},{8,7},{9,8},{10,9},{11,1... | collective-permute-start | bytes 786440 | tf_op jit(solution)/shard_map/ppermute | solution.py:42
  17.6 35.3 %collective-permute-start.2 = (f32[16,1,16,128]{3,2,1,0:T(8,128)}, f32[16,1,16,128]{3,2,1,0:T(8,128)S(1)}, u32[]{:S(2)}, u32[]{:S(2)}) collective-permute-start(f32[16,1,16,128]{3,2,1,0:T(8,128)} %get-tuple-element.95), channel_id=1, source_target_pairs={{1,0},{2,1},{3,2},{4,3},{5,4},{6,5},{7,6},{8,7},{9,8},{10,9},{11,1... | collective-permute-start | bytes 393224 | tf_op jit(solution)/shard_map/ppermute | solution.py:184
  18.9 34.0 %collective-permute-start.3 = (f32[16,1,16,128]{3,2,1,0:T(8,128)}, f32[16,1,16,128]{3,2,1,0:T(8,128)S(1)}, u32[]{:S(2)}, u32[]{:S(2)}) collective-permute-start(f32[16,1,16,128]{3,2,1,0:T(8,128)} %get-tuple-element.96), channel_id=1, source_target_pairs={{0,1},{1,2},{2,3},{3,4},{4,5},{5,6},{6,7},{7,8},{8,9},{9,10},{10,1... | collective-permute-start | bytes 393224 | tf_op jit(solution)/shard_map/ppermute | solution.py:183
  26.5 62.6 %copy-start.48 = (f32[128]{0:T(128)}, f32[128]{0:T(128)S(1)}, u32[]{:S(2)}) copy-start(f32[128]{0:T(128)S(1)} %compare_convert_fusion.2) | copy-start | bytes 1540
  26.5 62.5 %copy-start.50 = (f32[16]{0:T(128)}, f32[16]{0:T(128)S(1)}, u32[]{:S(2)}) copy-start(f32[16]{0:T(128)S(1)} %compare_convert_fusion.3) | copy-start | bytes 196
  33.6 12.5 %copy-start.32 = (f32[16,4,16,128]{3,2,1,0:T(8,128)S(1)}, f32[16,4,16,128]{3,2,1,0:T(8,128)}, u32[]{:S(2)}) copy-start(f32[16,4,16,128]{3,2,1,0:T(8,128)} %param.11) | copy-start | bytes 1572868
  82.9 8.3 %copy-start.54 = (f32[2,16]{1,0:T(2,128)}, f32[2,16]{1,0:T(2,128)S(1)}, u32[]{:S(2)}) copy-start(f32[2,16]{1,0:T(2,128)S(1)} %psum.71) | copy-start | bytes 388
  83.5 8.2 %collective-permute-start.4 = (f32[16,1,16,128]{3,2,1,0:T(8,128)S(1)}, f32[16,1,16,128]{3,2,1,0:T(8,128)S(1)}, u32[]{:S(2)}, u32[]{:S(2)}) collective-permute-start(f32[16,1,16,128]{3,2,1,0:T(8,128)S(1)} %get-tuple-element.93), channel_id=1, source_target_pairs={{1,0},{2,1},{3,2},{4,3},{5,4},{6,5},{7,6},{8,7},{9,8},{10,9},{11,1... | collective-permute-start | bytes 393224 | tf_op jit(solution)/shard_map/ppermute | solution.py:184
  84.8 6.9 %collective-permute-start.5 = (f32[16,1,16,128]{3,2,1,0:T(8,128)S(1)}, f32[16,1,16,128]{3,2,1,0:T(8,128)S(1)}, u32[]{:S(2)}, u32[]{:S(2)}) collective-permute-start(f32[16,1,16,128]{3,2,1,0:T(8,128)S(1)} %get-tuple-element.94), channel_id=1, source_target_pairs={{0,1},{1,2},{2,3},{3,4},{4,5},{5,6},{6,7},{7,8},{8,9},{9,10},{10,1... | collective-permute-start | bytes 393224 | tf_op jit(solution)/shard_map/ppermute | solution.py:183
  115.3 10.1 %copy-start.58 = (f32[16]{0:T(128)}, f32[16]{0:T(128)S(1)}, u32[]{:S(2)}) copy-start(f32[16]{0:T(128)S(1)} %get-tuple-element.110) | copy-start | bytes 196
  117.4 7.9 %collective-permute-start.6 = (f32[16,1,16,128]{3,2,1,0:T(8,128)S(1)}, f32[16,1,16,128]{3,2,1,0:T(8,128)S(1)}, u32[]{:S(2)}, u32[]{:S(2)}) collective-permute-start(f32[16,1,16,128]{3,2,1,0:T(8,128)S(1)} %get-tuple-element.91), channel_id=1, source_target_pairs={{1,0},{2,1},{3,2},{4,3},{5,4},{6,5},{7,6},{8,7},{9,8},{10,9},{11,1... | collective-permute-start | bytes 393224 | tf_op jit(solution)/shard_map/ppermute | solution.py:184
  118.7 6.6 %collective-permute-start.7 = (f32[16,1,16,128]{3,2,1,0:T(8,128)S(1)}, f32[16,1,16,128]{3,2,1,0:T(8,128)S(1)}, u32[]{:S(2)}, u32[]{:S(2)}) collective-permute-start(f32[16,1,16,128]{3,2,1,0:T(8,128)S(1)} %get-tuple-element.92), channel_id=1, source_target_pairs={{0,1},{1,2},{2,3},{3,4},{4,5},{5,6},{6,7},{7,8},{8,9},{9,10},{10,1... | collective-permute-start | bytes 393224 | tf_op jit(solution)/shard_map/ppermute | solution.py:183
  152.1 12.0 %copy-start.46 = (f32[16]{0:T(128)}, f32[16]{0:T(128)S(1)}, u32[]{:S(2)}) copy-start(f32[16]{0:T(128)S(1)} %sqrt_bitcast_fusion.1) | copy-start | bytes 196
  152.9 9.8 %copy-start.56 = (f32[16]{0:T(128)}, f32[16]{0:T(128)S(1)}, u32[]{:S(2)}) copy-start(f32[16]{0:T(128)S(1)} %get-tuple-element.105) | copy-start | bytes 196
  152.9 7.9 %copy-start.9 = (f32[16,4,16,128]{3,2,1,0:T(8,128)S(1)}, f32[16,4,16,128]{3,2,1,0:T(8,128)}, u32[]{:S(2)}) copy-start(f32[16,4,16,128]{3,2,1,0:T(8,128)} %copy-done.8) | copy-start | bytes 1572868
  152.9 7.9 %copy-start.11 = (f32[16,4,16,128]{3,2,1,0:T(8,128)S(1)}, f32[16,4,16,128]{3,2,1,0:T(8,128)}, u32[]{:S(2)}) copy-start(f32[16,4,16,128]{3,2,1,0:T(8,128)} %copy-done.10) | copy-start | bytes 1572868
  152.9 7.9 %copy-start.21 = (f32[16,4,16,128]{3,2,1,0:T(8,128)S(1)}, f32[16,4,16,128]{3,2,1,0:T(8,128)}, u32[]{:S(2)}) copy-start(f32[16,4,16,128]{3,2,1,0:T(8,128)} %get-tuple-element.50) | copy-start | bytes 1572868
  152.9 7.8 %copy-start.22 = (f32[16,4,16,128]{3,2,1,0:T(8,128)S(1)}, f32[16,4,16,128]{3,2,1,0:T(8,128)}, u32[]{:S(2)}) copy-start(f32[16,4,16,128]{3,2,1,0:T(8,128)} %get-tuple-element.72) | copy-start | bytes 1572868
  155.1 9.0 %copy-start.3 = (f32[16,2,4,16,128]{4,3,2,0,1:T(8,128)}, f32[16,2,4,16,128]{4,3,2,0,1:T(8,128)S(1)}, u32[]{:S(2)}) copy-start(f32[16,2,4,16,128]{4,3,2,0,1:T(8,128)S(1)} %multiply_subtract_fusion) | copy-start | bytes 3145732
  155.5 6.5 %collective-permute-start.8 = (f32[16,1,16,128]{3,2,1,0:T(8,128)S(1)}, f32[16,1,16,128]{3,2,1,0:T(8,128)S(1)}, u32[]{:S(2)}, u32[]{:S(2)}) collective-permute-start(f32[16,1,16,128]{3,2,1,0:T(8,128)S(1)} %get-tuple-element.89), channel_id=1, source_target_pairs={{1,0},{2,1},{3,2},{4,3},{5,4},{6,5},{7,6},{8,7},{9,8},{10,9},{11,1... | collective-permute-start | bytes 393224 | tf_op jit(solution)/shard_map/ppermute | solution.py:184
  156.8 5.9 %collective-permute-start.9 = (f32[16,1,16,128]{3,2,1,0:T(8,128)S(1)}, f32[16,1,16,128]{3,2,1,0:T(8,128)S(1)}, u32[]{:S(2)}, u32[]{:S(2)}) collective-permute-start(f32[16,1,16,128]{3,2,1,0:T(8,128)S(1)} %get-tuple-element.90), channel_id=1, source_target_pairs={{0,1},{1,2},{2,3},{3,4},{4,5},{5,6},{6,7},{7,8},{8,9},{9,10},{10,1... | collective-permute-start | bytes 393224 | tf_op jit(solution)/shard_map/ppermute | solution.py:183
  164.1 54.6 %copy-start.45 = (f32[4,16]{1,0:T(4,128)S(1)}, f32[4,16]{1,0:T(4,128)}, u32[]{:S(2)}) copy-start(f32[4,16]{1,0:T(4,128)} %psum.75) | copy-start | bytes 772
  164.2 54.6 %copy-start.53 = (f32[3,16]{1,0:T(4,128)S(1)}, f32[3,16]{1,0:T(4,128)}, u32[]{:S(2)}) copy-start(f32[3,16]{1,0:T(4,128)} %copy-done.52) | copy-start | bytes 580
  164.2 54.6 %copy-start.55 = (f32[2,16]{1,0:T(2,128)S(1)}, f32[2,16]{1,0:T(2,128)}, u32[]{:S(2)}) copy-start(f32[2,16]{1,0:T(2,128)} %copy-done.54) | copy-start | bytes 388
  164.2 54.6 %copy-start.57 = (f32[16]{0:T(128)S(1)}, f32[16]{0:T(128)}, u32[]{:S(2)}) copy-start(f32[16]{0:T(128)} %copy-done.56) | copy-start | bytes 196
  164.2 54.6 %copy-start.59 = (f32[16]{0:T(128)S(1)}, f32[16]{0:T(128)}, u32[]{:S(2)}) copy-start(f32[16]{0:T(128)} %copy-done.58) | copy-start | bytes 196
  164.2 54.6 %copy-start.62 = (f32[16]{0:T(128)S(1)}, f32[16]{0:T(128)}, u32[]{:S(2)}) copy-start(f32[16]{0:T(128)} %get-tuple-element.109) | copy-start | bytes 196
  165.0 53.9 %copy-start.47 = (f32[16]{0:T(128)S(1)}, f32[16]{0:T(128)}, u32[]{:S(2)}) copy-start(f32[16]{0:T(128)} %copy-done.46) | copy-start | bytes 196
  221.8 9.6 %copy-start.43 = (f32[256,16]{1,0:T(8,128)S(1)}, f32[256,16]{1,0:T(8,128)}, u32[]{:S(2)}) copy-start(f32[256,16]{1,0:T(8,128)} %gather_fusion.1) | copy-start | bytes 49156
  221.8 9.6 %copy-start.44 = (f32[256,16]{1,0:T(8,128)S(1)}, f32[256,16]{1,0:T(8,128)}, u32[]{:S(2)}) copy-start(f32[256,16]{1,0:T(8,128)} %gather_fusion.2) | copy-start | bytes 49156
  221.8 9.7 %copy-start.60 = (f32[256]{0:T(256)S(1)}, f32[256]{0:T(256)}, u32[]{:S(2)}) copy-start(f32[256]{0:T(256)} %get-tuple-element.33) | copy-start | bytes 3076
  221.8 9.7 %copy-start.64 = (pred[256]{0:T(512)(128)(4,1)S(1)}, pred[256]{0:T(512)(128)(4,1)}, u32[]{:S(2)}) copy-start(pred[256]{0:T(512)(128)(4,1)} %fusion.80) | copy-start | bytes 772
  221.8 33.4 %copy-start.63 = (f32[256]{0:T(256)S(1)}, f32[256]{0:T(256)}, u32[]{:S(2)}) copy-start(f32[256]{0:T(256)} %param.16) | copy-start | bytes 3076
  221.8 33.4 %copy-start.20 = (f32[16,2,4,16,128]{4,3,2,0,1:T(8,128)S(1)}, f32[16,2,4,16,128]{4,3,2,0,1:T(8,128)}, u32[]{:S(2)}) copy-start(f32[16,2,4,16,128]{4,3,2,0,1:T(8,128)} %multiply_add_fusion) | copy-start | bytes 3145732
  227.9 105.2 %copy-start.65 = (f32[128,256]{1,0:T(8,128)S(1)}, f32[128,256]{1,0:T(8,128)}, u32[]{:S(2)}) copy-start(f32[128,256]{1,0:T(8,128)} %param.17) | copy-start | bytes 393220
  227.9 105.2 %copy-start.66 = (f32[256]{0:T(256)S(1)}, f32[256]{0:T(256)}, u32[]{:S(2)}) copy-start(f32[256]{0:T(256)} %param.15) | copy-start | bytes 3076
  227.9 106.1 %copy-start.19 = (f32[16,2,4,16,128]{4,3,2,1,0:T(8,128)S(1)}, f32[16,2,4,16,128]{4,3,2,1,0:T(8,128)}, u32[]{:S(2)}) copy-start(f32[16,2,4,16,128]{4,3,2,1,0:T(8,128)} %copy-done.18) | copy-start | bytes 3145732
  231.6 4.2 %collective-permute-start.10 = (f32[16,256]{0,1:T(8,128)S(1)}, f32[16,256]{0,1:T(8,128)S(1)}, u32[]{:S(2)}, u32[]{:S(2)}) collective-permute-start(f32[16,256]{0,1:T(8,128)S(1)} %multiply_bitcast_fusion), channel_id=1, source_target_pairs={{0,1},{1,0},{2,3},{3,2},{4,5},{5,4},{6,7},{7,6},{8,9},{9,8},{10,11... | collective-permute-start | bytes 49160 | tf_op jit(solution)/shard_map/ppermute | solution.py:29
  235.9 5.8 %collective-permute-start.11 = (f32[16,256]{0,1:T(8,128)S(1)}, f32[16,256]{0,1:T(8,128)S(1)}, u32[]{:S(2)}, u32[]{:S(2)}) collective-permute-start(f32[16,256]{0,1:T(8,128)S(1)} %add.497), channel_id=1, source_target_pairs={{0,2},{1,3},{2,0},{3,1},{4,6},{5,7},{6,4},{7,5},{8,10},{9,11},{10,... | collective-permute-start | bytes 49160 | tf_op jit(solution)/shard_map/ppermute | solution.py:29
  241.7 8.5 %collective-permute-start.12 = (f32[16,256]{0,1:T(8,128)S(1)}, f32[16,256]{0,1:T(8,128)S(1)}, u32[]{:S(2)}, u32[]{:S(2)}) collective-permute-start(f32[16,256]{0,1:T(8,128)S(1)} %add.498), channel_id=1, source_target_pairs={{0,4},{1,5},{2,6},{3,7},{4,0},{5,1},{6,2},{7,3},{8,12},{9,13},{10,... | collective-permute-start | bytes 49160 | tf_op jit(solution)/shard_map/ppermute | solution.py:29
  250.2 3.9 %collective-permute-start.13 = (f32[16,256]{0,1:T(8,128)S(1)}, f32[16,256]{0,1:T(8,128)S(1)}, u32[]{:S(2)}, u32[]{:S(2)}) collective-permute-start(f32[16,256]{0,1:T(8,128)S(1)} %add.499), channel_id=1, source_target_pairs={{0,8},{8,0},{16,24},{24,16},{1,9},{9,1},{17,25},{25,17},{2,10},{10... | collective-permute-start | bytes 49160 | tf_op jit(solution)/shard_map/ppermute | solution.py:29
  254.1 5.4 %collective-permute-start.14 = (f32[16,256]{0,1:T(8,128)S(1)}, f32[16,256]{0,1:T(8,128)S(1)}, u32[]{:S(2)}, u32[]{:S(2)}) collective-permute-start(f32[16,256]{0,1:T(8,128)S(1)} %add.500), channel_id=1, source_target_pairs={{0,16},{8,24},{16,0},{24,8},{1,17},{9,25},{17,1},{25,9},{2,18},{10... | collective-permute-start | bytes 49160 | tf_op jit(solution)/shard_map/ppermute | solution.py:29
  334.1 8.4 %copy-start.1 = (s32[128]{0:T(128)S(1)}, s32[128]{0:T(128)}, u32[]{:S(2)}) copy-start(s32[128]{0:T(128)} %param.18) | copy-start | bytes 1540
  (35 other events, 89.3 us)
Sparse Core Ops, SparseCore 0:
  26.6 56.9 all-gather.1

commit v4 on v3

--- a/solution.py
+++ b/solution.py
@@ -127,17 +127,18 @@
     return solved
 
 
-def ensemble_weights(predicted, obs_values, obs_error, noise):
+def ensemble_weights(predicted, obs_values, obs_error, noise, offset, count):
     members = predicted.shape[0]
     sigma = math.sqrt(inflation) * obs_error
     center = jnp.mean(predicted, axis=0)
     spread = (predicted - center) / (math.sqrt(members - 1.0) * sigma)
     innov = (obs_values + sigma * noise - predicted) / sigma
+    own_innov = lax.dynamic_slice_in_dim(innov, offset, count, 0)
     gram = jnp.eye(members, dtype=jnp.float32) + jnp.dot(
         spread, spread.T, precision=lax.Precision.HIGHEST, preferred_element_type=jnp.float32
     )
     cross = jnp.dot(
-        spread, innov.T, precision=lax.Precision.HIGHEST, preferred_element_type=jnp.float32
+        spread, own_innov.T, precision=lax.Precision.HIGHEST, preferred_element_type=jnp.float32
     )
     factor = jnp.linalg.cholesky(gram)
     return jax.scipy.linalg.cho_solve((factor, True), cross)
@@ -240,23 +241,30 @@
     component = (jnp.arange(obs_well.shape[0], dtype=jnp.int32) >= wells).astype(jnp.int32)
     slab_row = cells // plane - slab_index * slab_x
     inside = (slab_row >= 0) & (slab_row < slab_x)
-    row = jnp.where(inside, slab_row, 0)
-    col_y = (cells % plane) // plane_cols
+    rows = 2 * slab_x * plane_rows
+    row = component * (slab_x * plane_rows) + slab_row * plane_rows + (cells % plane) // plane_cols
     col_z = cells % plane_cols
-    state = jnp.where(
-        component[None, :] > 0,
-        saturation[:, row, col_y, col_z],
-        pressure[:, row, col_y, col_z],
-    )
-    picked = (state + increment[:, component, row, col_y, col_z]) * inside.astype(jnp.float32)
+    state = jnp.stack([pressure + increment[:, 0], saturation + increment[:, 1]], 1)
+    table = state.reshape(local_members * rows, plane_cols)
+    pick_z = (lax.broadcasted_iota(jnp.int32, (plane_cols, cells.shape[0]), 0) == col_z[None, :])
+    by_row = jnp.dot(
+        table,
+        pick_z.astype(jnp.float32),
+        precision=lax.Precision.HIGHEST,
+        preferred_element_type=jnp.float32,
+    )
+    pick_row = (lax.broadcasted_iota(jnp.int32, (rows, cells.shape[0]), 0) == row[None, :]) & inside[None, :]
+    picked = jnp.sum(
+        by_row.reshape(local_members, rows, cells.shape[0]) * pick_row.astype(jnp.float32)[None],
+        axis=1,
+    )
     slab_pred = cell_sum(picked, doubling=True)
     predicted = lax.all_gather(slab_pred, "grp", axis=0, tiled=True)
-    weights = ensemble_weights(predicted, obs_values, obs_error, noise)
     params = jnp.stack([log_perm, porosity], 1).reshape(local_members, 2 * cells_dev)
     offset = lax.axis_index("grp") * local_members
+    own_columns = ensemble_weights(predicted, obs_values, obs_error, noise, offset, local_members)
     scale_factor = 1.0 / math.sqrt(members - 1.0)
     scaled = params * scale_factor
-    own_columns = lax.dynamic_slice_in_dim(weights, offset, local_members, 1)
     update = jnp.dot(
         own_columns.T,
         lax.all_gather(scaled, "grp", axis=0, tiled=True),

time: 353 us -> 313 us (0.89)
  local copies, waits for them, and re-layouts: 36.8 us -> 18.7 us
  blocking collectives: 171 us -> 161 us
  waiting for transfers between devices: 22.6 us -> 15.8 us
  other arithmetic: 61.7 us -> 57.2 us
    psum x10, blocking collectives: 121 us -> 110 us  [cell_sum(): values = lax.psum(values, axis)]
    gather x3 -> x0, local copies, waits for them, and re-layouts: 9.81 us -> none  [the longest x1 3.51 us: local(): increment[:, component, row, col_y, col_z]]
    ppermute x5, waiting for transfers between devices: 21.8 us -> 14.3 us  [cell_sum(): lax.ppermute(values, axis, [(i, i ^ step) for i in range(size)])]
    add x2 -> x0, local copies, waits for them, and re-layouts: 6.14 us -> none  [the longest x1 6.08 us: local(): increment = increment + expand(solved[jdx]) * basis[jdx]]
    mul x5, other arithmetic: 9.13 us -> 4.25 us  [net(): flow_z = coef_z * diff_z]
    unnamed x138 -> x151, local copies, waits for them, and re-layouts: 8.98 us -> 10.4 us
  transfers between devices with their start and end apart: 16 -> 16, of which waited for: 6 -> 7; matrix products, arithmetic and copies ran while one was open for 27% -> 21% of each run, Pallas kernels for 0% -> 0%
where the time goes in v4:
time: 313 us; the launch traced here: 311 us
  blocking collectives  161 us (51%)
  other arithmetic  57.2 us (18%)
  starting transfers between devices  33.4 us (11%)
  local copies, waits for them, and re-layouts  18.7 us (6%)
  waiting for transfers between devices  15.8 us (5%)
  between operations  15.6 us (5%)
  matrix products  9.86 us (3%)
    psum x10, blocking collectives, cell_sum(): values = lax.psum(values, axis)  110 us
    all_gather x1, blocking collectives, local(): predicted = lax.all_gather(slab_pred, 'grp', axis=0, tiled=True)  50.6 us
    ppermute x4, starting transfers between devices, planes(): low = lax.ppermute(field[:, -1:], CELL, forward)  16.8 us
    ppermute x5, waiting for transfers between devices, cell_sum(): lax.ppermute(values, axis, [(i, i ^ step) for i in range(size)])  14.3 us
    another operation x3, other arithmetic, ensemble_weights(): factor = jnp.linalg.cholesky(gram)  12.4 us
    another operation x2, other arithmetic, ensemble_weights(): return jax.scipy.linalg.cho_solve((factor, True), cross)  10.5 us
    unnamed x151, local copies, waits for them, and re-layouts  10.4 us
    dot_general x1, matrix products, local(): jnp.dot(own_columns.T, lax.all_gather(scaled, 'grp', axis=0, tiled=True),...  7.1 us
  transfers between devices with their start and end apart: 16, of which 7 were waited for; matrix products, arithmetic and copies ran while one was open for 21% of the time, Pallas kernels for 0%

profile of v4, /device:TPU:1, one launch (start us, length us, event | category | flops | bytes accessed | tf_op | source)
XLA Modules:
  0.0 311.5 jit_solution(745330859704109445)
XLA Ops:
  7.3 2.1 fusion.58
  9.3 5.1 %collective-permute-start = (f32[16,2,1,16,128]{4,3,2,0,1:T(8,128)}, f32[16,2,1,16,128]{4,3,2,0,1:T(8,128)}, u32[]{:S(2)}, u32[]{:S(2)}) collective-permute-start(f32[16,2,1,16,128]{4,3,2,0,1:T(8,128)} %get-tuple-element.65), channel_id=1, source_target_pairs={{0,1},{1,2},{2,3},{3,4},{4,5},{5,6},{6,7},{7,8},{8,9},{9,10},{10,1... | collective-permute-start | bytes 786440 | tf_op jit(solution)/shard_map/ppermute | solution.py:39
  14.4 1.3 collective-permute-start.1
  16.4 1.3 collective-permute-start.2
  17.7 4.6 %collective-permute-start.3 = (f32[16,1,16,128]{3,2,1,0:T(8,128)S(1)}, f32[16,1,16,128]{3,2,1,0:T(8,128)S(1)}, u32[]{:S(2)}, u32[]{:S(2)}) collective-permute-start(f32[16,1,16,128]{3,2,1,0:T(8,128)S(1)} %get-tuple-element.80), channel_id=1, source_target_pairs={{0,1},{1,2},{2,3},{3,4},{4,5},{5,6},{6,7},{7,8},{8,9},{9,10},{10,1... | collective-permute-start | bytes 393224 | tf_op jit(solution)/shard_map/ppermute | solution.py:184
  22.6 1.0 copy-done.27
  23.6 1.7 bitcast_multiply_fusion
  26.1 2.4 gather_fusion
  28.6 1.3 and_select_fusion.3
  31.1 1.1 pad_maximum_fusion
  33.8 1.6 fusion.96
  35.9 1.7 fusion.57
  39.3 19.1 %psum.70 = f32[2,16]{1,0:T(2,128)S(1)} all-reduce(f32[2,16]{1,0:T(2,128)S(1)} %pad_maximum_fusion.14), channel_id=1, replica_groups=mesh['grp'=8,'cy'=4,'cz'=8] {'cz'}, use_global_device_ids=true, to_apply=%region_2.3 | all-reduce | flops 32 | bytes 256 | tf_op jit(solution)/shard_map/psum | solution.py:25
  58.4 8.1 %psum.71 = f32[2,16]{1,0:T(2,128)S(1)} all-reduce(f32[2,16]{1,0:T(2,128)S(1)} %psum.70), channel_id=1, replica_groups=mesh['grp'=8,'cy'=4,'cz'=8] {'cy'}, use_global_device_ids=true, to_apply=%region_3.4 | all-reduce | flops 32 | bytes 256 | tf_op jit(solution)/shard_map/psum | solution.py:25
  67.4 1.4 collective-permute-start.4
  68.9 4.0 %collective-permute-start.5 = (f32[16,1,16,128]{3,2,1,0:T(8,128)S(1)}, f32[16,1,16,128]{3,2,1,0:T(8,128)S(1)}, u32[]{:S(2)}, u32[]{:S(2)}) collective-permute-start(f32[16,1,16,128]{3,2,1,0:T(8,128)S(1)} %get-tuple-element.78), channel_id=1, source_target_pairs={{0,1},{1,2},{2,3},{3,4},{4,5},{5,6},{6,7},{7,8},{8,9},{9,10},{10,1... | collective-permute-start | bytes 393224 | tf_op jit(solution)/shard_map/ppermute | solution.py:184
  73.5 1.2 broadcast_divide_fusion
  78.2 12.4 %psum.72 = f32[3,16]{1,0:T(4,128)S(1)} all-reduce(f32[3,16]{1,0:T(4,128)S(1)} %pad_maximum_fusion.12), channel_id=1, replica_groups=mesh['grp'=8,'cy'=4,'cz'=8] {'cz'}, use_global_device_ids=true, to_apply=%region_7.8 | all-reduce | flops 48 | bytes 384 | tf_op jit(solution)/shard_map/psum | solution.py:25
  90.6 7.3 %psum.73 = f32[3,16]{1,0:T(4,128)S(1)} all-reduce(f32[3,16]{1,0:T(4,128)S(1)} %psum.72), channel_id=1, replica_groups=mesh['grp'=8,'cy'=4,'cz'=8] {'cy'}, use_global_device_ids=true, to_apply=%region_8.9 | all-reduce | flops 48 | bytes 384 | tf_op jit(solution)/shard_map/psum | solution.py:25
  98.5 2.5 multiply_subtract_fusion.1
  102.1 1.3 collective-permute-start.6
  103.4 4.2 %collective-permute-start.7 = (f32[16,1,16,128]{3,2,1,0:T(8,128)S(1)}, f32[16,1,16,128]{3,2,1,0:T(8,128)S(1)}, u32[]{:S(2)}, u32[]{:S(2)}) collective-permute-start(f32[16,1,16,128]{3,2,1,0:T(8,128)S(1)} %get-tuple-element.76), channel_id=1, source_target_pairs={{0,1},{1,2},{2,3},{3,4},{4,5},{5,6},{6,7},{7,8},{8,9},{9,10},{10,1... | collective-permute-start | bytes 393224 | tf_op jit(solution)/shard_map/ppermute | solution.py:184
  113.7 14.9 %psum.74 = f32[4,16]{1,0:T(4,128)} all-reduce(f32[4,16]{1,0:T(4,128)S(1)} %pad_maximum_fusion.13), channel_id=1, replica_groups=mesh['grp'=8,'cy'=4,'cz'=8] {'cz'}, use_global_device_ids=true, to_apply=%region_13.14 | all-reduce | flops 64 | bytes 512 | tf_op jit(solution)/shard_map/psum | solution.py:25
  128.6 8.6 %psum.75 = f32[4,16]{1,0:T(4,128)} all-reduce(f32[4,16]{1,0:T(4,128)} %psum.74), channel_id=1, replica_groups=mesh['grp'=8,'cy'=4,'cz'=8] {'cy'}, use_global_device_ids=true, to_apply=%region_14.15 | all-reduce | flops 64 | bytes 512 | tf_op jit(solution)/shard_map/psum | solution.py:25
  138.7 2.3 copy_subtract_fusion
  141.4 1.0 copy-done.38
  142.5 1.3 collective-permute-start.8
  143.8 4.0 %collective-permute-start.9 = (f32[16,1,16,128]{3,2,1,0:T(8,128)S(1)}, f32[16,1,16,128]{3,2,1,0:T(8,128)S(1)}, u32[]{:S(2)}, u32[]{:S(2)}) collective-permute-start(f32[16,1,16,128]{3,2,1,0:T(8,128)S(1)} %get-tuple-element.74), channel_id=1, source_target_pairs={{0,1},{1,2},{2,3},{3,4},{4,5},{5,6},{6,7},{7,8},{8,9},{9,10},{10,1... | collective-permute-start | bytes 393224 | tf_op jit(solution)/shard_map/ppermute | solution.py:184
  153.6 14.0 %psum.76 = f32[5,16]{1,0:T(8,128)S(1)} all-reduce(f32[5,16]{1,0:T(8,128)S(1)} %stack.147), channel_id=1, replica_groups=mesh['grp'=8,'cy'=4,'cz'=8] {'cz'}, use_global_device_ids=true, to_apply=%region_20.21 | all-reduce | flops 80 | bytes 640 | tf_op jit(solution)/shard_map/psum | solution.py:25
  167.6 7.9 %psum.77 = f32[5,16]{1,0:T(8,128)S(1)} all-reduce(f32[5,16]{1,0:T(8,128)S(1)} %psum.76), channel_id=1, replica_groups=mesh['grp'=8,'cy'=4,'cz'=8] {'cy'}, use_global_device_ids=true, to_apply=%region_21.22 | all-reduce | flops 80 | bytes 640 | tf_op jit(solution)/shard_map/psum | solution.py:25
  175.6 2.3 multiply_reduce_fusion.1
  177.9 12.1 %psum.78 = f32[16]{0:T(128)S(1)} all-reduce(f32[16]{0:T(128)S(1)} %multiply_reduce_fusion.1), channel_id=1, replica_groups=mesh['grp'=8,'cy'=4,'cz'=8] {'cz'}, use_global_device_ids=true, to_apply=%region_23.24 | all-reduce | flops 16 | bytes 128 | tf_op jit(solution)/shard_map/psum | solution.py:25
  190.0 6.0 %psum.79 = f32[16]{0:T(128)S(1)} all-reduce(f32[16]{0:T(128)S(1)} %psum.78), channel_id=1, replica_groups=mesh['grp'=8,'cy'=4,'cz'=8] {'cy'}, use_global_device_ids=true, to_apply=%region_24.25 | all-reduce | flops 16 | bytes 128 | tf_op jit(solution)/shard_map/psum | solution.py:25
  196.2 2.1 multiply_add_fusion
  200.3 1.0 multiply_reduce_fusion
  201.4 2.6 collective-permute-done.10
  204.0 3.5 %collective-permute-done.11 = f32[16,256]{1,0:T(8,128)S(1)} collective-permute-done((f32[16,256]{1,0:T(8,128)S(1)}, f32[16,256]{1,0:T(8,128)S(1)}, u32[]{:S(2)}, u32[]{:S(2)}) %collective-permute-start.11) | collective-permute-done | bytes 16416 | tf_op jit(solution)/shard_map/ppermute | solution.py:29
  207.5 2.1 collective-permute-start.12
  209.6 4.4 %collective-permute-done.12 = f32[16,256]{1,0:T(8,128)S(1)} collective-permute-done((f32[16,256]{1,0:T(8,128)S(1)}, f32[16,256]{1,0:T(8,128)S(1)}, u32[]{:S(2)}, u32[]{:S(2)}) %collective-permute-start.12) | collective-permute-done | bytes 16416 | tf_op jit(solution)/shard_map/ppermute | solution.py:29
  214.0 1.4 collective-permute-start.13
  215.4 1.1 collective-permute-done.13
  216.6 1.4 collective-permute-start.14
  218.0 2.7 collective-permute-done.14
  220.7 50.6 %all_gather.6 = f32[128,256]{1,0:T(8,128)S(1)} all-gather(f32[16,256]{1,0:T(8,128)S(1)} %add.480), channel_id=1, replica_groups=mesh['grp'=8,'cy'=4,'cz'=8] {'grp'}, dimensions={0}, use_global_device_ids=true | all-gather | bytes 147456 | tf_op jit(solution)/shard_map/all_gather | solution.py:262
  271.8 11.7 %cholesky.17 = f32[128,128]{1,0:T(8,128)S(1)} custom-call(f32[128,128]{1,0:T(8,128)S(1)} %fusion.73), custom_call_target="Cholesky" | custom-call | tf_op jit(solution)/shard_map/jit(cholesky)/cholesky | solution.py:143
  284.9 9.8 %custom-call.10 = f32[1,128,128]{1,2,0:T(8,128)S(1)} custom-call(f32[1,128,128]{2,1,0:T(8,128)S(1)} %fusion.67), custom_call_target="InvertDiagBlocksLowerTriangular" | custom-call | tf_op jit(solution)/shard_map/jit(_cho_solve)/triangular_solve | solution.py:144
  296.2 7.1 %fusion = f32[2,8,128,128]{3,1,2,0:T(8,128)S(1)} fusion(f32[128,16]{1,0:T(8,128)S(1)} %fusion.68, f32[128,16384]{1,0:T(8,128)} %all-gather.2.cloned.1.call-done, f32[2,8,128,128]{3,2,1,0:T(8,128)S(1)} %bitcast.449), kind=kOutput, calls=%fused_computation.4 | convolution fusion | flops 402915328 | bytes 10493952 | tf_op jit(solution)/shard_map/dot_general | solution.py:268
  303.5 1.1 slice_bitcast_fusion.1
  (275 shorter events, 32.3 us)
Async XLA Ops:
  7.2 19.0 %copy-start = (s32[128]{0:T(128)S(1)}, s32[128]{0:T(128)}, u32[]{:S(2)}) copy-start(s32[128]{0:T(128)} %param.18) | copy-start | bytes 1540
  7.2 8.5 %copy-start.2 = (f32[16,2,4,16,128]{4,3,2,1,0:T(8,128)S(1)}, f32[16,2,4,16,128]{4,3,2,1,0:T(8,128)}, u32[]{:S(2)}) copy-start(f32[16,2,4,16,128]{4,3,2,1,0:T(8,128)} %param.10) | copy-start | bytes 3145732
  7.2 289.0 %all-gather.2.cloned.1.call-start = ((), (), s32[]{:S(2)}) async-start(), calls=%async_computation | async-start | bytes 9437184 | tf_op jit(solution)/shard_map/all_gather | solution.py:270
  7.2 15.1 %copy-start.8 = (f32[16,4,16,128]{3,2,1,0:T(8,128)S(1)}, f32[16,4,16,128]{3,2,1,0:T(8,128)}, u32[]{:S(2)}) copy-start(f32[16,4,16,128]{3,2,1,0:T(8,128)} %param.12) | copy-start | bytes 1572868
  7.2 15.1 %copy-start.40 = (f32[16,4,16,128]{3,2,1,0:T(8,128)S(1)}, f32[16,4,16,128]{3,2,1,0:T(8,128)}, u32[]{:S(2)}) copy-start(f32[16,4,16,128]{3,2,1,0:T(8,128)} %param.11) | copy-start | bytes 1572868
  9.3 21.8 %collective-permute-start = (f32[16,2,1,16,128]{4,3,2,0,1:T(8,128)}, f32[16,2,1,16,128]{4,3,2,0,1:T(8,128)}, u32[]{:S(2)}, u32[]{:S(2)}) collective-permute-start(f32[16,2,1,16,128]{4,3,2,0,1:T(8,128)} %get-tuple-element.65), channel_id=1, source_target_pairs={{0,1},{1,2},{2,3},{3,4},{4,5},{5,6},{6,7},{7,8},{8,9},{9,10},{10,1... | collective-permute-start | bytes 786440 | tf_op jit(solution)/shard_map/ppermute | solution.py:39
  14.4 16.8 %collective-permute-start.1 = (f32[16,2,1,16,128]{4,3,2,0,1:T(8,128)}, f32[16,2,1,16,128]{4,3,2,0,1:T(8,128)}, u32[]{:S(2)}, u32[]{:S(2)}) collective-permute-start(f32[16,2,1,16,128]{4,3,2,0,1:T(8,128)} %get-tuple-element.66), channel_id=1, source_target_pairs={{1,0},{2,1},{3,2},{4,3},{5,4},{6,5},{7,6},{8,7},{9,8},{10,9},{11,1... | collective-permute-start | bytes 786440 | tf_op jit(solution)/shard_map/ppermute | solution.py:42
  16.4 19.5 %collective-permute-start.2 = (f32[16,1,16,128]{3,2,1,0:T(8,128)}, f32[16,1,16,128]{3,2,1,0:T(8,128)S(1)}, u32[]{:S(2)}, u32[]{:S(2)}) collective-permute-start(f32[16,1,16,128]{3,2,1,0:T(8,128)} %get-tuple-element.79), channel_id=1, source_target_pairs={{1,0},{2,1},{3,2},{4,3},{5,4},{6,5},{7,6},{8,7},{9,8},{10,9},{11,1... | collective-permute-start | bytes 393224 | tf_op jit(solution)/shard_map/ppermute | solution.py:185
  17.7 18.2 %collective-permute-start.3 = (f32[16,1,16,128]{3,2,1,0:T(8,128)S(1)}, f32[16,1,16,128]{3,2,1,0:T(8,128)S(1)}, u32[]{:S(2)}, u32[]{:S(2)}) collective-permute-start(f32[16,1,16,128]{3,2,1,0:T(8,128)S(1)} %get-tuple-element.80), channel_id=1, source_target_pairs={{0,1},{1,2},{2,3},{3,4},{4,5},{5,6},{6,7},{7,8},{8,9},{9,10},{10,1... | collective-permute-start | bytes 393224 | tf_op jit(solution)/shard_map/ppermute | solution.py:184
  25.3 82.3 %copy-start.55 = (f32[128]{0:T(128)}, f32[128]{0:T(128)S(1)}, u32[]{:S(2)}) copy-start(f32[128]{0:T(128)S(1)} %compare_convert_fusion) | copy-start | bytes 1540
  25.3 47.6 %copy-start.57 = (f32[16]{0:T(128)}, f32[16]{0:T(128)S(1)}, u32[]{:S(2)}) copy-start(f32[16]{0:T(128)S(1)} %compare_convert_fusion.1) | copy-start | bytes 196
  38.6 38.7 %copy-start.5 = (f32[16,1,4,16,128]{4,3,2,0,1:T(8,128)}, f32[16,1,4,16,128]{4,3,2,0,1:T(8,128)S(1)}, u32[]{:S(2)}) copy-start(f32[16,1,4,16,128]{4,3,2,0,1:T(8,128)S(1)} %fusion.46) | copy-start | bytes 1572868
  67.0 9.7 %copy-start.12 = (f32[16,2,4,16,128]{4,3,2,0,1:T(8,128)}, f32[16,2,4,16,128]{4,3,2,0,1:T(8,128)S(1)}, u32[]{:S(2)}) copy-start(f32[16,2,4,16,128]{4,3,2,0,1:T(8,128)S(1)} %multiply_subtract_fusion.2) | copy-start | bytes 3145732
  67.4 7.7 %collective-permute-start.4 = (f32[16,1,16,128]{3,2,1,0:T(8,128)S(1)}, f32[16,1,16,128]{3,2,1,0:T(8,128)S(1)}, u32[]{:S(2)}, u32[]{:S(2)}) collective-permute-start(f32[16,1,16,128]{3,2,1,0:T(8,128)S(1)} %get-tuple-element.77), channel_id=1, source_target_pairs={{1,0},{2,1},{3,2},{4,3},{5,4},{6,5},{7,6},{8,7},{9,8},{10,9},{11,1... | collective-permute-start | bytes 393224 | tf_op jit(solution)/shard_map/ppermute | solution.py:185
  68.9 6.3 %collective-permute-start.5 = (f32[16,1,16,128]{3,2,1,0:T(8,128)S(1)}, f32[16,1,16,128]{3,2,1,0:T(8,128)S(1)}, u32[]{:S(2)}, u32[]{:S(2)}) collective-permute-start(f32[16,1,16,128]{3,2,1,0:T(8,128)S(1)} %get-tuple-element.78), channel_id=1, source_target_pairs={{0,1},{1,2},{2,3},{3,4},{4,5},{5,6},{6,7},{7,8},{8,9},{9,10},{10,1... | collective-permute-start | bytes 393224 | tf_op jit(solution)/shard_map/ppermute | solution.py:184
  77.6 20.3 %copy-start.63 = (f32[2,16]{1,0:T(2,128)S(1)}, f32[2,16]{1,0:T(2,128)}, u32[]{:S(2)}) copy-start(f32[2,16]{1,0:T(2,128)} %copy-done.62) | copy-start | bytes 388
  98.5 10.8 %copy-start.67 = (f32[16]{0:T(128)}, f32[16]{0:T(128)S(1)}, u32[]{:S(2)}) copy-start(f32[16]{0:T(128)S(1)} %get-tuple-element.94) | copy-start | bytes 196
  101.1 6.5 %copy-start.15 = (f32[16,4,16,128]{3,2,1,0:T(8,128)S(1)}, f32[16,4,16,128]{3,2,1,0:T(8,128)}, u32[]{:S(2)}) copy-start(f32[16,4,16,128]{3,2,1,0:T(8,128)} %copy-done.13) | copy-start | bytes 1572868
  101.1 6.5 %copy-start.19 = (f32[16,4,16,128]{3,2,1,0:T(8,128)S(1)}, f32[16,4,16,128]{3,2,1,0:T(8,128)}, u32[]{:S(2)}) copy-start(f32[16,4,16,128]{3,2,1,0:T(8,128)} %copy-done.17) | copy-start | bytes 1572868
  101.1 6.5 %copy-start.30 = (f32[16,4,16,128]{3,2,1,0:T(8,128)S(1)}, f32[16,4,16,128]{3,2,1,0:T(8,128)}, u32[]{:S(2)}) copy-start(f32[16,4,16,128]{3,2,1,0:T(8,128)} %get-tuple-element.30) | copy-start | bytes 1572868
  101.1 6.5 %copy-start.33 = (f32[16,4,16,128]{3,2,1,0:T(8,128)S(1)}, f32[16,4,16,128]{3,2,1,0:T(8,128)}, u32[]{:S(2)}) copy-start(f32[16,4,16,128]{3,2,1,0:T(8,128)} %get-tuple-element.52) | copy-start | bytes 1572868
  101.1 6.5 %copy-start.58 = (f32[16]{0:T(128)S(1)}, f32[16]{0:T(128)}, u32[]{:S(2)}) copy-start(f32[16]{0:T(128)} %copy-done.57) | copy-start | bytes 196
  102.1 6.6 %collective-permute-start.6 = (f32[16,1,16,128]{3,2,1,0:T(8,128)S(1)}, f32[16,1,16,128]{3,2,1,0:T(8,128)S(1)}, u32[]{:S(2)}, u32[]{:S(2)}) collective-permute-start(f32[16,1,16,128]{3,2,1,0:T(8,128)S(1)} %get-tuple-element.75), channel_id=1, source_target_pairs={{1,0},{2,1},{3,2},{4,3},{5,4},{6,5},{7,6},{8,7},{9,8},{10,9},{11,1... | collective-permute-start | bytes 393224 | tf_op jit(solution)/shard_map/ppermute | solution.py:185
  103.4 5.9 %collective-permute-start.7 = (f32[16,1,16,128]{3,2,1,0:T(8,128)S(1)}, f32[16,1,16,128]{3,2,1,0:T(8,128)S(1)}, u32[]{:S(2)}, u32[]{:S(2)}) collective-permute-start(f32[16,1,16,128]{3,2,1,0:T(8,128)S(1)} %get-tuple-element.76), channel_id=1, source_target_pairs={{0,1},{1,2},{2,3},{3,4},{4,5},{5,6},{6,7},{7,8},{8,9},{9,10},{10,1... | collective-permute-start | bytes 393224 | tf_op jit(solution)/shard_map/ppermute | solution.py:184
  138.6 11.0 %copy-start.65 = (f32[16]{0:T(128)}, f32[16]{0:T(128)S(1)}, u32[]{:S(2)}) copy-start(f32[16]{0:T(128)S(1)} %get-tuple-element.87) | copy-start | bytes 196
  141.0 11.0 %copy-start.3 = (f32[16,2,4,16,128]{4,3,2,1,0:T(8,128)}, f32[16,2,4,16,128]{4,3,2,1,0:T(8,128)S(1)}, u32[]{:S(2)}) copy-start(f32[16,2,4,16,128]{4,3,2,1,0:T(8,128)S(1)} %copy_subtract_fusion) | copy-start | bytes 3145732
  141.1 6.7 %copy-start.16 = (f32[16,4,16,128]{3,2,1,0:T(8,128)S(1)}, f32[16,4,16,128]{3,2,1,0:T(8,128)}, u32[]{:S(2)}) copy-start(f32[16,4,16,128]{3,2,1,0:T(8,128)} %copy-done.13) | copy-start | bytes 1572868
  141.1 6.7 %copy-start.20 = (f32[16,4,16,128]{3,2,1,0:T(8,128)S(1)}, f32[16,4,16,128]{3,2,1,0:T(8,128)}, u32[]{:S(2)}) copy-start(f32[16,4,16,128]{3,2,1,0:T(8,128)} %copy-done.17) | copy-start | bytes 1572868
  141.1 6.7 %copy-start.31 = (f32[16,4,16,128]{3,2,1,0:T(8,128)S(1)}, f32[16,4,16,128]{3,2,1,0:T(8,128)}, u32[]{:S(2)}) copy-start(f32[16,4,16,128]{3,2,1,0:T(8,128)} %get-tuple-element.30) | copy-start | bytes 1572868
  141.1 6.7 %copy-start.34 = (f32[16,4,16,128]{3,2,1,0:T(8,128)S(1)}, f32[16,4,16,128]{3,2,1,0:T(8,128)}, u32[]{:S(2)}) copy-start(f32[16,4,16,128]{3,2,1,0:T(8,128)} %get-tuple-element.52) | copy-start | bytes 1572868
  141.1 6.7 %copy-start.56 = (f32[128]{0:T(128)S(1)}, f32[128]{0:T(128)}, u32[]{:S(2)}) copy-start(f32[128]{0:T(128)} %copy-done.55) | copy-start | bytes 1540
  141.1 6.7 %copy-start.59 = (f32[16]{0:T(128)S(1)}, f32[16]{0:T(128)}, u32[]{:S(2)}) copy-start(f32[16]{0:T(128)} %copy-done.57) | copy-start | bytes 196
  142.5 6.4 %collective-permute-start.8 = (f32[16,1,16,128]{3,2,1,0:T(8,128)S(1)}, f32[16,1,16,128]{3,2,1,0:T(8,128)S(1)}, u32[]{:S(2)}, u32[]{:S(2)}) collective-permute-start(f32[16,1,16,128]{3,2,1,0:T(8,128)S(1)} %get-tuple-element.73), channel_id=1, source_target_pairs={{1,0},{2,1},{3,2},{4,3},{5,4},{6,5},{7,6},{8,7},{9,8},{10,9},{11,1... | collective-permute-start | bytes 393224 | tf_op jit(solution)/shard_map/ppermute | solution.py:185
  143.8 5.9 %collective-permute-start.9 = (f32[16,1,16,128]{3,2,1,0:T(8,128)S(1)}, f32[16,1,16,128]{3,2,1,0:T(8,128)S(1)}, u32[]{:S(2)}, u32[]{:S(2)}) collective-permute-start(f32[16,1,16,128]{3,2,1,0:T(8,128)S(1)} %get-tuple-element.74), channel_id=1, source_target_pairs={{0,1},{1,2},{2,3},{3,4},{4,5},{5,6},{6,7},{7,8},{8,9},{9,10},{10,1... | collective-permute-start | bytes 393224 | tf_op jit(solution)/shard_map/ppermute | solution.py:184
  175.5 20.5 %copy-start.54 = (f32[4,16]{1,0:T(4,128)S(1)}, f32[4,16]{1,0:T(4,128)}, u32[]{:S(2)}) copy-start(f32[4,16]{1,0:T(4,128)} %psum.75) | copy-start | bytes 772
  175.5 20.5 %copy-start.61 = (f32[3,16]{1,0:T(4,128)S(1)}, f32[3,16]{1,0:T(4,128)}, u32[]{:S(2)}) copy-start(f32[3,16]{1,0:T(4,128)} %copy-done.60) | copy-start | bytes 580
  175.5 20.5 %copy-start.64 = (f32[2,16]{1,0:T(2,128)S(1)}, f32[2,16]{1,0:T(2,128)}, u32[]{:S(2)}) copy-start(f32[2,16]{1,0:T(2,128)} %copy-done.62) | copy-start | bytes 388
  175.5 20.5 %copy-start.66 = (f32[16]{0:T(128)S(1)}, f32[16]{0:T(128)}, u32[]{:S(2)}) copy-start(f32[16]{0:T(128)} %copy-done.65) | copy-start | bytes 196
  175.6 20.5 %copy-start.68 = (f32[16]{0:T(128)S(1)}, f32[16]{0:T(128)}, u32[]{:S(2)}) copy-start(f32[16]{0:T(128)} %copy-done.67) | copy-start | bytes 196
  175.6 20.5 %copy-start.72 = (f32[16]{0:T(128)S(1)}, f32[16]{0:T(128)}, u32[]{:S(2)}) copy-start(f32[16]{0:T(128)} %get-tuple-element.93) | copy-start | bytes 196
  199.4 18.6 %copy-start.73 = (f32[256]{0:T(256)S(1)}, f32[256]{0:T(256)}, u32[]{:S(2)}) copy-start(f32[256]{0:T(256)} %param.16) | copy-start | bytes 3076
  199.5 95.1 %copy-start.74 = (f32[256]{0:T(256)S(1)}, f32[256]{0:T(256)}, u32[]{:S(2)}) copy-start(f32[256]{0:T(256)} %param.15) | copy-start | bytes 3076
  200.3 95.9 %copy-start.28 = (f32[16,2,4,16,128]{4,3,2,1,0:T(8,128)S(1)}, f32[16,2,4,16,128]{4,3,2,1,0:T(8,128)}, u32[]{:S(2)}) copy-start(f32[16,2,4,16,128]{4,3,2,1,0:T(8,128)} %copy-done.27) | copy-start | bytes 3145732
  201.3 2.7 collective-permute-start.10
  204.0 3.5 %collective-permute-start.11 = (f32[16,256]{1,0:T(8,128)S(1)}, f32[16,256]{1,0:T(8,128)S(1)}, u32[]{:S(2)}, u32[]{:S(2)}) collective-permute-start(f32[16,256]{1,0:T(8,128)S(1)} %add.476), channel_id=1, source_target_pairs={{0,2},{1,3},{2,0},{3,1},{4,6},{5,7},{6,4},{7,5},{8,10},{9,11},{10,... | collective-permute-start | bytes 49160 | tf_op jit(solution)/shard_map/ppermute | solution.py:29
  207.5 6.5 %collective-permute-start.12 = (f32[16,256]{1,0:T(8,128)S(1)}, f32[16,256]{1,0:T(8,128)S(1)}, u32[]{:S(2)}, u32[]{:S(2)}) collective-permute-start(f32[16,256]{1,0:T(8,128)S(1)} %add.477), channel_id=1, source_target_pairs={{0,4},{1,5},{2,6},{3,7},{4,0},{5,1},{6,2},{7,3},{8,12},{9,13},{10,... | collective-permute-start | bytes 49160 | tf_op jit(solution)/shard_map/ppermute | solution.py:29
  214.0 2.6 collective-permute-start.13
  216.6 4.1 %collective-permute-start.14 = (f32[16,256]{1,0:T(8,128)S(1)}, f32[16,256]{1,0:T(8,128)S(1)}, u32[]{:S(2)}, u32[]{:S(2)}) collective-permute-start(f32[16,256]{1,0:T(8,128)S(1)} %add.479), channel_id=1, source_target_pairs={{0,16},{8,24},{16,0},{24,8},{1,17},{9,25},{17,1},{25,9},{2,18},{10... | collective-permute-start | bytes 49160 | tf_op jit(solution)/shard_map/ppermute | solution.py:29
  (43 other events, 71.2 us)
Sparse Core Ops, SparseCore 0:
  25.4 57.0 all-gather.1

commit v5 on v4

--- a/solution.py
+++ b/solution.py
@@ -161,10 +161,14 @@
     cells_dev = slab_x * plane
     slab_index = lax.axis_index("cy") * lax.axis_size("cz") + lax.axis_index("cz")
     slab_count = lax.axis_size("cy") * lax.axis_size("cz")
-    stacked = jnp.stack([log_perm, saturation], axis=1)
-    rimmed = with_halo(stacked, ((CELL, 2),), 1)
-    perm_pad = jnp.exp(rimmed[:, 0])
-    sat_pad = rimmed[:, 1]
+    count = slab_count
+    forward = [(i, i + 1) for i in range(count - 1)]
+    backward = [(target, source) for source, target in forward]
+    edges = (log_perm, saturation, rhs[:, 0])
+    low = lax.ppermute(jnp.stack([field[:, -1:] for field in edges], 1), CELL, forward)
+    high = lax.ppermute(jnp.stack([field[:, :1] for field in edges], 1), CELL, backward)
+    perm_pad = jnp.exp(jnp.concatenate([low[:, 0], log_perm, high[:, 0]], axis=1))
+    sat_pad = jnp.concatenate([low[:, 1], saturation, high[:, 1]], axis=1)
     trans_x, frac_x = face_pair(perm_pad[:, :-1], perm_pad[:, 1:], sat_pad[:, :-1], sat_pad[:, 1:])
     face_pos = lax.broadcasted_iota(jnp.int32, (slab_x + 1, 1, 1), 0)
     keep_face = jnp.where(
@@ -176,9 +180,6 @@
     frac_x = frac_x * keep_face
     trans_y, frac_y, trans_z, frac_z = plane_faces(perm_pad[:, 1:-1], saturation)
     coeffs = (porosity / time_step, trans_x, frac_x, trans_y, frac_y, trans_z, frac_z)
-    count = slab_count
-    forward = [(i, i + 1) for i in range(count - 1)]
-    backward = [(target, source) for source, target in forward]
 
     def planes(field):
         low = lax.ppermute(field[:, -1:], CELL, forward)
@@ -194,7 +195,7 @@
         factor = scale[:, None, None, None]
         return (ghosts[0] / factor, ghosts[1] / factor)
 
-    rhs_planes = planes(rhs[:, 0])
+    rhs_planes = (low[:, 2], high[:, 2])
     image = apply(rhs, rhs_planes)
     image_planes = planes(image[:, 0])
     reduced = cell_sum(jnp.stack([inner(rhs, rhs), inner(rhs, image)], 0))

time: 313 us -> 308 us (0.984)
  other arithmetic: 57.2 us -> 64.7 us
  local copies, waits for them, and re-layouts: 18.7 us -> 12.4 us
  starting transfers between devices: 33.4 us -> 27.4 us
    unnamed x151 -> x117, local copies, waits for them, and re-layouts: 10.4 us -> 2.28 us
    ppermute x4 -> x3, starting transfers between devices: 16.8 us -> 12.2 us  [planes(): low = lax.ppermute(field[:, -1:], CELL, forward)]
    mul x5, other arithmetic: 4.25 us -> 7.78 us  [net(): flow_z = coef_z * diff_z]
  transfers between devices with their start and end apart: 16 -> 14, of which waited for: 7 -> 6; matrix products, arithmetic and copies ran while one was open for 21% -> 24% of each run, Pallas kernels for 0% -> 0%
where the time goes in v5:
time: 308 us
  blocking collectives  163 us (53%)
  other arithmetic  64.7 us (21%)
  starting transfers between devices  27.4 us (9%)
  between operations  15.4 us (5%)
  waiting for transfers between devices  15 us (5%)
  local copies, waits for them, and re-layouts  12.4 us (4%)
  matrix products  9.87 us (3%)
    psum x10, blocking collectives, cell_sum(): values = lax.psum(values, axis)  112 us
    all_gather x1, blocking collectives, local(): predicted = lax.all_gather(slab_pred, 'grp', axis=0, tiled=True)  50.4 us
    ppermute x5, waiting for transfers between devices, cell_sum(): lax.ppermute(values, axis, [(i, i ^ step) for i in range(size)])  14.8 us
    another operation x3, other arithmetic, ensemble_weights(): factor = jnp.linalg.cholesky(gram)  12.4 us
    ppermute x3, starting transfers between devices, planes(): low = lax.ppermute(field[:, -1:], CELL, forward)  12.2 us
    another operation x2, other arithmetic, ensemble_weights(): return jax.scipy.linalg.cho_solve((factor, True), cross)  10.5 us
    mul x5, other arithmetic, net(): flow_z = coef_z * diff_z  7.78 us
    dot_general x1, matrix products, local(): jnp.dot(own_columns.T, lax.all_gather(scaled, 'grp', axis=0, tiled=True),...  7.11 us
  transfers between devices with their start and end apart: 14, of which 6 were waited for; matrix products, arithmetic and copies ran while one was open for 24% of the time, Pallas kernels for 0%

profile of v5, /device:TPU:1, one launch (start us, length us, event | category | flops | bytes accessed | tf_op | source)
XLA Modules:
  0.0 307.5 jit_solution(6333934453051698767)
XLA Ops:
  7.3 1.2 slice_bitcast_fusion.11
  11.3 1.3 collective-permute-start.1
  13.3 5.0 %collective-permute-start = (f32[16,3,1,16,128]{4,3,0,2,1:T(8,128)}, f32[16,3,1,16,128]{4,3,0,2,1:T(8,128)S(1)}, u32[]{:S(2)}, u32[]{:S(2)}) collective-permute-start(f32[16,3,1,16,128]{4,3,0,2,1:T(8,128)} %pad_maximum_fusion.12), channel_id=1, source_target_pairs={{0,1},{1,2},{2,3},{3,4},{4,5},{5,6},{6,7},{7,8},{8,9},{9,10},{10,1... | collective-permute-start | bytes 1179656 | tf_op jit(solution)/shard_map/ppermute | solution.py:168
  18.3 1.3 pad_maximum_fusion.4
  20.8 1.6 bitcast_multiply_fusion
  22.6 1.9 gather_fusion
  27.1 1.2 fusion.56
  28.4 1.3 fusion.55
  31.0 1.6 fusion.94
  34.1 19.3 %psum.70 = f32[2,16]{1,0:T(2,128)S(1)} all-reduce(f32[2,16]{1,0:T(2,128)S(1)} %pad_maximum_fusion.16), channel_id=1, replica_groups=mesh['grp'=8,'cy'=4,'cz'=8] {'cz'}, use_global_device_ids=true, to_apply=%region_2.3 | all-reduce | flops 32 | bytes 256 | tf_op jit(solution)/shard_map/psum | solution.py:25
  53.5 10.3 %psum.71 = f32[2,16]{1,0:T(2,128)S(1)} all-reduce(f32[2,16]{1,0:T(2,128)S(1)} %psum.70), channel_id=1, replica_groups=mesh['grp'=8,'cy'=4,'cz'=8] {'cy'}, use_global_device_ids=true, to_apply=%region_3.4 | all-reduce | flops 32 | bytes 256 | tf_op jit(solution)/shard_map/psum | solution.py:25
  64.4 1.4 collective-permute-start.2
  65.8 4.0 %collective-permute-start.3 = (f32[16,1,16,128]{3,2,1,0:T(8,128)S(1)}, f32[16,1,16,128]{3,2,1,0:T(8,128)S(1)}, u32[]{:S(2)}, u32[]{:S(2)}) collective-permute-start(f32[16,1,16,128]{3,2,1,0:T(8,128)S(1)} %get-tuple-element.72), channel_id=1, source_target_pairs={{0,1},{1,2},{2,3},{3,4},{4,5},{5,6},{6,7},{7,8},{8,9},{9,10},{10,1... | collective-permute-start | bytes 393224 | tf_op jit(solution)/shard_map/ppermute | solution.py:185
  69.8 2.0 multiply_multiply_fusion.10
  71.8 1.2 broadcast_divide_fusion
  73.5 1.1 multiply_subtract_fusion.8
  76.6 14.2 %psum.72 = f32[3,16]{1,0:T(4,128)S(1)} all-reduce(f32[3,16]{1,0:T(4,128)S(1)} %pad_maximum_fusion.14), channel_id=1, replica_groups=mesh['grp'=8,'cy'=4,'cz'=8] {'cz'}, use_global_device_ids=true, to_apply=%region_7.8 | all-reduce | flops 48 | bytes 384 | tf_op jit(solution)/shard_map/psum | solution.py:25
  90.9 6.0 %psum.73 = f32[3,16]{1,0:T(4,128)S(1)} all-reduce(f32[3,16]{1,0:T(4,128)S(1)} %psum.72), channel_id=1, replica_groups=mesh['grp'=8,'cy'=4,'cz'=8] {'cy'}, use_global_device_ids=true, to_apply=%region_8.9 | all-reduce | flops 48 | bytes 384 | tf_op jit(solution)/shard_map/psum | solution.py:25
  97.4 2.6 multiply_subtract_fusion.1
  100.4 1.3 collective-permute-start.4
  101.7 4.2 %collective-permute-start.5 = (f32[16,1,16,128]{3,2,1,0:T(8,128)S(1)}, f32[16,1,16,128]{3,2,1,0:T(8,128)S(1)}, u32[]{:S(2)}, u32[]{:S(2)}) collective-permute-start(f32[16,1,16,128]{3,2,1,0:T(8,128)S(1)} %get-tuple-element.70), channel_id=1, source_target_pairs={{0,1},{1,2},{2,3},{3,4},{4,5},{5,6},{6,7},{7,8},{8,9},{9,10},{10,1... | collective-permute-start | bytes 393224 | tf_op jit(solution)/shard_map/ppermute | solution.py:185
  105.9 2.0 multiply_multiply_fusion.9
  108.4 1.3 multiply_subtract_fusion.6
  112.2 14.7 %psum.74 = f32[4,16]{1,0:T(4,128)} all-reduce(f32[4,16]{1,0:T(4,128)S(1)} %pad_maximum_fusion.15), channel_id=1, replica_groups=mesh['grp'=8,'cy'=4,'cz'=8] {'cz'}, use_global_device_ids=true, to_apply=%region_13.14 | all-reduce | flops 64 | bytes 512 | tf_op jit(solution)/shard_map/psum | solution.py:25
  126.9 7.4 %psum.75 = f32[4,16]{1,0:T(4,128)} all-reduce(f32[4,16]{1,0:T(4,128)} %psum.74), channel_id=1, replica_groups=mesh['grp'=8,'cy'=4,'cz'=8] {'cy'}, use_global_device_ids=true, to_apply=%region_14.15 | all-reduce | flops 64 | bytes 512 | tf_op jit(solution)/shard_map/psum | solution.py:25
  136.1 2.4 copy_subtract_fusion
  138.9 1.4 collective-permute-start.6
  140.3 4.0 %collective-permute-start.7 = (f32[16,1,16,128]{3,2,1,0:T(8,128)S(1)}, f32[16,1,16,128]{3,2,1,0:T(8,128)S(1)}, u32[]{:S(2)}, u32[]{:S(2)}) collective-permute-start(f32[16,1,16,128]{3,2,1,0:T(8,128)S(1)} %get-tuple-element.68), channel_id=1, source_target_pairs={{0,1},{1,2},{2,3},{3,4},{4,5},{5,6},{6,7},{7,8},{8,9},{9,10},{10,1... | collective-permute-start | bytes 393224 | tf_op jit(solution)/shard_map/ppermute | solution.py:185
  144.4 1.2 multiply_multiply_fusion.8
  146.2 1.2 multiply_subtract_fusion.4
  149.6 14.1 %psum.76 = f32[5,16]{1,0:T(8,128)S(1)} all-reduce(f32[5,16]{1,0:T(8,128)S(1)} %stack.169), channel_id=1, replica_groups=mesh['grp'=8,'cy'=4,'cz'=8] {'cz'}, use_global_device_ids=true, to_apply=%region_20.21 | all-reduce | flops 80 | bytes 640 | tf_op jit(solution)/shard_map/psum | solution.py:25
  163.7 7.9 %psum.77 = f32[5,16]{1,0:T(8,128)S(1)} all-reduce(f32[5,16]{1,0:T(8,128)S(1)} %psum.76), channel_id=1, replica_groups=mesh['grp'=8,'cy'=4,'cz'=8] {'cy'}, use_global_device_ids=true, to_apply=%region_21.22 | all-reduce | flops 80 | bytes 640 | tf_op jit(solution)/shard_map/psum | solution.py:25
  171.7 2.3 multiply_reduce_fusion.1
  174.0 12.3 %psum.78 = f32[16]{0:T(128)S(1)} all-reduce(f32[16]{0:T(128)S(1)} %multiply_reduce_fusion.1), channel_id=1, replica_groups=mesh['grp'=8,'cy'=4,'cz'=8] {'cz'}, use_global_device_ids=true, to_apply=%region_23.24 | all-reduce | flops 16 | bytes 128 | tf_op jit(solution)/shard_map/psum | solution.py:25
  186.3 6.1 %psum.79 = f32[16]{0:T(128)S(1)} all-reduce(f32[16]{0:T(128)S(1)} %psum.78), channel_id=1, replica_groups=mesh['grp'=8,'cy'=4,'cz'=8] {'cy'}, use_global_device_ids=true, to_apply=%region_24.25 | all-reduce | flops 16 | bytes 128 | tf_op jit(solution)/shard_map/psum | solution.py:25
  192.5 2.1 multiply_add_fusion
  194.6 1.6 fusion.19
  197.7 2.5 collective-permute-done.8
  200.1 3.5 %collective-permute-done.9 = f32[16,256]{1,0:T(8,128)S(1)} collective-permute-done((f32[16,256]{1,0:T(8,128)S(1)}, f32[16,256]{1,0:T(8,128)S(1)}, u32[]{:S(2)}, u32[]{:S(2)}) %collective-permute-start.9) | collective-permute-done | bytes 16416 | tf_op jit(solution)/shard_map/ppermute | solution.py:29
  203.7 2.3 collective-permute-start.10
  205.9 4.4 %collective-permute-done.10 = f32[16,256]{1,0:T(8,128)S(1)} collective-permute-done((f32[16,256]{1,0:T(8,128)S(1)}, f32[16,256]{1,0:T(8,128)S(1)}, u32[]{:S(2)}, u32[]{:S(2)}) %collective-permute-start.10) | collective-permute-done | bytes 16416 | tf_op jit(solution)/shard_map/ppermute | solution.py:29
  210.3 1.4 collective-permute-start.11
  211.7 1.2 collective-permute-done.11
  213.8 3.2 %collective-permute-done.12 = f32[16,256]{1,0:T(8,128)S(1)} collective-permute-done((f32[16,256]{1,0:T(8,128)S(1)}, f32[16,256]{1,0:T(8,128)S(1)}, u32[]{:S(2)}, u32[]{:S(2)}) %collective-permute-start.12) | collective-permute-done | bytes 16416 | tf_op jit(solution)/shard_map/ppermute | solution.py:29
  217.0 50.4 %all_gather.6 = f32[128,256]{1,0:T(8,128)S(1)} all-gather(f32[16,256]{1,0:T(8,128)S(1)} %add.480), channel_id=1, replica_groups=mesh['grp'=8,'cy'=4,'cz'=8] {'grp'}, dimensions={0}, use_global_device_ids=true | all-gather | bytes 147456 | tf_op jit(solution)/shard_map/all_gather | solution.py:263
  267.9 11.7 %cholesky.17 = f32[128,128]{1,0:T(8,128)S(1)} custom-call(f32[128,128]{1,0:T(8,128)S(1)} %fusion.71), custom_call_target="Cholesky" | custom-call | tf_op jit(solution)/shard_map/jit(cholesky)/cholesky | solution.py:143
  280.9 9.8 %custom-call.10 = f32[1,128,128]{1,2,0:T(8,128)S(1)} custom-call(f32[1,128,128]{2,1,0:T(8,128)S(1)} %fusion.65), custom_call_target="InvertDiagBlocksLowerTriangular" | custom-call | tf_op jit(solution)/shard_map/jit(_cho_solve)/triangular_solve | solution.py:144
  292.3 7.1 %fusion = f32[2,8,128,128]{3,1,2,0:T(8,128)S(1)} fusion(f32[128,16]{1,0:T(8,128)S(1)} %fusion.66, f32[128,16384]{1,0:T(8,128)} %all-gather.2.cloned.1.call-done, f32[2,8,128,128]{3,2,1,0:T(8,128)S(1)} %bitcast.504), kind=kOutput, calls=%fused_computation.3 | convolution fusion | flops 402915328 | bytes 10493952 | tf_op jit(solution)/shard_map/dot_general | solution.py:269
  (241 shorter events, 28.8 us)
Async XLA Ops:
  7.2 15.4 %copy-start = (s32[128]{0:T(128)S(1)}, s32[128]{0:T(128)}, u32[]{:S(2)}) copy-start(s32[128]{0:T(128)} %param.18) | copy-start | bytes 1540
  7.2 19.2 %copy-start.2 = (f32[16,2,4,16,128]{4,3,2,1,0:T(8,128)S(1)}, f32[16,2,4,16,128]{4,3,2,1,0:T(8,128)}, u32[]{:S(2)}) copy-start(f32[16,2,4,16,128]{4,3,2,1,0:T(8,128)} %param.10) | copy-start | bytes 3145732
  7.2 18.9 %copy-start.3 = (f32[16,4,16,128]{3,2,1,0:T(8,128)S(1)}, f32[16,4,16,128]{3,2,1,0:T(8,128)}, u32[]{:S(2)}) copy-start(f32[16,4,16,128]{3,2,1,0:T(8,128)} %param.13) | copy-start | bytes 1572868
  7.2 15.3 %copy-start.53 = (s32[256]{0:T(256)S(1)}, s32[256]{0:T(256)}, u32[]{:S(2)}) copy-start(s32[256]{0:T(256)} %param.19) | copy-start | bytes 3076
  7.2 285.1 %all-gather.2.cloned.1.call-start = ((), (), s32[]{:S(2)}) async-start(), calls=%async_computation | async-start | bytes 9437184 | tf_op jit(solution)/shard_map/all_gather | solution.py:271
  10.5 16.2 %copy-start.27 = (f32[16,4,16,128]{3,2,1,0:T(8,128)S(1)}, f32[16,4,16,128]{3,2,1,0:T(8,128)}, u32[]{:S(2)}) copy-start(f32[16,4,16,128]{3,2,1,0:T(8,128)} %param.11) | copy-start | bytes 1572868
  11.3 15.3 %collective-permute-start.1 = (f32[16,3,1,16,128]{4,3,0,2,1:T(8,128)}, f32[16,3,1,16,128]{4,3,0,2,1:T(8,128)S(1)}, u32[]{:S(2)}, u32[]{:S(2)}) collective-permute-start(f32[16,3,1,16,128]{4,3,0,2,1:T(8,128)} %pad_maximum_fusion.13), channel_id=1, source_target_pairs={{1,0},{2,1},{3,2},{4,3},{5,4},{6,5},{7,6},{8,7},{9,8},{10,9},{11,1... | collective-permute-start | bytes 1179656 | tf_op jit(solution)/shard_map/ppermute | solution.py:169
  13.3 13.3 %collective-permute-start = (f32[16,3,1,16,128]{4,3,0,2,1:T(8,128)}, f32[16,3,1,16,128]{4,3,0,2,1:T(8,128)S(1)}, u32[]{:S(2)}, u32[]{:S(2)}) collective-permute-start(f32[16,3,1,16,128]{4,3,0,2,1:T(8,128)} %pad_maximum_fusion.12), channel_id=1, source_target_pairs={{0,1},{1,2},{2,3},{3,4},{4,5},{5,6},{6,7},{7,8},{8,9},{9,10},{10,1... | collective-permute-start | bytes 1179656 | tf_op jit(solution)/shard_map/ppermute | solution.py:168
  25.8 80.1 %copy-start.43 = (f32[128]{0:T(128)}, f32[128]{0:T(128)S(1)}, u32[]{:S(2)}) copy-start(f32[128]{0:T(128)S(1)} %compare_convert_fusion) | copy-start | bytes 1540
  25.8 80.1 %copy-start.44 = (f32[16]{0:T(128)}, f32[16]{0:T(128)S(1)}, u32[]{:S(2)}) copy-start(f32[16]{0:T(128)S(1)} %compare_convert_fusion.1) | copy-start | bytes 196
  33.9 41.9 %copy-start.5 = (f32[16,1,4,16,128]{4,3,2,0,1:T(8,128)}, f32[16,1,4,16,128]{4,3,2,0,1:T(8,128)S(1)}, u32[]{:S(2)}) copy-start(f32[16,1,4,16,128]{4,3,2,0,1:T(8,128)S(1)} %fusion.45) | copy-start | bytes 1572868
  63.7 33.1 %copy-start.47 = (f32[2,16]{1,0:T(2,128)}, f32[2,16]{1,0:T(2,128)S(1)}, u32[]{:S(2)}) copy-start(f32[2,16]{1,0:T(2,128)S(1)} %psum.71) | copy-start | bytes 388
  63.8 10.8 %copy-start.17 = (f32[16,5,16,128]{3,2,1,0:T(8,128)S(1)}, f32[16,5,16,128]{3,2,1,0:T(8,128)}, u32[]{:S(2)}) copy-start(f32[16,5,16,128]{3,2,1,0:T(8,128)} %get-tuple-element.28) | copy-start | bytes 1966084
  63.8 10.8 %copy-start.20 = (f32[16,5,16,128]{3,2,1,0:T(8,128)S(1)}, f32[16,5,16,128]{3,2,1,0:T(8,128)}, u32[]{:S(2)}) copy-start(f32[16,5,16,128]{3,2,1,0:T(8,128)} %get-tuple-element.34) | copy-start | bytes 1966084
  64.0 11.3 %copy-start.12 = (f32[16,2,4,16,128]{4,3,2,0,1:T(8,128)}, f32[16,2,4,16,128]{4,3,2,0,1:T(8,128)S(1)}, u32[]{:S(2)}) copy-start(f32[16,2,4,16,128]{4,3,2,0,1:T(8,128)S(1)} %multiply_subtract_fusion.2) | copy-start | bytes 3145732
  64.4 9.1 %collective-permute-start.2 = (f32[16,1,16,128]{3,2,1,0:T(8,128)S(1)}, f32[16,1,16,128]{3,2,1,0:T(8,128)S(1)}, u32[]{:S(2)}, u32[]{:S(2)}) collective-permute-start(f32[16,1,16,128]{3,2,1,0:T(8,128)S(1)} %get-tuple-element.71), channel_id=1, source_target_pairs={{1,0},{2,1},{3,2},{4,3},{5,4},{6,5},{7,6},{8,7},{9,8},{10,9},{11,1... | collective-permute-start | bytes 393224 | tf_op jit(solution)/shard_map/ppermute | solution.py:186
  65.8 7.7 %collective-permute-start.3 = (f32[16,1,16,128]{3,2,1,0:T(8,128)S(1)}, f32[16,1,16,128]{3,2,1,0:T(8,128)S(1)}, u32[]{:S(2)}, u32[]{:S(2)}) collective-permute-start(f32[16,1,16,128]{3,2,1,0:T(8,128)S(1)} %get-tuple-element.72), channel_id=1, source_target_pairs={{0,1},{1,2},{2,3},{3,4},{4,5},{5,6},{6,7},{7,8},{8,9},{9,10},{10,1... | collective-permute-start | bytes 393224 | tf_op jit(solution)/shard_map/ppermute | solution.py:185
  96.9 11.5 %copy-start.45 = (f32[3,16]{1,0:T(4,128)}, f32[3,16]{1,0:T(4,128)S(1)}, u32[]{:S(2)}) copy-start(f32[3,16]{1,0:T(4,128)S(1)} %psum.73) | copy-start | bytes 580
  97.4 11.0 %copy-start.51 = (f32[16]{0:T(128)}, f32[16]{0:T(128)S(1)}, u32[]{:S(2)}) copy-start(f32[16]{0:T(128)S(1)} %get-tuple-element.98) | copy-start | bytes 196
  97.4 12.3 %copy-start.18 = (f32[16,5,16,128]{3,2,1,0:T(8,128)S(1)}, f32[16,5,16,128]{3,2,1,0:T(8,128)}, u32[]{:S(2)}) copy-start(f32[16,5,16,128]{3,2,1,0:T(8,128)} %get-tuple-element.28) | copy-start | bytes 1966084
  97.4 12.3 %copy-start.21 = (f32[16,5,16,128]{3,2,1,0:T(8,128)S(1)}, f32[16,5,16,128]{3,2,1,0:T(8,128)}, u32[]{:S(2)}) copy-start(f32[16,5,16,128]{3,2,1,0:T(8,128)} %get-tuple-element.34) | copy-start | bytes 1966084
  100.0 10.3 %copy-start.9 = (f32[16,4,16,128]{3,2,1,0:T(8,128)S(1)}, f32[16,4,16,128]{3,2,1,0:T(8,128)}, u32[]{:S(2)}) copy-start(f32[16,4,16,128]{3,2,1,0:T(8,128)} %param.12) | copy-start | bytes 1572868
  100.4 8.0 %collective-permute-start.4 = (f32[16,1,16,128]{3,2,1,0:T(8,128)S(1)}, f32[16,1,16,128]{3,2,1,0:T(8,128)S(1)}, u32[]{:S(2)}, u32[]{:S(2)}) collective-permute-start(f32[16,1,16,128]{3,2,1,0:T(8,128)S(1)} %get-tuple-element.69), channel_id=1, source_target_pairs={{1,0},{2,1},{3,2},{4,3},{5,4},{6,5},{7,6},{8,7},{9,8},{10,9},{11,1... | collective-permute-start | bytes 393224 | tf_op jit(solution)/shard_map/ppermute | solution.py:186
  101.7 6.7 %collective-permute-start.5 = (f32[16,1,16,128]{3,2,1,0:T(8,128)S(1)}, f32[16,1,16,128]{3,2,1,0:T(8,128)S(1)}, u32[]{:S(2)}, u32[]{:S(2)}) collective-permute-start(f32[16,1,16,128]{3,2,1,0:T(8,128)S(1)} %get-tuple-element.70), channel_id=1, source_target_pairs={{0,1},{1,2},{2,3},{3,4},{4,5},{5,6},{6,7},{7,8},{8,9},{9,10},{10,1... | collective-permute-start | bytes 393224 | tf_op jit(solution)/shard_map/ppermute | solution.py:185
  136.0 10.2 %copy-start.49 = (f32[16]{0:T(128)}, f32[16]{0:T(128)S(1)}, u32[]{:S(2)}) copy-start(f32[16]{0:T(128)S(1)} %get-tuple-element.91) | copy-start | bytes 196
  136.0 10.2 %copy-start.40 = (f32[16,1,16,128]{3,2,1,0:T(8,128)S(1)}, f32[16,1,16,128]{3,2,1,0:T(8,128)}, u32[]{:S(2)}) copy-start(f32[16,1,16,128]{3,2,1,0:T(8,128)} %copy-done.39) | copy-start | bytes 393220
  136.0 11.4 %copy-start.19 = (f32[16,5,16,128]{3,2,1,0:T(8,128)S(1)}, f32[16,5,16,128]{3,2,1,0:T(8,128)}, u32[]{:S(2)}) copy-start(f32[16,5,16,128]{3,2,1,0:T(8,128)} %get-tuple-element.28) | copy-start | bytes 1966084
  136.0 11.4 %copy-start.22 = (f32[16,5,16,128]{3,2,1,0:T(8,128)S(1)}, f32[16,5,16,128]{3,2,1,0:T(8,128)}, u32[]{:S(2)}) copy-start(f32[16,5,16,128]{3,2,1,0:T(8,128)} %get-tuple-element.34) | copy-start | bytes 1966084
  138.5 10.2 %copy-start.4 = (f32[16,2,4,16,128]{4,3,2,1,0:T(8,128)}, f32[16,2,4,16,128]{4,3,2,1,0:T(8,128)S(1)}, u32[]{:S(2)}) copy-start(f32[16,2,4,16,128]{4,3,2,1,0:T(8,128)S(1)} %copy_subtract_fusion) | copy-start | bytes 3145732
  138.9 7.2 %collective-permute-start.6 = (f32[16,1,16,128]{3,2,1,0:T(8,128)S(1)}, f32[16,1,16,128]{3,2,1,0:T(8,128)S(1)}, u32[]{:S(2)}, u32[]{:S(2)}) collective-permute-start(f32[16,1,16,128]{3,2,1,0:T(8,128)S(1)} %get-tuple-element.67), channel_id=1, source_target_pairs={{1,0},{2,1},{3,2},{4,3},{5,4},{6,5},{7,6},{8,7},{9,8},{10,9},{11,1... | collective-permute-start | bytes 393224 | tf_op jit(solution)/shard_map/ppermute | solution.py:186
  140.3 5.9 %collective-permute-start.7 = (f32[16,1,16,128]{3,2,1,0:T(8,128)S(1)}, f32[16,1,16,128]{3,2,1,0:T(8,128)S(1)}, u32[]{:S(2)}, u32[]{:S(2)}) collective-permute-start(f32[16,1,16,128]{3,2,1,0:T(8,128)S(1)} %get-tuple-element.68), channel_id=1, source_target_pairs={{0,1},{1,2},{2,3},{3,4},{4,5},{5,6},{6,7},{7,8},{8,9},{9,10},{10,1... | collective-permute-start | bytes 393224 | tf_op jit(solution)/shard_map/ppermute | solution.py:185
  148.2 44.2 %copy-start.42 = (f32[4,16]{1,0:T(4,128)S(1)}, f32[4,16]{1,0:T(4,128)}, u32[]{:S(2)}) copy-start(f32[4,16]{1,0:T(4,128)} %psum.75) | copy-start | bytes 772
  148.2 44.2 %copy-start.46 = (f32[3,16]{1,0:T(4,128)S(1)}, f32[3,16]{1,0:T(4,128)}, u32[]{:S(2)}) copy-start(f32[3,16]{1,0:T(4,128)} %copy-done.45) | copy-start | bytes 580
  148.2 44.2 %copy-start.48 = (f32[2,16]{1,0:T(2,128)S(1)}, f32[2,16]{1,0:T(2,128)}, u32[]{:S(2)}) copy-start(f32[2,16]{1,0:T(2,128)} %copy-done.47) | copy-start | bytes 388
  148.2 44.2 %copy-start.50 = (f32[16]{0:T(128)S(1)}, f32[16]{0:T(128)}, u32[]{:S(2)}) copy-start(f32[16]{0:T(128)} %copy-done.49) | copy-start | bytes 196
  148.2 44.2 %copy-start.52 = (f32[16]{0:T(128)S(1)}, f32[16]{0:T(128)}, u32[]{:S(2)}) copy-start(f32[16]{0:T(128)} %copy-done.51) | copy-start | bytes 196
  148.2 44.2 %copy-start.55 = (f32[16]{0:T(128)S(1)}, f32[16]{0:T(128)}, u32[]{:S(2)}) copy-start(f32[16]{0:T(128)} %get-tuple-element.97) | copy-start | bytes 196
  173.9 22.5 %copy-start.41 = (f32[128,256]{1,0:T(8,128)S(1)}, f32[128,256]{1,0:T(8,128)}, u32[]{:S(2)}) copy-start(f32[128,256]{1,0:T(8,128)} %fusion.60) | copy-start | bytes 393220
  174.0 22.5 %copy-start.54 = (s32[256]{0:T(256)S(1)}, s32[256]{0:T(256)}, u32[]{:S(2)}) copy-start(s32[256]{0:T(256)} %get-tuple-element.15) | copy-start | bytes 3076
  174.0 39.9 %copy-start.56 = (f32[256]{0:T(256)S(1)}, f32[256]{0:T(256)}, u32[]{:S(2)}) copy-start(f32[256]{0:T(256)} %param.16) | copy-start | bytes 3076
  174.0 116.8 %copy-start.57 = (f32[256]{0:T(256)S(1)}, f32[256]{0:T(256)}, u32[]{:S(2)}) copy-start(f32[256]{0:T(256)} %param.15) | copy-start | bytes 3076
  194.6 97.7 %copy-start.24 = (f32[16,2,4,16,128]{4,3,2,1,0:T(8,128)S(1)}, f32[16,2,4,16,128]{4,3,2,1,0:T(8,128)}, u32[]{:S(2)}) copy-start(f32[16,2,4,16,128]{4,3,2,1,0:T(8,128)} %copy-done.23) | copy-start | bytes 3145732
  197.5 2.7 collective-permute-start.8
  200.1 3.5 %collective-permute-start.9 = (f32[16,256]{1,0:T(8,128)S(1)}, f32[16,256]{1,0:T(8,128)S(1)}, u32[]{:S(2)}, u32[]{:S(2)}) collective-permute-start(f32[16,256]{1,0:T(8,128)S(1)} %add.476), channel_id=1, source_target_pairs={{0,2},{1,3},{2,0},{3,1},{4,6},{5,7},{6,4},{7,5},{8,10},{9,11},{10,... | collective-permute-start | bytes 49160 | tf_op jit(solution)/shard_map/ppermute | solution.py:29
  203.7 6.7 %collective-permute-start.10 = (f32[16,256]{1,0:T(8,128)S(1)}, f32[16,256]{1,0:T(8,128)S(1)}, u32[]{:S(2)}, u32[]{:S(2)}) collective-permute-start(f32[16,256]{1,0:T(8,128)S(1)} %add.477), channel_id=1, source_target_pairs={{0,4},{1,5},{2,6},{3,7},{4,0},{5,1},{6,2},{7,3},{8,12},{9,13},{10,... | collective-permute-start | bytes 49160 | tf_op jit(solution)/shard_map/ppermute | solution.py:29
  210.3 2.6 collective-permute-start.11
  212.9 4.1 %collective-permute-start.12 = (f32[16,256]{1,0:T(8,128)S(1)}, f32[16,256]{1,0:T(8,128)S(1)}, u32[]{:S(2)}, u32[]{:S(2)}) collective-permute-start(f32[16,256]{1,0:T(8,128)S(1)} %add.479), channel_id=1, source_target_pairs={{0,16},{8,24},{16,0},{24,8},{1,17},{9,25},{17,1},{25,9},{2,18},{10... | collective-permute-start | bytes 49160 | tf_op jit(solution)/shard_map/ppermute | solution.py:29
  267.4 33.3 %copy-start.1 = (s32[128]{0:T(128)S(1)}, s32[128]{0:T(128)}, u32[]{:S(2)}) copy-start(s32[128]{0:T(128)} %param.18) | copy-start | bytes 1540
  (24 other events, 93.7 us)
Sparse Core Ops, SparseCore 0:
  22.6 56.6 all-gather.1

commit v6 on v5

--- a/solution.py
+++ b/solution.py
@@ -29,19 +29,6 @@
             values = values + lax.ppermute(values, axis, [(i, i ^ step) for i in range(size)])
             step *= 2
     return values
-
-
-def with_halo(block, sides, width):
-    for axis, dim in sides:
-        count = lax.axis_size(axis[0]) * lax.axis_size(axis[1])
-        forward = [(i, i + 1) for i in range(count - 1)]
-        backward = [(target, source) for source, target in forward]
-        low = lax.ppermute(
-            lax.slice_in_dim(block, block.shape[dim] - width, None, axis=dim), axis, forward
-        )
-        high = lax.ppermute(lax.slice_in_dim(block, 0, width, axis=dim), axis, backward)
-        block = jnp.concatenate([low, block, high], axis=dim)
-    return block
 
 
 def mobility(sat_field):
@@ -197,8 +184,9 @@
 
     rhs_planes = (low[:, 2], high[:, 2])
     image = apply(rhs, rhs_planes)
+    parts = jnp.stack([inner(rhs, rhs), inner(rhs, image)], 0)
     image_planes = planes(image[:, 0])
-    reduced = cell_sum(jnp.stack([inner(rhs, rhs), inner(rhs, image)], 0))
+    reduced = cell_sum(parts)
     beta = jnp.sqrt(reduced[0] + epsilon)
     basis = [rhs / expand(beta)]
     basis_planes = [scale_planes(rhs_planes, beta)]
@@ -220,11 +208,12 @@
             columns.append(projected + [height])
             break
         image = apply(ortho, ortho_planes)
-        image_planes = planes(image[:, 0])
         parts = [inner(ortho, ortho)]
         parts += [inner(basis[idx], image) for idx in range(jdx + 1)]
         parts.append(inner(ortho, image))
-        reduced = cell_sum(jnp.stack(parts, 0))
+        parts = jnp.stack(parts, 0)
+        image_planes = planes(image[:, 0])
+        reduced = cell_sum(parts)
         height = jnp.sqrt(reduced[0] + epsilon)
         columns.append(projected + [height])
         basis.append(ortho / expand(height))

time: 308 us -> 308 us (level)
  no operation moved by 1% of the time
where the time goes in v6:
time: 308 us
  blocking collectives  163 us (53%)
  other arithmetic  64.7 us (21%)
  starting transfers between devices  27.4 us (9%)
  between operations  15.4 us (5%)
  waiting for transfers between devices  15 us (5%)
  local copies, waits for them, and re-layouts  12.4 us (4%)
  matrix products  9.87 us (3%)
    psum x10, blocking collectives, cell_sum(): values = lax.psum(values, axis)  112 us
    all_gather x1, blocking collectives, local(): predicted = lax.all_gather(slab_pred, 'grp', axis=0, tiled=True)  50.4 us
    ppermute x5, waiting for transfers between devices, cell_sum(): lax.ppermute(values, axis, [(i, i ^ step) for i in range(size)])  14.8 us
    another operation x3, other arithmetic, ensemble_weights(): factor = jnp.linalg.cholesky(gram)  12.4 us
    ppermute x3, starting transfers between devices, planes(): low = lax.ppermute(field[:, -1:], CELL, forward)  12.2 us
    another operation x2, other arithmetic, ensemble_weights(): return jax.scipy.linalg.cho_solve((factor, True), cross)  10.5 us
    mul x5, other arithmetic, net(): flow_z = coef_z * diff_z  7.78 us
    dot_general x1, matrix products, local(): jnp.dot(own_columns.T, lax.all_gather(scaled, 'grp', axis=0, tiled=True),...  7.11 us
  transfers between devices with their start and end apart: 14, of which 6 were waited for; matrix products, arithmetic and copies ran while one was open for 24% of the time, Pallas kernels for 0%

profile of v6, /device:TPU:1, one launch (start us, length us, event | category | flops | bytes accessed | tf_op | source)
XLA Modules:
  0.0 307.5 jit_solution(6333934453051698767)
XLA Ops:
  7.3 1.2 slice_bitcast_fusion.11
  11.3 1.3 collective-permute-start.1
  13.3 5.0 %collective-permute-start = (f32[16,3,1,16,128]{4,3,0,2,1:T(8,128)}, f32[16,3,1,16,128]{4,3,0,2,1:T(8,128)S(1)}, u32[]{:S(2)}, u32[]{:S(2)}) collective-permute-start(f32[16,3,1,16,128]{4,3,0,2,1:T(8,128)} %pad_maximum_fusion.12), channel_id=1, source_target_pairs={{0,1},{1,2},{2,3},{3,4},{4,5},{5,6},{6,7},{7,8},{8,9},{9,10},{10,1... | collective-permute-start | bytes 1179656 | tf_op jit(solution)/shard_map/ppermute | solution.py:155
  18.3 1.3 pad_maximum_fusion.4
  20.8 1.6 bitcast_multiply_fusion
  22.6 1.9 gather_fusion
  27.1 1.2 fusion.56
  28.4 1.3 fusion.55
  31.0 1.6 fusion.94
  34.1 19.3 %psum.70 = f32[2,16]{1,0:T(2,128)S(1)} all-reduce(f32[2,16]{1,0:T(2,128)S(1)} %pad_maximum_fusion.16), channel_id=1, replica_groups=mesh['grp'=8,'cy'=4,'cz'=8] {'cz'}, use_global_device_ids=true, to_apply=%region_2.3 | all-reduce | flops 32 | bytes 256 | tf_op jit(solution)/shard_map/psum | solution.py:25
  53.5 10.3 %psum.71 = f32[2,16]{1,0:T(2,128)S(1)} all-reduce(f32[2,16]{1,0:T(2,128)S(1)} %psum.70), channel_id=1, replica_groups=mesh['grp'=8,'cy'=4,'cz'=8] {'cy'}, use_global_device_ids=true, to_apply=%region_3.4 | all-reduce | flops 32 | bytes 256 | tf_op jit(solution)/shard_map/psum | solution.py:25
  64.4 1.4 collective-permute-start.2
  65.8 4.0 %collective-permute-start.3 = (f32[16,1,16,128]{3,2,1,0:T(8,128)S(1)}, f32[16,1,16,128]{3,2,1,0:T(8,128)S(1)}, u32[]{:S(2)}, u32[]{:S(2)}) collective-permute-start(f32[16,1,16,128]{3,2,1,0:T(8,128)S(1)} %get-tuple-element.72), channel_id=1, source_target_pairs={{0,1},{1,2},{2,3},{3,4},{4,5},{5,6},{6,7},{7,8},{8,9},{9,10},{10,1... | collective-permute-start | bytes 393224 | tf_op jit(solution)/shard_map/ppermute | solution.py:172
  69.8 2.0 multiply_multiply_fusion.10
  71.8 1.2 broadcast_divide_fusion
  73.5 1.1 multiply_subtract_fusion.8
  76.6 14.2 %psum.72 = f32[3,16]{1,0:T(4,128)S(1)} all-reduce(f32[3,16]{1,0:T(4,128)S(1)} %pad_maximum_fusion.14), channel_id=1, replica_groups=mesh['grp'=8,'cy'=4,'cz'=8] {'cz'}, use_global_device_ids=true, to_apply=%region_7.8 | all-reduce | flops 48 | bytes 384 | tf_op jit(solution)/shard_map/psum | solution.py:25
  90.9 6.0 %psum.73 = f32[3,16]{1,0:T(4,128)S(1)} all-reduce(f32[3,16]{1,0:T(4,128)S(1)} %psum.72), channel_id=1, replica_groups=mesh['grp'=8,'cy'=4,'cz'=8] {'cy'}, use_global_device_ids=true, to_apply=%region_8.9 | all-reduce | flops 48 | bytes 384 | tf_op jit(solution)/shard_map/psum | solution.py:25
  97.4 2.6 multiply_subtract_fusion.1
  100.4 1.3 collective-permute-start.4
  101.7 4.2 %collective-permute-start.5 = (f32[16,1,16,128]{3,2,1,0:T(8,128)S(1)}, f32[16,1,16,128]{3,2,1,0:T(8,128)S(1)}, u32[]{:S(2)}, u32[]{:S(2)}) collective-permute-start(f32[16,1,16,128]{3,2,1,0:T(8,128)S(1)} %get-tuple-element.70), channel_id=1, source_target_pairs={{0,1},{1,2},{2,3},{3,4},{4,5},{5,6},{6,7},{7,8},{8,9},{9,10},{10,1... | collective-permute-start | bytes 393224 | tf_op jit(solution)/shard_map/ppermute | solution.py:172
  105.9 2.0 multiply_multiply_fusion.9
  108.4 1.3 multiply_subtract_fusion.6
  112.2 14.7 %psum.74 = f32[4,16]{1,0:T(4,128)} all-reduce(f32[4,16]{1,0:T(4,128)S(1)} %pad_maximum_fusion.15), channel_id=1, replica_groups=mesh['grp'=8,'cy'=4,'cz'=8] {'cz'}, use_global_device_ids=true, to_apply=%region_13.14 | all-reduce | flops 64 | bytes 512 | tf_op jit(solution)/shard_map/psum | solution.py:25
  126.9 7.4 %psum.75 = f32[4,16]{1,0:T(4,128)} all-reduce(f32[4,16]{1,0:T(4,128)} %psum.74), channel_id=1, replica_groups=mesh['grp'=8,'cy'=4,'cz'=8] {'cy'}, use_global_device_ids=true, to_apply=%region_14.15 | all-reduce | flops 64 | bytes 512 | tf_op jit(solution)/shard_map/psum | solution.py:25
  136.1 2.4 copy_subtract_fusion
  138.9 1.4 collective-permute-start.6
  140.3 4.0 %collective-permute-start.7 = (f32[16,1,16,128]{3,2,1,0:T(8,128)S(1)}, f32[16,1,16,128]{3,2,1,0:T(8,128)S(1)}, u32[]{:S(2)}, u32[]{:S(2)}) collective-permute-start(f32[16,1,16,128]{3,2,1,0:T(8,128)S(1)} %get-tuple-element.68), channel_id=1, source_target_pairs={{0,1},{1,2},{2,3},{3,4},{4,5},{5,6},{6,7},{7,8},{8,9},{9,10},{10,1... | collective-permute-start | bytes 393224 | tf_op jit(solution)/shard_map/ppermute | solution.py:172
  144.4 1.2 multiply_multiply_fusion.8
  146.2 1.2 multiply_subtract_fusion.4
  149.6 14.1 %psum.76 = f32[5,16]{1,0:T(8,128)S(1)} all-reduce(f32[5,16]{1,0:T(8,128)S(1)} %stack.169), channel_id=1, replica_groups=mesh['grp'=8,'cy'=4,'cz'=8] {'cz'}, use_global_device_ids=true, to_apply=%region_20.21 | all-reduce | flops 80 | bytes 640 | tf_op jit(solution)/shard_map/psum | solution.py:25
  163.7 7.9 %psum.77 = f32[5,16]{1,0:T(8,128)S(1)} all-reduce(f32[5,16]{1,0:T(8,128)S(1)} %psum.76), channel_id=1, replica_groups=mesh['grp'=8,'cy'=4,'cz'=8] {'cy'}, use_global_device_ids=true, to_apply=%region_21.22 | all-reduce | flops 80 | bytes 640 | tf_op jit(solution)/shard_map/psum | solution.py:25
  171.7 2.3 multiply_reduce_fusion.1
  174.0 12.3 %psum.78 = f32[16]{0:T(128)S(1)} all-reduce(f32[16]{0:T(128)S(1)} %multiply_reduce_fusion.1), channel_id=1, replica_groups=mesh['grp'=8,'cy'=4,'cz'=8] {'cz'}, use_global_device_ids=true, to_apply=%region_23.24 | all-reduce | flops 16 | bytes 128 | tf_op jit(solution)/shard_map/psum | solution.py:25
  186.3 6.1 %psum.79 = f32[16]{0:T(128)S(1)} all-reduce(f32[16]{0:T(128)S(1)} %psum.78), channel_id=1, replica_groups=mesh['grp'=8,'cy'=4,'cz'=8] {'cy'}, use_global_device_ids=true, to_apply=%region_24.25 | all-reduce | flops 16 | bytes 128 | tf_op jit(solution)/shard_map/psum | solution.py:25
  192.5 2.1 multiply_add_fusion
  194.6 1.6 fusion.19
  197.7 2.5 collective-permute-done.8
  200.1 3.5 %collective-permute-done.9 = f32[16,256]{1,0:T(8,128)S(1)} collective-permute-done((f32[16,256]{1,0:T(8,128)S(1)}, f32[16,256]{1,0:T(8,128)S(1)}, u32[]{:S(2)}, u32[]{:S(2)}) %collective-permute-start.9) | collective-permute-done | bytes 16416 | tf_op jit(solution)/shard_map/ppermute | solution.py:29
  203.7 2.3 collective-permute-start.10
  205.9 4.4 %collective-permute-done.10 = f32[16,256]{1,0:T(8,128)S(1)} collective-permute-done((f32[16,256]{1,0:T(8,128)S(1)}, f32[16,256]{1,0:T(8,128)S(1)}, u32[]{:S(2)}, u32[]{:S(2)}) %collective-permute-start.10) | collective-permute-done | bytes 16416 | tf_op jit(solution)/shard_map/ppermute | solution.py:29
  210.3 1.4 collective-permute-start.11
  211.7 1.2 collective-permute-done.11
  213.8 3.2 %collective-permute-done.12 = f32[16,256]{1,0:T(8,128)S(1)} collective-permute-done((f32[16,256]{1,0:T(8,128)S(1)}, f32[16,256]{1,0:T(8,128)S(1)}, u32[]{:S(2)}, u32[]{:S(2)}) %collective-permute-start.12) | collective-permute-done | bytes 16416 | tf_op jit(solution)/shard_map/ppermute | solution.py:29
  217.0 50.4 %all_gather.6 = f32[128,256]{1,0:T(8,128)S(1)} all-gather(f32[16,256]{1,0:T(8,128)S(1)} %add.480), channel_id=1, replica_groups=mesh['grp'=8,'cy'=4,'cz'=8] {'grp'}, dimensions={0}, use_global_device_ids=true | all-gather | bytes 147456 | tf_op jit(solution)/shard_map/all_gather | solution.py:252
  267.9 11.7 %cholesky.17 = f32[128,128]{1,0:T(8,128)S(1)} custom-call(f32[128,128]{1,0:T(8,128)S(1)} %fusion.71), custom_call_target="Cholesky" | custom-call | tf_op jit(solution)/shard_map/jit(cholesky)/cholesky | solution.py:130
  280.9 9.8 %custom-call.10 = f32[1,128,128]{1,2,0:T(8,128)S(1)} custom-call(f32[1,128,128]{2,1,0:T(8,128)S(1)} %fusion.65), custom_call_target="InvertDiagBlocksLowerTriangular" | custom-call | tf_op jit(solution)/shard_map/jit(_cho_solve)/triangular_solve | solution.py:131
  292.3 7.1 %fusion = f32[2,8,128,128]{3,1,2,0:T(8,128)S(1)} fusion(f32[128,16]{1,0:T(8,128)S(1)} %fusion.66, f32[128,16384]{1,0:T(8,128)} %all-gather.2.cloned.1.call-done, f32[2,8,128,128]{3,2,1,0:T(8,128)S(1)} %bitcast.504), kind=kOutput, calls=%fused_computation.3 | convolution fusion | flops 402915328 | bytes 10493952 | tf_op jit(solution)/shard_map/dot_general | solution.py:258
  (241 shorter events, 28.8 us)
Async XLA Ops:
  7.2 15.4 %copy-start = (s32[128]{0:T(128)S(1)}, s32[128]{0:T(128)}, u32[]{:S(2)}) copy-start(s32[128]{0:T(128)} %param.18) | copy-start | bytes 1540
  7.2 19.2 %copy-start.2 = (f32[16,2,4,16,128]{4,3,2,1,0:T(8,128)S(1)}, f32[16,2,4,16,128]{4,3,2,1,0:T(8,128)}, u32[]{:S(2)}) copy-start(f32[16,2,4,16,128]{4,3,2,1,0:T(8,128)} %param.10) | copy-start | bytes 3145732
  7.2 18.9 %copy-start.3 = (f32[16,4,16,128]{3,2,1,0:T(8,128)S(1)}, f32[16,4,16,128]{3,2,1,0:T(8,128)}, u32[]{:S(2)}) copy-start(f32[16,4,16,128]{3,2,1,0:T(8,128)} %param.13) | copy-start | bytes 1572868
  7.2 15.3 %copy-start.53 = (s32[256]{0:T(256)S(1)}, s32[256]{0:T(256)}, u32[]{:S(2)}) copy-start(s32[256]{0:T(256)} %param.19) | copy-start | bytes 3076
  7.2 285.1 %all-gather.2.cloned.1.call-start = ((), (), s32[]{:S(2)}) async-start(), calls=%async_computation | async-start | bytes 9437184 | tf_op jit(solution)/shard_map/all_gather | solution.py:260
  10.5 16.2 %copy-start.27 = (f32[16,4,16,128]{3,2,1,0:T(8,128)S(1)}, f32[16,4,16,128]{3,2,1,0:T(8,128)}, u32[]{:S(2)}) copy-start(f32[16,4,16,128]{3,2,1,0:T(8,128)} %param.11) | copy-start | bytes 1572868
  11.3 15.3 %collective-permute-start.1 = (f32[16,3,1,16,128]{4,3,0,2,1:T(8,128)}, f32[16,3,1,16,128]{4,3,0,2,1:T(8,128)S(1)}, u32[]{:S(2)}, u32[]{:S(2)}) collective-permute-start(f32[16,3,1,16,128]{4,3,0,2,1:T(8,128)} %pad_maximum_fusion.13), channel_id=1, source_target_pairs={{1,0},{2,1},{3,2},{4,3},{5,4},{6,5},{7,6},{8,7},{9,8},{10,9},{11,1... | collective-permute-start | bytes 1179656 | tf_op jit(solution)/shard_map/ppermute | solution.py:156
  13.3 13.3 %collective-permute-start = (f32[16,3,1,16,128]{4,3,0,2,1:T(8,128)}, f32[16,3,1,16,128]{4,3,0,2,1:T(8,128)S(1)}, u32[]{:S(2)}, u32[]{:S(2)}) collective-permute-start(f32[16,3,1,16,128]{4,3,0,2,1:T(8,128)} %pad_maximum_fusion.12), channel_id=1, source_target_pairs={{0,1},{1,2},{2,3},{3,4},{4,5},{5,6},{6,7},{7,8},{8,9},{9,10},{10,1... | collective-permute-start | bytes 1179656 | tf_op jit(solution)/shard_map/ppermute | solution.py:155
  25.8 80.1 %copy-start.43 = (f32[128]{0:T(128)}, f32[128]{0:T(128)S(1)}, u32[]{:S(2)}) copy-start(f32[128]{0:T(128)S(1)} %compare_convert_fusion) | copy-start | bytes 1540
  25.8 80.1 %copy-start.44 = (f32[16]{0:T(128)}, f32[16]{0:T(128)S(1)}, u32[]{:S(2)}) copy-start(f32[16]{0:T(128)S(1)} %compare_convert_fusion.1) | copy-start | bytes 196
  33.9 41.9 %copy-start.5 = (f32[16,1,4,16,128]{4,3,2,0,1:T(8,128)}, f32[16,1,4,16,128]{4,3,2,0,1:T(8,128)S(1)}, u32[]{:S(2)}) copy-start(f32[16,1,4,16,128]{4,3,2,0,1:T(8,128)S(1)} %fusion.45) | copy-start | bytes 1572868
  63.7 33.1 %copy-start.47 = (f32[2,16]{1,0:T(2,128)}, f32[2,16]{1,0:T(2,128)S(1)}, u32[]{:S(2)}) copy-start(f32[2,16]{1,0:T(2,128)S(1)} %psum.71) | copy-start | bytes 388
  63.8 10.8 %copy-start.17 = (f32[16,5,16,128]{3,2,1,0:T(8,128)S(1)}, f32[16,5,16,128]{3,2,1,0:T(8,128)}, u32[]{:S(2)}) copy-start(f32[16,5,16,128]{3,2,1,0:T(8,128)} %get-tuple-element.28) | copy-start | bytes 1966084
  63.8 10.8 %copy-start.20 = (f32[16,5,16,128]{3,2,1,0:T(8,128)S(1)}, f32[16,5,16,128]{3,2,1,0:T(8,128)}, u32[]{:S(2)}) copy-start(f32[16,5,16,128]{3,2,1,0:T(8,128)} %get-tuple-element.34) | copy-start | bytes 1966084
  64.0 11.3 %copy-start.12 = (f32[16,2,4,16,128]{4,3,2,0,1:T(8,128)}, f32[16,2,4,16,128]{4,3,2,0,1:T(8,128)S(1)}, u32[]{:S(2)}) copy-start(f32[16,2,4,16,128]{4,3,2,0,1:T(8,128)S(1)} %multiply_subtract_fusion.2) | copy-start | bytes 3145732
  64.4 9.1 %collective-permute-start.2 = (f32[16,1,16,128]{3,2,1,0:T(8,128)S(1)}, f32[16,1,16,128]{3,2,1,0:T(8,128)S(1)}, u32[]{:S(2)}, u32[]{:S(2)}) collective-permute-start(f32[16,1,16,128]{3,2,1,0:T(8,128)S(1)} %get-tuple-element.71), channel_id=1, source_target_pairs={{1,0},{2,1},{3,2},{4,3},{5,4},{6,5},{7,6},{8,7},{9,8},{10,9},{11,1... | collective-permute-start | bytes 393224 | tf_op jit(solution)/shard_map/ppermute | solution.py:173
  65.8 7.7 %collective-permute-start.3 = (f32[16,1,16,128]{3,2,1,0:T(8,128)S(1)}, f32[16,1,16,128]{3,2,1,0:T(8,128)S(1)}, u32[]{:S(2)}, u32[]{:S(2)}) collective-permute-start(f32[16,1,16,128]{3,2,1,0:T(8,128)S(1)} %get-tuple-element.72), channel_id=1, source_target_pairs={{0,1},{1,2},{2,3},{3,4},{4,5},{5,6},{6,7},{7,8},{8,9},{9,10},{10,1... | collective-permute-start | bytes 393224 | tf_op jit(solution)/shard_map/ppermute | solution.py:172
  96.9 11.5 %copy-start.45 = (f32[3,16]{1,0:T(4,128)}, f32[3,16]{1,0:T(4,128)S(1)}, u32[]{:S(2)}) copy-start(f32[3,16]{1,0:T(4,128)S(1)} %psum.73) | copy-start | bytes 580
  97.4 11.0 %copy-start.51 = (f32[16]{0:T(128)}, f32[16]{0:T(128)S(1)}, u32[]{:S(2)}) copy-start(f32[16]{0:T(128)S(1)} %get-tuple-element.98) | copy-start | bytes 196
  97.4 12.3 %copy-start.18 = (f32[16,5,16,128]{3,2,1,0:T(8,128)S(1)}, f32[16,5,16,128]{3,2,1,0:T(8,128)}, u32[]{:S(2)}) copy-start(f32[16,5,16,128]{3,2,1,0:T(8,128)} %get-tuple-element.28) | copy-start | bytes 1966084
  97.4 12.3 %copy-start.21 = (f32[16,5,16,128]{3,2,1,0:T(8,128)S(1)}, f32[16,5,16,128]{3,2,1,0:T(8,128)}, u32[]{:S(2)}) copy-start(f32[16,5,16,128]{3,2,1,0:T(8,128)} %get-tuple-element.34) | copy-start | bytes 1966084
  100.0 10.3 %copy-start.9 = (f32[16,4,16,128]{3,2,1,0:T(8,128)S(1)}, f32[16,4,16,128]{3,2,1,0:T(8,128)}, u32[]{:S(2)}) copy-start(f32[16,4,16,128]{3,2,1,0:T(8,128)} %param.12) | copy-start | bytes 1572868
  100.4 8.0 %collective-permute-start.4 = (f32[16,1,16,128]{3,2,1,0:T(8,128)S(1)}, f32[16,1,16,128]{3,2,1,0:T(8,128)S(1)}, u32[]{:S(2)}, u32[]{:S(2)}) collective-permute-start(f32[16,1,16,128]{3,2,1,0:T(8,128)S(1)} %get-tuple-element.69), channel_id=1, source_target_pairs={{1,0},{2,1},{3,2},{4,3},{5,4},{6,5},{7,6},{8,7},{9,8},{10,9},{11,1... | collective-permute-start | bytes 393224 | tf_op jit(solution)/shard_map/ppermute | solution.py:173
  101.7 6.7 %collective-permute-start.5 = (f32[16,1,16,128]{3,2,1,0:T(8,128)S(1)}, f32[16,1,16,128]{3,2,1,0:T(8,128)S(1)}, u32[]{:S(2)}, u32[]{:S(2)}) collective-permute-start(f32[16,1,16,128]{3,2,1,0:T(8,128)S(1)} %get-tuple-element.70), channel_id=1, source_target_pairs={{0,1},{1,2},{2,3},{3,4},{4,5},{5,6},{6,7},{7,8},{8,9},{9,10},{10,1... | collective-permute-start | bytes 393224 | tf_op jit(solution)/shard_map/ppermute | solution.py:172
  136.0 10.2 %copy-start.49 = (f32[16]{0:T(128)}, f32[16]{0:T(128)S(1)}, u32[]{:S(2)}) copy-start(f32[16]{0:T(128)S(1)} %get-tuple-element.91) | copy-start | bytes 196
  136.0 10.2 %copy-start.40 = (f32[16,1,16,128]{3,2,1,0:T(8,128)S(1)}, f32[16,1,16,128]{3,2,1,0:T(8,128)}, u32[]{:S(2)}) copy-start(f32[16,1,16,128]{3,2,1,0:T(8,128)} %copy-done.39) | copy-start | bytes 393220
  136.0 11.4 %copy-start.19 = (f32[16,5,16,128]{3,2,1,0:T(8,128)S(1)}, f32[16,5,16,128]{3,2,1,0:T(8,128)}, u32[]{:S(2)}) copy-start(f32[16,5,16,128]{3,2,1,0:T(8,128)} %get-tuple-element.28) | copy-start | bytes 1966084
  136.0 11.4 %copy-start.22 = (f32[16,5,16,128]{3,2,1,0:T(8,128)S(1)}, f32[16,5,16,128]{3,2,1,0:T(8,128)}, u32[]{:S(2)}) copy-start(f32[16,5,16,128]{3,2,1,0:T(8,128)} %get-tuple-element.34) | copy-start | bytes 1966084
  138.5 10.2 %copy-start.4 = (f32[16,2,4,16,128]{4,3,2,1,0:T(8,128)}, f32[16,2,4,16,128]{4,3,2,1,0:T(8,128)S(1)}, u32[]{:S(2)}) copy-start(f32[16,2,4,16,128]{4,3,2,1,0:T(8,128)S(1)} %copy_subtract_fusion) | copy-start | bytes 3145732
  138.9 7.2 %collective-permute-start.6 = (f32[16,1,16,128]{3,2,1,0:T(8,128)S(1)}, f32[16,1,16,128]{3,2,1,0:T(8,128)S(1)}, u32[]{:S(2)}, u32[]{:S(2)}) collective-permute-start(f32[16,1,16,128]{3,2,1,0:T(8,128)S(1)} %get-tuple-element.67), channel_id=1, source_target_pairs={{1,0},{2,1},{3,2},{4,3},{5,4},{6,5},{7,6},{8,7},{9,8},{10,9},{11,1... | collective-permute-start | bytes 393224 | tf_op jit(solution)/shard_map/ppermute | solution.py:173
  140.3 5.9 %collective-permute-start.7 = (f32[16,1,16,128]{3,2,1,0:T(8,128)S(1)}, f32[16,1,16,128]{3,2,1,0:T(8,128)S(1)}, u32[]{:S(2)}, u32[]{:S(2)}) collective-permute-start(f32[16,1,16,128]{3,2,1,0:T(8,128)S(1)} %get-tuple-element.68), channel_id=1, source_target_pairs={{0,1},{1,2},{2,3},{3,4},{4,5},{5,6},{6,7},{7,8},{8,9},{9,10},{10,1... | collective-permute-start | bytes 393224 | tf_op jit(solution)/shard_map/ppermute | solution.py:172
  148.2 44.2 %copy-start.42 = (f32[4,16]{1,0:T(4,128)S(1)}, f32[4,16]{1,0:T(4,128)}, u32[]{:S(2)}) copy-start(f32[4,16]{1,0:T(4,128)} %psum.75) | copy-start | bytes 772
  148.2 44.2 %copy-start.46 = (f32[3,16]{1,0:T(4,128)S(1)}, f32[3,16]{1,0:T(4,128)}, u32[]{:S(2)}) copy-start(f32[3,16]{1,0:T(4,128)} %copy-done.45) | copy-start | bytes 580
  148.2 44.2 %copy-start.48 = (f32[2,16]{1,0:T(2,128)S(1)}, f32[2,16]{1,0:T(2,128)}, u32[]{:S(2)}) copy-start(f32[2,16]{1,0:T(2,128)} %copy-done.47) | copy-start | bytes 388
  148.2 44.2 %copy-start.50 = (f32[16]{0:T(128)S(1)}, f32[16]{0:T(128)}, u32[]{:S(2)}) copy-start(f32[16]{0:T(128)} %copy-done.49) | copy-start | bytes 196
  148.2 44.2 %copy-start.52 = (f32[16]{0:T(128)S(1)}, f32[16]{0:T(128)}, u32[]{:S(2)}) copy-start(f32[16]{0:T(128)} %copy-done.51) | copy-start | bytes 196
  148.2 44.2 %copy-start.55 = (f32[16]{0:T(128)S(1)}, f32[16]{0:T(128)}, u32[]{:S(2)}) copy-start(f32[16]{0:T(128)} %get-tuple-element.97) | copy-start | bytes 196
  173.9 22.5 %copy-start.41 = (f32[128,256]{1,0:T(8,128)S(1)}, f32[128,256]{1,0:T(8,128)}, u32[]{:S(2)}) copy-start(f32[128,256]{1,0:T(8,128)} %fusion.60) | copy-start | bytes 393220
  174.0 22.5 %copy-start.54 = (s32[256]{0:T(256)S(1)}, s32[256]{0:T(256)}, u32[]{:S(2)}) copy-start(s32[256]{0:T(256)} %get-tuple-element.15) | copy-start | bytes 3076
  174.0 39.9 %copy-start.56 = (f32[256]{0:T(256)S(1)}, f32[256]{0:T(256)}, u32[]{:S(2)}) copy-start(f32[256]{0:T(256)} %param.16) | copy-start | bytes 3076
  174.0 116.8 %copy-start.57 = (f32[256]{0:T(256)S(1)}, f32[256]{0:T(256)}, u32[]{:S(2)}) copy-start(f32[256]{0:T(256)} %param.15) | copy-start | bytes 3076
  194.6 97.7 %copy-start.24 = (f32[16,2,4,16,128]{4,3,2,1,0:T(8,128)S(1)}, f32[16,2,4,16,128]{4,3,2,1,0:T(8,128)}, u32[]{:S(2)}) copy-start(f32[16,2,4,16,128]{4,3,2,1,0:T(8,128)} %copy-done.23) | copy-start | bytes 3145732
  197.5 2.7 collective-permute-start.8
  200.1 3.5 %collective-permute-start.9 = (f32[16,256]{1,0:T(8,128)S(1)}, f32[16,256]{1,0:T(8,128)S(1)}, u32[]{:S(2)}, u32[]{:S(2)}) collective-permute-start(f32[16,256]{1,0:T(8,128)S(1)} %add.476), channel_id=1, source_target_pairs={{0,2},{1,3},{2,0},{3,1},{4,6},{5,7},{6,4},{7,5},{8,10},{9,11},{10,... | collective-permute-start | bytes 49160 | tf_op jit(solution)/shard_map/ppermute | solution.py:29
  203.7 6.7 %collective-permute-start.10 = (f32[16,256]{1,0:T(8,128)S(1)}, f32[16,256]{1,0:T(8,128)S(1)}, u32[]{:S(2)}, u32[]{:S(2)}) collective-permute-start(f32[16,256]{1,0:T(8,128)S(1)} %add.477), channel_id=1, source_target_pairs={{0,4},{1,5},{2,6},{3,7},{4,0},{5,1},{6,2},{7,3},{8,12},{9,13},{10,... | collective-permute-start | bytes 49160 | tf_op jit(solution)/shard_map/ppermute | solution.py:29
  210.3 2.6 collective-permute-start.11
  212.9 4.1 %collective-permute-start.12 = (f32[16,256]{1,0:T(8,128)S(1)}, f32[16,256]{1,0:T(8,128)S(1)}, u32[]{:S(2)}, u32[]{:S(2)}) collective-permute-start(f32[16,256]{1,0:T(8,128)S(1)} %add.479), channel_id=1, source_target_pairs={{0,16},{8,24},{16,0},{24,8},{1,17},{9,25},{17,1},{25,9},{2,18},{10... | collective-permute-start | bytes 49160 | tf_op jit(solution)/shard_map/ppermute | solution.py:29
  267.4 33.3 %copy-start.1 = (s32[128]{0:T(128)S(1)}, s32[128]{0:T(128)}, u32[]{:S(2)}) copy-start(s32[128]{0:T(128)} %param.18) | copy-start | bytes 1540
  (24 other events, 93.7 us)
Sparse Core Ops, SparseCore 0:
  22.6 56.6 all-gather.1

commit v7 on v6

--- a/solution.py
+++ b/solution.py
@@ -254,10 +254,9 @@
     offset = lax.axis_index("grp") * local_members
     own_columns = ensemble_weights(predicted, obs_values, obs_error, noise, offset, local_members)
     scale_factor = 1.0 / math.sqrt(members - 1.0)
-    scaled = params * scale_factor
     update = jnp.dot(
-        own_columns.T,
-        lax.all_gather(scaled, "grp", axis=0, tiled=True),
+        own_columns.T * scale_factor,
+        lax.all_gather(params, "grp", axis=0, tiled=True),
         precision=lax.Precision.HIGHEST,
         preferred_element_type=jnp.float32,
     )

time: 308 us -> 309 us (level)
  no operation moved by 1% of the time
where the time goes in v7:
time: 309 us; the launch traced here: 308 us
  blocking collectives  163 us (53%)
  other arithmetic  63.1 us (20%)
  starting transfers between devices  27.4 us (9%)
  between operations  15.4 us (5%)
  waiting for transfers between devices  15 us (5%)
  local copies, waits for them, and re-layouts  14.1 us (5%)
  matrix products  9.86 us (3%)
    psum x10, blocking collectives, cell_sum(): values = lax.psum(values, axis)  112 us
    all_gather x1, blocking collectives, local(): predicted = lax.all_gather(slab_pred, 'grp', axis=0, tiled=True)  50.5 us
    ppermute x5, waiting for transfers between devices, cell_sum(): lax.ppermute(values, axis, [(i, i ^ step) for i in range(size)])  14.8 us
    another operation x3, other arithmetic, ensemble_weights(): factor = jnp.linalg.cholesky(gram)  12.4 us
    ppermute x3, starting transfers between devices, planes(): low = lax.ppermute(field[:, -1:], CELL, forward)  12.2 us
    another operation x2, other arithmetic, ensemble_weights(): return jax.scipy.linalg.cho_solve((factor, True), cross)  10.5 us
    mul x5, other arithmetic, net(): flow_z = coef_z * diff_z  7.78 us
    dot_general x1, matrix products, local(): jnp.dot(own_columns.T * scale_factor, lax.all_gather(params, 'grp', axis=...  7.08 us
  transfers between devices with their start and end apart: 14, of which 6 were waited for; matrix products, arithmetic and copies ran while one was open for 24% of the time, Pallas kernels for 0%

profile of v7, /device:TPU:1, one launch (start us, length us, event | category | flops | bytes accessed | tf_op | source)
XLA Modules:
  0.0 307.7 jit_solution(13888019850334713012)
XLA Ops:
  7.3 1.2 slice_bitcast_fusion.11
  11.3 1.3 collective-permute-start.1
  13.3 5.0 %collective-permute-start = (f32[16,3,1,16,128]{4,3,0,2,1:T(8,128)}, f32[16,3,1,16,128]{4,3,0,2,1:T(8,128)S(1)}, u32[]{:S(2)}, u32[]{:S(2)}) collective-permute-start(f32[16,3,1,16,128]{4,3,0,2,1:T(8,128)} %pad_maximum_fusion.12), channel_id=1, source_target_pairs={{0,1},{1,2},{2,3},{3,4},{4,5},{5,6},{6,7},{7,8},{8,9},{9,10},{10,1... | collective-permute-start | bytes 1179656 | tf_op jit(solution)/shard_map/ppermute | solution.py:155
  18.3 1.3 pad_maximum_fusion.4
  20.8 1.6 copy.165
  22.5 1.9 gather_fusion
  27.1 1.2 fusion.56
  28.3 1.3 fusion.55
  30.9 1.6 fusion.93
  34.1 19.3 %psum.70 = f32[2,16]{1,0:T(2,128)S(1)} all-reduce(f32[2,16]{1,0:T(2,128)S(1)} %pad_maximum_fusion.16), channel_id=1, replica_groups=mesh['grp'=8,'cy'=4,'cz'=8] {'cz'}, use_global_device_ids=true, to_apply=%region_2.3 | all-reduce | flops 32 | bytes 256 | tf_op jit(solution)/shard_map/psum | solution.py:25
  53.4 10.3 %psum.71 = f32[2,16]{1,0:T(2,128)S(1)} all-reduce(f32[2,16]{1,0:T(2,128)S(1)} %psum.70), channel_id=1, replica_groups=mesh['grp'=8,'cy'=4,'cz'=8] {'cy'}, use_global_device_ids=true, to_apply=%region_3.4 | all-reduce | flops 32 | bytes 256 | tf_op jit(solution)/shard_map/psum | solution.py:25
  64.4 1.4 collective-permute-start.2
  65.8 4.0 %collective-permute-start.3 = (f32[16,1,16,128]{3,2,1,0:T(8,128)S(1)}, f32[16,1,16,128]{3,2,1,0:T(8,128)S(1)}, u32[]{:S(2)}, u32[]{:S(2)}) collective-permute-start(f32[16,1,16,128]{3,2,1,0:T(8,128)S(1)} %get-tuple-element.72), channel_id=1, source_target_pairs={{0,1},{1,2},{2,3},{3,4},{4,5},{5,6},{6,7},{7,8},{8,9},{9,10},{10,1... | collective-permute-start | bytes 393224 | tf_op jit(solution)/shard_map/ppermute | solution.py:172
  69.8 2.0 multiply_multiply_fusion.10
  71.8 1.2 broadcast_divide_fusion
  73.5 1.1 multiply_subtract_fusion.8
  76.6 14.2 %psum.72 = f32[3,16]{1,0:T(4,128)S(1)} all-reduce(f32[3,16]{1,0:T(4,128)S(1)} %pad_maximum_fusion.14), channel_id=1, replica_groups=mesh['grp'=8,'cy'=4,'cz'=8] {'cz'}, use_global_device_ids=true, to_apply=%region_7.8 | all-reduce | flops 48 | bytes 384 | tf_op jit(solution)/shard_map/psum | solution.py:25
  90.9 6.0 %psum.73 = f32[3,16]{1,0:T(4,128)S(1)} all-reduce(f32[3,16]{1,0:T(4,128)S(1)} %psum.72), channel_id=1, replica_groups=mesh['grp'=8,'cy'=4,'cz'=8] {'cy'}, use_global_device_ids=true, to_apply=%region_8.9 | all-reduce | flops 48 | bytes 384 | tf_op jit(solution)/shard_map/psum | solution.py:25
  97.4 2.6 multiply_subtract_fusion.1
  100.4 1.3 collective-permute-start.4
  101.7 4.2 %collective-permute-start.5 = (f32[16,1,16,128]{3,2,1,0:T(8,128)S(1)}, f32[16,1,16,128]{3,2,1,0:T(8,128)S(1)}, u32[]{:S(2)}, u32[]{:S(2)}) collective-permute-start(f32[16,1,16,128]{3,2,1,0:T(8,128)S(1)} %get-tuple-element.70), channel_id=1, source_target_pairs={{0,1},{1,2},{2,3},{3,4},{4,5},{5,6},{6,7},{7,8},{8,9},{9,10},{10,1... | collective-permute-start | bytes 393224 | tf_op jit(solution)/shard_map/ppermute | solution.py:172
  105.9 2.0 multiply_multiply_fusion.9
  108.4 1.3 multiply_subtract_fusion.6
  112.2 14.7 %psum.74 = f32[4,16]{1,0:T(4,128)} all-reduce(f32[4,16]{1,0:T(4,128)S(1)} %pad_maximum_fusion.15), channel_id=1, replica_groups=mesh['grp'=8,'cy'=4,'cz'=8] {'cz'}, use_global_device_ids=true, to_apply=%region_13.14 | all-reduce | flops 64 | bytes 512 | tf_op jit(solution)/shard_map/psum | solution.py:25
  126.9 7.4 %psum.75 = f32[4,16]{1,0:T(4,128)} all-reduce(f32[4,16]{1,0:T(4,128)} %psum.74), channel_id=1, replica_groups=mesh['grp'=8,'cy'=4,'cz'=8] {'cy'}, use_global_device_ids=true, to_apply=%region_14.15 | all-reduce | flops 64 | bytes 512 | tf_op jit(solution)/shard_map/psum | solution.py:25
  136.1 2.4 copy_subtract_fusion
  138.9 1.4 collective-permute-start.6
  140.3 4.0 %collective-permute-start.7 = (f32[16,1,16,128]{3,2,1,0:T(8,128)S(1)}, f32[16,1,16,128]{3,2,1,0:T(8,128)S(1)}, u32[]{:S(2)}, u32[]{:S(2)}) collective-permute-start(f32[16,1,16,128]{3,2,1,0:T(8,128)S(1)} %get-tuple-element.68), channel_id=1, source_target_pairs={{0,1},{1,2},{2,3},{3,4},{4,5},{5,6},{6,7},{7,8},{8,9},{9,10},{10,1... | collective-permute-start | bytes 393224 | tf_op jit(solution)/shard_map/ppermute | solution.py:172
  144.4 1.2 multiply_multiply_fusion.8
  146.2 1.2 multiply_subtract_fusion.4
  149.6 14.1 %psum.76 = f32[5,16]{1,0:T(8,128)S(1)} all-reduce(f32[5,16]{1,0:T(8,128)S(1)} %stack.169), channel_id=1, replica_groups=mesh['grp'=8,'cy'=4,'cz'=8] {'cz'}, use_global_device_ids=true, to_apply=%region_20.21 | all-reduce | flops 80 | bytes 640 | tf_op jit(solution)/shard_map/psum | solution.py:25
  163.7 7.9 %psum.77 = f32[5,16]{1,0:T(8,128)S(1)} all-reduce(f32[5,16]{1,0:T(8,128)S(1)} %psum.76), channel_id=1, replica_groups=mesh['grp'=8,'cy'=4,'cz'=8] {'cy'}, use_global_device_ids=true, to_apply=%region_21.22 | all-reduce | flops 80 | bytes 640 | tf_op jit(solution)/shard_map/psum | solution.py:25
  171.7 2.3 multiply_reduce_fusion.1
  174.0 12.3 %psum.78 = f32[16]{0:T(128)S(1)} all-reduce(f32[16]{0:T(128)S(1)} %multiply_reduce_fusion.1), channel_id=1, replica_groups=mesh['grp'=8,'cy'=4,'cz'=8] {'cz'}, use_global_device_ids=true, to_apply=%region_23.24 | all-reduce | flops 16 | bytes 128 | tf_op jit(solution)/shard_map/psum | solution.py:25
  186.3 6.1 %psum.79 = f32[16]{0:T(128)S(1)} all-reduce(f32[16]{0:T(128)S(1)} %psum.78), channel_id=1, replica_groups=mesh['grp'=8,'cy'=4,'cz'=8] {'cy'}, use_global_device_ids=true, to_apply=%region_24.25 | all-reduce | flops 16 | bytes 128 | tf_op jit(solution)/shard_map/psum | solution.py:25
  192.5 2.1 multiply_add_fusion
  194.6 1.6 fusion.19
  197.7 2.5 collective-permute-done.8
  200.1 3.5 %collective-permute-done.9 = f32[16,256]{1,0:T(8,128)S(1)} collective-permute-done((f32[16,256]{1,0:T(8,128)S(1)}, f32[16,256]{1,0:T(8,128)S(1)}, u32[]{:S(2)}, u32[]{:S(2)}) %collective-permute-start.9) | collective-permute-done | bytes 16416 | tf_op jit(solution)/shard_map/ppermute | solution.py:29
  203.7 2.3 collective-permute-start.10
  205.9 4.4 %collective-permute-done.10 = f32[16,256]{1,0:T(8,128)S(1)} collective-permute-done((f32[16,256]{1,0:T(8,128)S(1)}, f32[16,256]{1,0:T(8,128)S(1)}, u32[]{:S(2)}, u32[]{:S(2)}) %collective-permute-start.10) | collective-permute-done | bytes 16416 | tf_op jit(solution)/shard_map/ppermute | solution.py:29
  210.3 1.4 collective-permute-start.11
  211.7 1.2 collective-permute-done.11
  213.8 3.2 %collective-permute-done.12 = f32[16,256]{1,0:T(8,128)S(1)} collective-permute-done((f32[16,256]{1,0:T(8,128)S(1)}, f32[16,256]{1,0:T(8,128)S(1)}, u32[]{:S(2)}, u32[]{:S(2)}) %collective-permute-start.12) | collective-permute-done | bytes 16416 | tf_op jit(solution)/shard_map/ppermute | solution.py:29
  217.0 50.5 %all_gather.6 = f32[128,256]{1,0:T(8,128)S(1)} all-gather(f32[16,256]{1,0:T(8,128)S(1)} %add.480), channel_id=1, replica_groups=mesh['grp'=8,'cy'=4,'cz'=8] {'grp'}, dimensions={0}, use_global_device_ids=true | all-gather | bytes 147456 | tf_op jit(solution)/shard_map/all_gather | solution.py:252
  268.0 11.7 %cholesky.17 = f32[128,128]{1,0:T(8,128)S(1)} custom-call(f32[128,128]{1,0:T(8,128)S(1)} %fusion.70), custom_call_target="Cholesky" | custom-call | tf_op jit(solution)/shard_map/jit(cholesky)/cholesky | solution.py:130
  281.1 9.8 %custom-call.10 = f32[1,128,128]{1,2,0:T(8,128)S(1)} custom-call(f32[1,128,128]{2,1,0:T(8,128)S(1)} %fusion.65), custom_call_target="InvertDiagBlocksLowerTriangular" | custom-call | tf_op jit(solution)/shard_map/jit(_cho_solve)/triangular_solve | solution.py:131
  292.4 7.1 %fusion = f32[2,8,128,128]{3,1,2,0:T(8,128)S(1)} fusion(f32[16,128]{1,0:T(8,128)S(1)} %convolution_multiply_fusion, f32[128,16384]{1,0:T(8,128)} %all-gather.2.cloned.1.call-done, f32[2,8,128,128]{3,2,1,0:T(8,128)S(1)} %bitcast.506), kind=kOutput, calls=%fused_computation.3 | convolution fusion | flops 402915328 | bytes 10493952 | tf_op jit(solution)/shard_map/dot_general | solution.py:257
  (241 shorter events, 28.8 us)
Async XLA Ops:
  7.2 15.3 %copy-start = (s32[128]{0:T(128)S(1)}, s32[128]{0:T(128)}, u32[]{:S(2)}) copy-start(s32[128]{0:T(128)} %param.18) | copy-start | bytes 1540
  7.2 19.1 %copy-start.2 = (f32[16,2,4,16,128]{4,3,2,1,0:T(8,128)S(1)}, f32[16,2,4,16,128]{4,3,2,1,0:T(8,128)}, u32[]{:S(2)}) copy-start(f32[16,2,4,16,128]{4,3,2,1,0:T(8,128)} %param.10) | copy-start | bytes 3145732
  7.2 18.8 %copy-start.3 = (f32[16,4,16,128]{3,2,1,0:T(8,128)S(1)}, f32[16,4,16,128]{3,2,1,0:T(8,128)}, u32[]{:S(2)}) copy-start(f32[16,4,16,128]{3,2,1,0:T(8,128)} %param.13) | copy-start | bytes 1572868
  7.2 15.3 %copy-start.53 = (s32[256]{0:T(256)S(1)}, s32[256]{0:T(256)}, u32[]{:S(2)}) copy-start(s32[256]{0:T(256)} %param.19) | copy-start | bytes 3076
  7.2 285.2 %all-gather.2.cloned.1.call-start = ((), (), s32[]{:S(2)}) async-start(), calls=%async_computation | async-start | bytes 9437184 | tf_op jit(solution)/shard_map/all_gather | solution.py:259
  10.5 16.1 %copy-start.27 = (f32[16,4,16,128]{3,2,1,0:T(8,128)S(1)}, f32[16,4,16,128]{3,2,1,0:T(8,128)}, u32[]{:S(2)}) copy-start(f32[16,4,16,128]{3,2,1,0:T(8,128)} %param.11) | copy-start | bytes 1572868
  11.3 15.3 %collective-permute-start.1 = (f32[16,3,1,16,128]{4,3,0,2,1:T(8,128)}, f32[16,3,1,16,128]{4,3,0,2,1:T(8,128)S(1)}, u32[]{:S(2)}, u32[]{:S(2)}) collective-permute-start(f32[16,3,1,16,128]{4,3,0,2,1:T(8,128)} %pad_maximum_fusion.13), channel_id=1, source_target_pairs={{1,0},{2,1},{3,2},{4,3},{5,4},{6,5},{7,6},{8,7},{9,8},{10,9},{11,1... | collective-permute-start | bytes 1179656 | tf_op jit(solution)/shard_map/ppermute | solution.py:156
  13.3 13.2 %collective-permute-start = (f32[16,3,1,16,128]{4,3,0,2,1:T(8,128)}, f32[16,3,1,16,128]{4,3,0,2,1:T(8,128)S(1)}, u32[]{:S(2)}, u32[]{:S(2)}) collective-permute-start(f32[16,3,1,16,128]{4,3,0,2,1:T(8,128)} %pad_maximum_fusion.12), channel_id=1, source_target_pairs={{0,1},{1,2},{2,3},{3,4},{4,5},{5,6},{6,7},{7,8},{8,9},{9,10},{10,1... | collective-permute-start | bytes 1179656 | tf_op jit(solution)/shard_map/ppermute | solution.py:155
  25.7 80.2 %copy-start.43 = (f32[128]{0:T(128)}, f32[128]{0:T(128)S(1)}, u32[]{:S(2)}) copy-start(f32[128]{0:T(128)S(1)} %compare_convert_fusion) | copy-start | bytes 1540
  25.7 80.2 %copy-start.44 = (f32[16]{0:T(128)}, f32[16]{0:T(128)S(1)}, u32[]{:S(2)}) copy-start(f32[16]{0:T(128)S(1)} %compare_convert_fusion.1) | copy-start | bytes 196
  33.8 42.0 %copy-start.5 = (f32[16,1,4,16,128]{4,3,2,0,1:T(8,128)}, f32[16,1,4,16,128]{4,3,2,0,1:T(8,128)S(1)}, u32[]{:S(2)}) copy-start(f32[16,1,4,16,128]{4,3,2,0,1:T(8,128)S(1)} %fusion.45) | copy-start | bytes 1572868
  63.7 33.1 %copy-start.47 = (f32[2,16]{1,0:T(2,128)}, f32[2,16]{1,0:T(2,128)S(1)}, u32[]{:S(2)}) copy-start(f32[2,16]{1,0:T(2,128)S(1)} %psum.71) | copy-start | bytes 388
  63.8 10.8 %copy-start.17 = (f32[16,5,16,128]{3,2,1,0:T(8,128)S(1)}, f32[16,5,16,128]{3,2,1,0:T(8,128)}, u32[]{:S(2)}) copy-start(f32[16,5,16,128]{3,2,1,0:T(8,128)} %get-tuple-element.28) | copy-start | bytes 1966084
  63.8 10.8 %copy-start.20 = (f32[16,5,16,128]{3,2,1,0:T(8,128)S(1)}, f32[16,5,16,128]{3,2,1,0:T(8,128)}, u32[]{:S(2)}) copy-start(f32[16,5,16,128]{3,2,1,0:T(8,128)} %get-tuple-element.34) | copy-start | bytes 1966084
  64.0 11.3 %copy-start.12 = (f32[16,2,4,16,128]{4,3,2,0,1:T(8,128)}, f32[16,2,4,16,128]{4,3,2,0,1:T(8,128)S(1)}, u32[]{:S(2)}) copy-start(f32[16,2,4,16,128]{4,3,2,0,1:T(8,128)S(1)} %multiply_subtract_fusion.2) | copy-start | bytes 3145732
  64.4 9.1 %collective-permute-start.2 = (f32[16,1,16,128]{3,2,1,0:T(8,128)S(1)}, f32[16,1,16,128]{3,2,1,0:T(8,128)S(1)}, u32[]{:S(2)}, u32[]{:S(2)}) collective-permute-start(f32[16,1,16,128]{3,2,1,0:T(8,128)S(1)} %get-tuple-element.71), channel_id=1, source_target_pairs={{1,0},{2,1},{3,2},{4,3},{5,4},{6,5},{7,6},{8,7},{9,8},{10,9},{11,1... | collective-permute-start | bytes 393224 | tf_op jit(solution)/shard_map/ppermute | solution.py:173
  65.8 7.7 %collective-permute-start.3 = (f32[16,1,16,128]{3,2,1,0:T(8,128)S(1)}, f32[16,1,16,128]{3,2,1,0:T(8,128)S(1)}, u32[]{:S(2)}, u32[]{:S(2)}) collective-permute-start(f32[16,1,16,128]{3,2,1,0:T(8,128)S(1)} %get-tuple-element.72), channel_id=1, source_target_pairs={{0,1},{1,2},{2,3},{3,4},{4,5},{5,6},{6,7},{7,8},{8,9},{9,10},{10,1... | collective-permute-start | bytes 393224 | tf_op jit(solution)/shard_map/ppermute | solution.py:172
  96.9 11.5 %copy-start.45 = (f32[3,16]{1,0:T(4,128)}, f32[3,16]{1,0:T(4,128)S(1)}, u32[]{:S(2)}) copy-start(f32[3,16]{1,0:T(4,128)S(1)} %psum.73) | copy-start | bytes 580
  97.4 11.0 %copy-start.51 = (f32[16]{0:T(128)}, f32[16]{0:T(128)S(1)}, u32[]{:S(2)}) copy-start(f32[16]{0:T(128)S(1)} %get-tuple-element.98) | copy-start | bytes 196
  97.4 12.3 %copy-start.18 = (f32[16,5,16,128]{3,2,1,0:T(8,128)S(1)}, f32[16,5,16,128]{3,2,1,0:T(8,128)}, u32[]{:S(2)}) copy-start(f32[16,5,16,128]{3,2,1,0:T(8,128)} %get-tuple-element.28) | copy-start | bytes 1966084
  97.4 12.3 %copy-start.21 = (f32[16,5,16,128]{3,2,1,0:T(8,128)S(1)}, f32[16,5,16,128]{3,2,1,0:T(8,128)}, u32[]{:S(2)}) copy-start(f32[16,5,16,128]{3,2,1,0:T(8,128)} %get-tuple-element.34) | copy-start | bytes 1966084
  100.0 10.3 %copy-start.9 = (f32[16,4,16,128]{3,2,1,0:T(8,128)S(1)}, f32[16,4,16,128]{3,2,1,0:T(8,128)}, u32[]{:S(2)}) copy-start(f32[16,4,16,128]{3,2,1,0:T(8,128)} %param.12) | copy-start | bytes 1572868
  100.4 8.0 %collective-permute-start.4 = (f32[16,1,16,128]{3,2,1,0:T(8,128)S(1)}, f32[16,1,16,128]{3,2,1,0:T(8,128)S(1)}, u32[]{:S(2)}, u32[]{:S(2)}) collective-permute-start(f32[16,1,16,128]{3,2,1,0:T(8,128)S(1)} %get-tuple-element.69), channel_id=1, source_target_pairs={{1,0},{2,1},{3,2},{4,3},{5,4},{6,5},{7,6},{8,7},{9,8},{10,9},{11,1... | collective-permute-start | bytes 393224 | tf_op jit(solution)/shard_map/ppermute | solution.py:173
  101.7 6.7 %collective-permute-start.5 = (f32[16,1,16,128]{3,2,1,0:T(8,128)S(1)}, f32[16,1,16,128]{3,2,1,0:T(8,128)S(1)}, u32[]{:S(2)}, u32[]{:S(2)}) collective-permute-start(f32[16,1,16,128]{3,2,1,0:T(8,128)S(1)} %get-tuple-element.70), channel_id=1, source_target_pairs={{0,1},{1,2},{2,3},{3,4},{4,5},{5,6},{6,7},{7,8},{8,9},{9,10},{10,1... | collective-permute-start | bytes 393224 | tf_op jit(solution)/shard_map/ppermute | solution.py:172
  136.0 10.2 %copy-start.49 = (f32[16]{0:T(128)}, f32[16]{0:T(128)S(1)}, u32[]{:S(2)}) copy-start(f32[16]{0:T(128)S(1)} %get-tuple-element.91) | copy-start | bytes 196
  136.0 10.2 %copy-start.40 = (f32[16,1,16,128]{3,2,1,0:T(8,128)S(1)}, f32[16,1,16,128]{3,2,1,0:T(8,128)}, u32[]{:S(2)}) copy-start(f32[16,1,16,128]{3,2,1,0:T(8,128)} %copy-done.39) | copy-start | bytes 393220
  136.0 11.4 %copy-start.19 = (f32[16,5,16,128]{3,2,1,0:T(8,128)S(1)}, f32[16,5,16,128]{3,2,1,0:T(8,128)}, u32[]{:S(2)}) copy-start(f32[16,5,16,128]{3,2,1,0:T(8,128)} %get-tuple-element.28) | copy-start | bytes 1966084
  136.0 11.4 %copy-start.22 = (f32[16,5,16,128]{3,2,1,0:T(8,128)S(1)}, f32[16,5,16,128]{3,2,1,0:T(8,128)}, u32[]{:S(2)}) copy-start(f32[16,5,16,128]{3,2,1,0:T(8,128)} %get-tuple-element.34) | copy-start | bytes 1966084
  138.5 10.2 %copy-start.4 = (f32[16,2,4,16,128]{4,3,2,1,0:T(8,128)}, f32[16,2,4,16,128]{4,3,2,1,0:T(8,128)S(1)}, u32[]{:S(2)}) copy-start(f32[16,2,4,16,128]{4,3,2,1,0:T(8,128)S(1)} %copy_subtract_fusion) | copy-start | bytes 3145732
  138.9 7.2 %collective-permute-start.6 = (f32[16,1,16,128]{3,2,1,0:T(8,128)S(1)}, f32[16,1,16,128]{3,2,1,0:T(8,128)S(1)}, u32[]{:S(2)}, u32[]{:S(2)}) collective-permute-start(f32[16,1,16,128]{3,2,1,0:T(8,128)S(1)} %get-tuple-element.67), channel_id=1, source_target_pairs={{1,0},{2,1},{3,2},{4,3},{5,4},{6,5},{7,6},{8,7},{9,8},{10,9},{11,1... | collective-permute-start | bytes 393224 | tf_op jit(solution)/shard_map/ppermute | solution.py:173
  140.3 5.9 %collective-permute-start.7 = (f32[16,1,16,128]{3,2,1,0:T(8,128)S(1)}, f32[16,1,16,128]{3,2,1,0:T(8,128)S(1)}, u32[]{:S(2)}, u32[]{:S(2)}) collective-permute-start(f32[16,1,16,128]{3,2,1,0:T(8,128)S(1)} %get-tuple-element.68), channel_id=1, source_target_pairs={{0,1},{1,2},{2,3},{3,4},{4,5},{5,6},{6,7},{7,8},{8,9},{9,10},{10,1... | collective-permute-start | bytes 393224 | tf_op jit(solution)/shard_map/ppermute | solution.py:172
  148.2 44.2 %copy-start.42 = (f32[4,16]{1,0:T(4,128)S(1)}, f32[4,16]{1,0:T(4,128)}, u32[]{:S(2)}) copy-start(f32[4,16]{1,0:T(4,128)} %psum.75) | copy-start | bytes 772
  148.2 44.2 %copy-start.46 = (f32[3,16]{1,0:T(4,128)S(1)}, f32[3,16]{1,0:T(4,128)}, u32[]{:S(2)}) copy-start(f32[3,16]{1,0:T(4,128)} %copy-done.45) | copy-start | bytes 580
  148.2 44.2 %copy-start.48 = (f32[2,16]{1,0:T(2,128)S(1)}, f32[2,16]{1,0:T(2,128)}, u32[]{:S(2)}) copy-start(f32[2,16]{1,0:T(2,128)} %copy-done.47) | copy-start | bytes 388
  148.2 44.2 %copy-start.50 = (f32[16]{0:T(128)S(1)}, f32[16]{0:T(128)}, u32[]{:S(2)}) copy-start(f32[16]{0:T(128)} %copy-done.49) | copy-start | bytes 196
  148.2 44.2 %copy-start.52 = (f32[16]{0:T(128)S(1)}, f32[16]{0:T(128)}, u32[]{:S(2)}) copy-start(f32[16]{0:T(128)} %copy-done.51) | copy-start | bytes 196
  148.2 44.2 %copy-start.55 = (f32[16]{0:T(128)S(1)}, f32[16]{0:T(128)}, u32[]{:S(2)}) copy-start(f32[16]{0:T(128)} %get-tuple-element.97) | copy-start | bytes 196
  173.9 22.5 %copy-start.41 = (f32[128,256]{1,0:T(8,128)S(1)}, f32[128,256]{1,0:T(8,128)}, u32[]{:S(2)}) copy-start(f32[128,256]{1,0:T(8,128)} %fusion.60) | copy-start | bytes 393220
  174.0 22.5 %copy-start.54 = (s32[256]{0:T(256)S(1)}, s32[256]{0:T(256)}, u32[]{:S(2)}) copy-start(s32[256]{0:T(256)} %get-tuple-element.15) | copy-start | bytes 3076
  174.0 39.9 %copy-start.56 = (f32[256]{0:T(256)S(1)}, f32[256]{0:T(256)}, u32[]{:S(2)}) copy-start(f32[256]{0:T(256)} %param.16) | copy-start | bytes 3076
  174.0 116.9 %copy-start.57 = (f32[256]{0:T(256)S(1)}, f32[256]{0:T(256)}, u32[]{:S(2)}) copy-start(f32[256]{0:T(256)} %param.15) | copy-start | bytes 3076
  194.6 97.8 %copy-start.24 = (f32[16,2,4,16,128]{4,3,2,1,0:T(8,128)S(1)}, f32[16,2,4,16,128]{4,3,2,1,0:T(8,128)}, u32[]{:S(2)}) copy-start(f32[16,2,4,16,128]{4,3,2,1,0:T(8,128)} %copy-done.23) | copy-start | bytes 3145732
  197.5 2.7 collective-permute-start.8
  200.1 3.5 %collective-permute-start.9 = (f32[16,256]{1,0:T(8,128)S(1)}, f32[16,256]{1,0:T(8,128)S(1)}, u32[]{:S(2)}, u32[]{:S(2)}) collective-permute-start(f32[16,256]{1,0:T(8,128)S(1)} %add.476), channel_id=1, source_target_pairs={{0,2},{1,3},{2,0},{3,1},{4,6},{5,7},{6,4},{7,5},{8,10},{9,11},{10,... | collective-permute-start | bytes 49160 | tf_op jit(solution)/shard_map/ppermute | solution.py:29
  203.7 6.7 %collective-permute-start.10 = (f32[16,256]{1,0:T(8,128)S(1)}, f32[16,256]{1,0:T(8,128)S(1)}, u32[]{:S(2)}, u32[]{:S(2)}) collective-permute-start(f32[16,256]{1,0:T(8,128)S(1)} %add.477), channel_id=1, source_target_pairs={{0,4},{1,5},{2,6},{3,7},{4,0},{5,1},{6,2},{7,3},{8,12},{9,13},{10,... | collective-permute-start | bytes 49160 | tf_op jit(solution)/shard_map/ppermute | solution.py:29
  210.3 2.6 collective-permute-start.11
  212.9 4.1 %collective-permute-start.12 = (f32[16,256]{1,0:T(8,128)S(1)}, f32[16,256]{1,0:T(8,128)S(1)}, u32[]{:S(2)}, u32[]{:S(2)}) collective-permute-start(f32[16,256]{1,0:T(8,128)S(1)} %add.479), channel_id=1, source_target_pairs={{0,16},{8,24},{16,0},{24,8},{1,17},{9,25},{17,1},{25,9},{2,18},{10... | collective-permute-start | bytes 49160 | tf_op jit(solution)/shard_map/ppermute | solution.py:29
  217.0 83.8 %copy-start.1 = (s32[128]{0:T(128)S(1)}, s32[128]{0:T(128)}, u32[]{:S(2)}) copy-start(s32[128]{0:T(128)} %param.18) | copy-start | bytes 1540
  (24 other events, 93.7 us)
Sparse Core Ops, SparseCore 0:
  22.6 56.6 all-gather.1

commit v8 on v7

--- a/solution.py
+++ b/solution.py
@@ -250,19 +250,21 @@
     )
     slab_pred = cell_sum(picked, doubling=True)
     predicted = lax.all_gather(slab_pred, "grp", axis=0, tiled=True)
-    params = jnp.stack([log_perm, porosity], 1).reshape(local_members, 2 * cells_dev)
     offset = lax.axis_index("grp") * local_members
     own_columns = ensemble_weights(predicted, obs_values, obs_error, noise, offset, local_members)
     scale_factor = 1.0 / math.sqrt(members - 1.0)
-    update = jnp.dot(
-        own_columns.T * scale_factor,
-        lax.all_gather(params, "grp", axis=0, tiled=True),
-        precision=lax.Precision.HIGHEST,
-        preferred_element_type=jnp.float32,
-    )
-    posterior = params + update
-    posterior = posterior.reshape(local_members, 2, slab_x, plane_rows, plane_cols)
-    return (increment, posterior[:, 0], posterior[:, 1])
+
+    def posterior_of(theta):
+        flat = theta.reshape(local_members, cells_dev)
+        update = jnp.dot(
+            own_columns.T,
+            lax.all_gather(flat * scale_factor, "grp", axis=0, tiled=True),
+            precision=lax.Precision.HIGHEST,
+            preferred_element_type=jnp.float32,
+        )
+        return (flat + update).reshape(theta.shape)
+
+    return (increment, posterior_of(log_perm), posterior_of(porosity))
 
 
 def split_mesh(mesh):

time: 309 us -> 314 us (1.016)
  blocking collectives: 163 us -> 167 us
    mul x5, other arithmetic: 7.78 us -> 4.34 us  [net(): flow_z = coef_z * diff_z]
    mul x0 -> x2, other arithmetic: none -> 3.36 us  [posterior_of(): flat * scale_factor]
    dot_general x1 -> x2, matrix products: 7.08 us -> 8.21 us  [posterior_of(): jnp.dot(own_columns.T, lax.all_gather(flat * scale_factor, 'grp', axis=0,...]
  transfers between devices with their start and end apart: 14 -> 15, of which waited for: 6 -> 8; matrix products, arithmetic and copies ran while one was open for 24% -> 25% of each run, Pallas kernels for 0% -> 0%
where the time goes in v8:
time: 314 us; the launch traced here: 313 us
  blocking collectives  167 us (53%)
  other arithmetic  61.2 us (19%)
  starting transfers between devices  27.8 us (9%)
  waiting for transfers between devices  17 us (5%)
  between operations  15.6 us (5%)
  local copies, waits for them, and re-layouts  13.4 us (4%)
  matrix products  11 us (4%)
    psum x10, blocking collectives, cell_sum(): values = lax.psum(values, axis)  115 us
    all_gather x1, blocking collectives, local(): predicted = lax.all_gather(slab_pred, 'grp', axis=0, tiled=True)  51.8 us
    ppermute x5, waiting for transfers between devices, cell_sum(): lax.ppermute(values, axis, [(i, i ^ step) for i in range(size)])  15.2 us
    ppermute x3, starting transfers between devices, planes(): low = lax.ppermute(field[:, -1:], CELL, forward)  12.5 us
    another operation x3, other arithmetic, ensemble_weights(): factor = jnp.linalg.cholesky(gram)  12.4 us
    another operation x2, other arithmetic, ensemble_weights(): return jax.scipy.linalg.cho_solve((factor, True), cross)  10.5 us
    dot_general x2, matrix products, posterior_of(): jnp.dot(own_columns.T, lax.all_gather(flat * scale_factor, 'grp', axis=0,...  8.21 us
  transfers between devices with their start and end apart: 15, of which 8 were waited for; matrix products, arithmetic and copies ran while one was open for 25% of the time, Pallas kernels for 0%

profile of v8, /device:TPU:1, one launch (start us, length us, event | category | flops | bytes accessed | tf_op | source)
XLA Modules:
  0.0 312.8 jit_solution(6254981057403881206)
XLA Ops:
  7.2 2.2 bitcast_multiply_fusion.1
  10.6 1.1 slice_bitcast_fusion.9
  11.7 1.0 slice_bitcast_fusion.15
  13.5 1.3 collective-permute-start.1
  15.6 5.7 %collective-permute-start = (f32[16,3,1,16,128]{4,3,0,2,1:T(8,128)}, f32[16,3,1,16,128]{4,3,0,2,1:T(8,128)}, u32[]{:S(2)}, u32[]{:S(2)}) collective-permute-start(f32[16,3,1,16,128]{4,3,0,2,1:T(8,128)} %pad_maximum_fusion.11), channel_id=1, source_target_pairs={{0,1},{1,2},{2,3},{3,4},{4,5},{5,6},{6,7},{7,8},{8,9},{9,10},{10,1... | collective-permute-start | bytes 1179656 | tf_op jit(solution)/shard_map/ppermute | solution.py:155
  21.3 1.1 bitcast_multiply_fusion
  22.6 1.9 gather_fusion
  26.9 1.1 slice_bitcast_fusion.16
  28.5 1.2 fusion.57
  29.7 1.3 fusion.56
  32.3 1.6 fusion.95
  35.5 20.3 %psum.70 = f32[2,16]{1,0:T(2,128)S(1)} all-reduce(f32[2,16]{1,0:T(2,128)S(1)} %pad_maximum_fusion.15), channel_id=1, replica_groups=mesh['grp'=8,'cy'=4,'cz'=8] {'cz'}, use_global_device_ids=true, to_apply=%region_2.3 | all-reduce | flops 32 | bytes 256 | tf_op jit(solution)/shard_map/psum | solution.py:25
  55.8 9.0 %psum.71 = f32[2,16]{1,0:T(2,128)S(1)} all-reduce(f32[2,16]{1,0:T(2,128)S(1)} %psum.70), channel_id=1, replica_groups=mesh['grp'=8,'cy'=4,'cz'=8] {'cy'}, use_global_device_ids=true, to_apply=%region_3.4 | all-reduce | flops 32 | bytes 256 | tf_op jit(solution)/shard_map/psum | solution.py:25
  65.4 1.4 collective-permute-start.2
  66.9 4.3 %collective-permute-start.3 = (f32[16,1,16,128]{3,2,1,0:T(8,128)S(1)}, f32[16,1,16,128]{3,2,1,0:T(8,128)S(1)}, u32[]{:S(2)}, u32[]{:S(2)}) collective-permute-start(f32[16,1,16,128]{3,2,1,0:T(8,128)S(1)} %get-tuple-element.70), channel_id=1, source_target_pairs={{0,1},{1,2},{2,3},{3,4},{4,5},{5,6},{6,7},{7,8},{8,9},{9,10},{10,1... | collective-permute-start | bytes 393224 | tf_op jit(solution)/shard_map/ppermute | solution.py:172
  71.8 1.2 broadcast_divide_fusion
  73.5 1.1 multiply_subtract_fusion.8
  76.7 14.6 %psum.72 = f32[3,16]{1,0:T(4,128)S(1)} all-reduce(f32[3,16]{1,0:T(4,128)S(1)} %pad_maximum_fusion.13), channel_id=1, replica_groups=mesh['grp'=8,'cy'=4,'cz'=8] {'cz'}, use_global_device_ids=true, to_apply=%region_7.8 | all-reduce | flops 48 | bytes 384 | tf_op jit(solution)/shard_map/psum | solution.py:25
  91.3 7.2 %psum.73 = f32[3,16]{1,0:T(4,128)S(1)} all-reduce(f32[3,16]{1,0:T(4,128)S(1)} %psum.72), channel_id=1, replica_groups=mesh['grp'=8,'cy'=4,'cz'=8] {'cy'}, use_global_device_ids=true, to_apply=%region_8.9 | all-reduce | flops 48 | bytes 384 | tf_op jit(solution)/shard_map/psum | solution.py:25
  99.2 2.8 multiply_subtract_fusion.1
  102.3 1.3 collective-permute-start.4
  103.6 4.2 %collective-permute-start.5 = (f32[16,1,16,128]{3,2,1,0:T(8,128)S(1)}, f32[16,1,16,128]{3,2,1,0:T(8,128)S(1)}, u32[]{:S(2)}, u32[]{:S(2)}) collective-permute-start(f32[16,1,16,128]{3,2,1,0:T(8,128)S(1)} %get-tuple-element.68), channel_id=1, source_target_pairs={{0,1},{1,2},{2,3},{3,4},{4,5},{5,6},{6,7},{7,8},{8,9},{9,10},{10,1... | collective-permute-start | bytes 393224 | tf_op jit(solution)/shard_map/ppermute | solution.py:172
  109.6 1.1 multiply_subtract_fusion.6
  113.7 15.0 %psum.74 = f32[4,16]{1,0:T(4,128)} all-reduce(f32[4,16]{1,0:T(4,128)} %pad_maximum_fusion.14), channel_id=1, replica_groups=mesh['grp'=8,'cy'=4,'cz'=8] {'cz'}, use_global_device_ids=true, to_apply=%region_13.14 | all-reduce | flops 64 | bytes 512 | tf_op jit(solution)/shard_map/psum | solution.py:25
  128.7 8.5 %psum.75 = f32[4,16]{1,0:T(4,128)} all-reduce(f32[4,16]{1,0:T(4,128)} %psum.74), channel_id=1, replica_groups=mesh['grp'=8,'cy'=4,'cz'=8] {'cy'}, use_global_device_ids=true, to_apply=%region_14.15 | all-reduce | flops 64 | bytes 512 | tf_op jit(solution)/shard_map/psum | solution.py:25
  138.8 2.5 copy_subtract_fusion
  141.7 1.3 collective-permute-start.6
  143.0 4.0 %collective-permute-start.7 = (f32[16,1,16,128]{3,2,1,0:T(8,128)S(1)}, f32[16,1,16,128]{3,2,1,0:T(8,128)S(1)}, u32[]{:S(2)}, u32[]{:S(2)}) collective-permute-start(f32[16,1,16,128]{3,2,1,0:T(8,128)S(1)} %get-tuple-element.66), channel_id=1, source_target_pairs={{0,1},{1,2},{2,3},{3,4},{4,5},{5,6},{6,7},{7,8},{8,9},{9,10},{10,1... | collective-permute-start | bytes 393224 | tf_op jit(solution)/shard_map/ppermute | solution.py:172
  148.9 1.2 multiply_subtract_fusion.4
  152.4 13.9 %psum.76 = f32[5,16]{1,0:T(8,128)S(1)} all-reduce(f32[5,16]{1,0:T(8,128)S(1)} %stack.160), channel_id=1, replica_groups=mesh['grp'=8,'cy'=4,'cz'=8] {'cz'}, use_global_device_ids=true, to_apply=%region_20.21 | all-reduce | flops 80 | bytes 640 | tf_op jit(solution)/shard_map/psum | solution.py:25
  166.4 7.6 %psum.77 = f32[5,16]{1,0:T(8,128)S(1)} all-reduce(f32[5,16]{1,0:T(8,128)S(1)} %psum.76), channel_id=1, replica_groups=mesh['grp'=8,'cy'=4,'cz'=8] {'cy'}, use_global_device_ids=true, to_apply=%region_21.22 | all-reduce | flops 80 | bytes 640 | tf_op jit(solution)/shard_map/psum | solution.py:25
  174.0 2.4 multiply_reduce_fusion.1
  176.4 12.7 %psum.78 = f32[16]{0:T(128)S(1)} all-reduce(f32[16]{0:T(128)S(1)} %multiply_reduce_fusion.1), channel_id=1, replica_groups=mesh['grp'=8,'cy'=4,'cz'=8] {'cz'}, use_global_device_ids=true, to_apply=%region_23.24 | all-reduce | flops 16 | bytes 128 | tf_op jit(solution)/shard_map/psum | solution.py:25
  189.1 6.0 %psum.79 = f32[16]{0:T(128)S(1)} all-reduce(f32[16]{0:T(128)S(1)} %psum.78), channel_id=1, replica_groups=mesh['grp'=8,'cy'=4,'cz'=8] {'cy'}, use_global_device_ids=true, to_apply=%region_24.25 | all-reduce | flops 16 | bytes 128 | tf_op jit(solution)/shard_map/psum | solution.py:25
  195.3 2.2 multiply_add_fusion
  198.6 1.0 multiply_reduce_fusion
  199.7 2.6 collective-permute-done.8
  202.3 3.5 %collective-permute-done.9 = f32[16,256]{1,0:T(8,128)S(1)} collective-permute-done((f32[16,256]{1,0:T(8,128)S(1)}, f32[16,256]{1,0:T(8,128)S(1)}, u32[]{:S(2)}, u32[]{:S(2)}) %collective-permute-start.9) | collective-permute-done | bytes 16416 | tf_op jit(solution)/shard_map/ppermute | solution.py:29
  205.8 1.9 collective-permute-start.10
  207.7 4.8 %collective-permute-done.10 = f32[16,256]{1,0:T(8,128)S(1)} collective-permute-done((f32[16,256]{1,0:T(8,128)S(1)}, f32[16,256]{1,0:T(8,128)S(1)}, u32[]{:S(2)}, u32[]{:S(2)}) %collective-permute-start.10) | collective-permute-done | bytes 16416 | tf_op jit(solution)/shard_map/ppermute | solution.py:29
  212.5 1.3 collective-permute-start.11
  213.8 1.3 collective-permute-done.11
  216.1 3.1 collective-permute-done.12
  219.2 51.8 %all_gather.9 = f32[128,256]{1,0:T(8,128)S(1)} all-gather(f32[16,256]{1,0:T(8,128)S(1)} %add.483), channel_id=1, replica_groups=mesh['grp'=8,'cy'=4,'cz'=8] {'grp'}, dimensions={0}, use_global_device_ids=true | all-gather | bytes 147456 | tf_op jit(solution)/shard_map/all_gather | solution.py:252
  271.5 11.7 %cholesky.17 = f32[128,128]{1,0:T(8,128)S(1)} custom-call(f32[128,128]{1,0:T(8,128)S(1)} %fusion.72), custom_call_target="Cholesky" | custom-call | tf_op jit(solution)/shard_map/jit(cholesky)/cholesky | solution.py:130
  284.6 9.8 %custom-call.10 = f32[1,128,128]{1,2,0:T(8,128)S(1)} custom-call(f32[1,128,128]{2,1,0:T(8,128)S(1)} %fusion.66), custom_call_target="InvertDiagBlocksLowerTriangular" | custom-call | tf_op jit(solution)/shard_map/jit(_cho_solve)/triangular_solve | solution.py:131
  295.9 4.1 %fusion = f32[2,8,64,128]{3,1,2,0:T(8,128)S(1)} fusion(f32[128,16]{0,1:T(8,128)S(1)} %fusion.67, f32[128,8192]{1,0:T(8,128)} %all-gather.3.cloned.1.call-done, f32[2,8,64,128]{3,2,1,0:T(8,128)S(1)} %bitcast.506), kind=kOutput, calls=%fused_computation.4 | convolution fusion | flops 201457664 | bytes 5251072 | tf_op jit(solution)/shard_map/dot_general | solution.py:259
  300.9 4.1 %fusion.1 = f32[2,8,64,128]{3,1,2,0:T(8,128)S(1)} fusion(f32[128,16]{0,1:T(8,128)S(1)} %fusion.67, f32[128,8192]{1,0:T(8,128)} %all-gather.5.cloned.1.call-done, f32[2,8,64,128]{3,2,1,0:T(8,128)S(1)} %bitcast.489), kind=kOutput, calls=%fused_computation.5 | convolution fusion | flops 201457664 | bytes 5251072 | tf_op jit(solution)/shard_map/dot_general | solution.py:259
  (270 shorter events, 30.6 us)
Async XLA Ops:
  7.2 15.4 %copy-start = (s32[128]{0:T(128)S(1)}, s32[128]{0:T(128)}, u32[]{:S(2)}) copy-start(s32[128]{0:T(128)} %param.18) | copy-start | bytes 1540
  7.2 14.2 %copy-start.2 = (f32[16,4,16,128]{3,2,1,0:T(8,128)S(1)}, f32[16,4,16,128]{3,2,1,0:T(8,128)}, u32[]{:S(2)}) copy-start(f32[16,4,16,128]{3,2,1,0:T(8,128)} %param.12) | copy-start | bytes 1572868
  7.2 15.3 %copy-start.66 = (s32[256]{0:T(256)S(1)}, s32[256]{0:T(256)}, u32[]{:S(2)}) copy-start(s32[256]{0:T(256)} %param.19) | copy-start | bytes 3076
  7.2 288.7 %all-gather.3.cloned.1.call-start = ((), (), s32[]{:S(2)}) async-start(), calls=%async_computation | async-start | bytes 4718592 | tf_op jit(solution)/shard_map/all_gather | solution.py:261
  9.5 291.4 %all-gather.5.cloned.1.call-start = ((), (), s32[]{:S(2)}) async-start(), calls=%async_computation.1 | async-start | bytes 4718592 | tf_op jit(solution)/shard_map/all_gather | solution.py:261
  10.5 15.5 %copy-start.3 = (f32[16,4,16,128]{3,2,1,0:T(8,128)S(1)}, f32[16,4,16,128]{3,2,1,0:T(8,128)}, u32[]{:S(2)}) copy-start(f32[16,4,16,128]{3,2,1,0:T(8,128)} %param.13) | copy-start | bytes 1572868
  12.7 13.6 %copy-start.1 = (f32[16,2,4,16,128]{4,3,2,1,0:T(8,128)S(1)}, f32[16,2,4,16,128]{4,3,2,1,0:T(8,128)}, u32[]{:S(2)}) copy-start(f32[16,2,4,16,128]{4,3,2,1,0:T(8,128)} %param.10) | copy-start | bytes 3145732
  13.5 13.0 %collective-permute-start.1 = (f32[16,3,1,16,128]{4,3,0,2,1:T(8,128)}, f32[16,3,1,16,128]{4,3,0,2,1:T(8,128)S(1)}, u32[]{:S(2)}, u32[]{:S(2)}) collective-permute-start(f32[16,3,1,16,128]{4,3,0,2,1:T(8,128)} %pad_maximum_fusion.12), channel_id=1, source_target_pairs={{1,0},{2,1},{3,2},{4,3},{5,4},{6,5},{7,6},{8,7},{9,8},{10,9},{11,1... | collective-permute-start | bytes 1179656 | tf_op jit(solution)/shard_map/ppermute | solution.py:156
  15.6 11.3 %collective-permute-start = (f32[16,3,1,16,128]{4,3,0,2,1:T(8,128)}, f32[16,3,1,16,128]{4,3,0,2,1:T(8,128)}, u32[]{:S(2)}, u32[]{:S(2)}) collective-permute-start(f32[16,3,1,16,128]{4,3,0,2,1:T(8,128)} %pad_maximum_fusion.11), channel_id=1, source_target_pairs={{0,1},{1,2},{2,3},{3,4},{4,5},{5,6},{6,7},{7,8},{8,9},{9,10},{10,1... | collective-permute-start | bytes 1179656 | tf_op jit(solution)/shard_map/ppermute | solution.py:155
  25.7 45.5 %copy-start.52 = (f32[128]{0:T(128)}, f32[128]{0:T(128)S(1)}, u32[]{:S(2)}) copy-start(f32[128]{0:T(128)S(1)} %compare_convert_fusion) | copy-start | bytes 1540
  34.7 41.2 %copy-start.4 = (f32[16,4,16,128]{3,2,1,0:T(8,128)}, f32[16,4,16,128]{3,2,1,0:T(8,128)S(1)}, u32[]{:S(2)}) copy-start(f32[16,4,16,128]{3,2,1,0:T(8,128)S(1)} %fusion.49) | copy-start | bytes 1572868
  35.2 40.7 %copy-start.8 = (f32[16,1,4,16,128]{4,3,2,0,1:T(8,128)}, f32[16,1,4,16,128]{4,3,2,0,1:T(8,128)S(1)}, u32[]{:S(2)}) copy-start(f32[16,1,4,16,128]{4,3,2,0,1:T(8,128)S(1)} %fusion.46) | copy-start | bytes 1572868
  35.2 35.9 %copy-start.56 = (f32[16]{0:T(128)S(1)}, f32[16]{0:T(128)}, u32[]{:S(2)}) copy-start(f32[16]{0:T(128)} %copy-done.55) | copy-start | bytes 196
  64.8 33.7 %copy-start.60 = (f32[2,16]{1,0:T(2,128)}, f32[2,16]{1,0:T(2,128)S(1)}, u32[]{:S(2)}) copy-start(f32[2,16]{1,0:T(2,128)S(1)} %psum.71) | copy-start | bytes 388
  65.1 10.4 %copy-start.12 = (f32[16,2,4,16,128]{4,3,2,0,1:T(8,128)}, f32[16,2,4,16,128]{4,3,2,0,1:T(8,128)S(1)}, u32[]{:S(2)}) copy-start(f32[16,2,4,16,128]{4,3,2,0,1:T(8,128)S(1)} %multiply_subtract_fusion.2) | copy-start | bytes 3145732
  65.4 8.1 %collective-permute-start.2 = (f32[16,1,16,128]{3,2,1,0:T(8,128)S(1)}, f32[16,1,16,128]{3,2,1,0:T(8,128)S(1)}, u32[]{:S(2)}, u32[]{:S(2)}) collective-permute-start(f32[16,1,16,128]{3,2,1,0:T(8,128)S(1)} %get-tuple-element.69), channel_id=1, source_target_pairs={{1,0},{2,1},{3,2},{4,3},{5,4},{6,5},{7,6},{8,7},{9,8},{10,9},{11,1... | collective-permute-start | bytes 393224 | tf_op jit(solution)/shard_map/ppermute | solution.py:173
  66.9 6.6 %collective-permute-start.3 = (f32[16,1,16,128]{3,2,1,0:T(8,128)S(1)}, f32[16,1,16,128]{3,2,1,0:T(8,128)S(1)}, u32[]{:S(2)}, u32[]{:S(2)}) collective-permute-start(f32[16,1,16,128]{3,2,1,0:T(8,128)S(1)} %get-tuple-element.70), channel_id=1, source_target_pairs={{0,1},{1,2},{2,3},{3,4},{4,5},{5,6},{6,7},{7,8},{8,9},{9,10},{10,1... | collective-permute-start | bytes 393224 | tf_op jit(solution)/shard_map/ppermute | solution.py:172
  99.1 10.4 %copy-start.64 = (f32[16]{0:T(128)}, f32[16]{0:T(128)S(1)}, u32[]{:S(2)}) copy-start(f32[16]{0:T(128)S(1)} %get-tuple-element.96) | copy-start | bytes 196
  99.1 8.7 %copy-start.15 = (f32[16,4,16,128]{3,2,1,0:T(8,128)S(1)}, f32[16,4,16,128]{3,2,1,0:T(8,128)}, u32[]{:S(2)}) copy-start(f32[16,4,16,128]{3,2,1,0:T(8,128)} %copy-done.13) | copy-start | bytes 1572868
  99.1 8.7 %copy-start.19 = (f32[16,4,16,128]{3,2,1,0:T(8,128)S(1)}, f32[16,4,16,128]{3,2,1,0:T(8,128)}, u32[]{:S(2)}) copy-start(f32[16,4,16,128]{3,2,1,0:T(8,128)} %copy-done.17) | copy-start | bytes 1572868
  99.2 8.7 %copy-start.30 = (f32[16,4,16,128]{3,2,1,0:T(8,128)S(1)}, f32[16,4,16,128]{3,2,1,0:T(8,128)}, u32[]{:S(2)}) copy-start(f32[16,4,16,128]{3,2,1,0:T(8,128)} %get-tuple-element.30) | copy-start | bytes 1572868
  99.2 8.7 %copy-start.33 = (f32[16,4,16,128]{3,2,1,0:T(8,128)S(1)}, f32[16,4,16,128]{3,2,1,0:T(8,128)}, u32[]{:S(2)}) copy-start(f32[16,4,16,128]{3,2,1,0:T(8,128)} %get-tuple-element.50) | copy-start | bytes 1572868
  99.2 8.7 %copy-start.53 = (f32[128]{0:T(128)S(1)}, f32[128]{0:T(128)}, u32[]{:S(2)}) copy-start(f32[128]{0:T(128)} %copy-done.52) | copy-start | bytes 1540
  102.3 6.6 %collective-permute-start.4 = (f32[16,1,16,128]{3,2,1,0:T(8,128)S(1)}, f32[16,1,16,128]{3,2,1,0:T(8,128)S(1)}, u32[]{:S(2)}, u32[]{:S(2)}) collective-permute-start(f32[16,1,16,128]{3,2,1,0:T(8,128)S(1)} %get-tuple-element.67), channel_id=1, source_target_pairs={{1,0},{2,1},{3,2},{4,3},{5,4},{6,5},{7,6},{8,7},{9,8},{10,9},{11,1... | collective-permute-start | bytes 393224 | tf_op jit(solution)/shard_map/ppermute | solution.py:173
  103.6 5.9 %collective-permute-start.5 = (f32[16,1,16,128]{3,2,1,0:T(8,128)S(1)}, f32[16,1,16,128]{3,2,1,0:T(8,128)S(1)}, u32[]{:S(2)}, u32[]{:S(2)}) collective-permute-start(f32[16,1,16,128]{3,2,1,0:T(8,128)S(1)} %get-tuple-element.68), channel_id=1, source_target_pairs={{0,1},{1,2},{2,3},{3,4},{4,5},{5,6},{6,7},{7,8},{8,9},{9,10},{10,1... | collective-permute-start | bytes 393224 | tf_op jit(solution)/shard_map/ppermute | solution.py:172
  138.1 10.9 %copy-start.62 = (f32[16]{0:T(128)}, f32[16]{0:T(128)S(1)}, u32[]{:S(2)}) copy-start(f32[16]{0:T(128)S(1)} %get-tuple-element.89) | copy-start | bytes 196
  138.8 12.6 %copy-start.49 = (f32[16]{0:T(128)}, f32[16]{0:T(128)S(1)}, u32[]{:S(2)}) copy-start(f32[16]{0:T(128)S(1)} %sqrt_bitcast_fusion.1) | copy-start | bytes 196
  138.8 8.2 %copy-start.20 = (f32[16,4,16,128]{3,2,1,0:T(8,128)S(1)}, f32[16,4,16,128]{3,2,1,0:T(8,128)}, u32[]{:S(2)}) copy-start(f32[16,4,16,128]{3,2,1,0:T(8,128)} %copy-done.17) | copy-start | bytes 1572868
  138.8 8.2 %copy-start.31 = (f32[16,4,16,128]{3,2,1,0:T(8,128)S(1)}, f32[16,4,16,128]{3,2,1,0:T(8,128)}, u32[]{:S(2)}) copy-start(f32[16,4,16,128]{3,2,1,0:T(8,128)} %get-tuple-element.30) | copy-start | bytes 1572868
  138.8 8.2 %copy-start.34 = (f32[16,4,16,128]{3,2,1,0:T(8,128)S(1)}, f32[16,4,16,128]{3,2,1,0:T(8,128)}, u32[]{:S(2)}) copy-start(f32[16,4,16,128]{3,2,1,0:T(8,128)} %get-tuple-element.50) | copy-start | bytes 1572868
  141.3 10.0 %copy-start.7 = (f32[16,2,4,16,128]{4,3,2,1,0:T(8,128)}, f32[16,2,4,16,128]{4,3,2,1,0:T(8,128)S(1)}, u32[]{:S(2)}) copy-start(f32[16,2,4,16,128]{4,3,2,1,0:T(8,128)S(1)} %copy_subtract_fusion) | copy-start | bytes 3145732
  141.7 6.4 %collective-permute-start.6 = (f32[16,1,16,128]{3,2,1,0:T(8,128)S(1)}, f32[16,1,16,128]{3,2,1,0:T(8,128)S(1)}, u32[]{:S(2)}, u32[]{:S(2)}) collective-permute-start(f32[16,1,16,128]{3,2,1,0:T(8,128)S(1)} %get-tuple-element.65), channel_id=1, source_target_pairs={{1,0},{2,1},{3,2},{4,3},{5,4},{6,5},{7,6},{8,7},{9,8},{10,9},{11,1... | collective-permute-start | bytes 393224 | tf_op jit(solution)/shard_map/ppermute | solution.py:173
  143.0 5.9 %collective-permute-start.7 = (f32[16,1,16,128]{3,2,1,0:T(8,128)S(1)}, f32[16,1,16,128]{3,2,1,0:T(8,128)S(1)}, u32[]{:S(2)}, u32[]{:S(2)}) collective-permute-start(f32[16,1,16,128]{3,2,1,0:T(8,128)S(1)} %get-tuple-element.66), channel_id=1, source_target_pairs={{0,1},{1,2},{2,3},{3,4},{4,5},{5,6},{6,7},{7,8},{8,9},{9,10},{10,1... | collective-permute-start | bytes 393224 | tf_op jit(solution)/shard_map/ppermute | solution.py:172
  152.3 42.8 %copy-start.51 = (f32[4,16]{1,0:T(4,128)S(1)}, f32[4,16]{1,0:T(4,128)}, u32[]{:S(2)}) copy-start(f32[4,16]{1,0:T(4,128)} %psum.75) | copy-start | bytes 772
  152.3 42.8 %copy-start.59 = (f32[3,16]{1,0:T(4,128)S(1)}, f32[3,16]{1,0:T(4,128)}, u32[]{:S(2)}) copy-start(f32[3,16]{1,0:T(4,128)} %copy-done.58) | copy-start | bytes 580
  152.3 42.8 %copy-start.61 = (f32[2,16]{1,0:T(2,128)S(1)}, f32[2,16]{1,0:T(2,128)}, u32[]{:S(2)}) copy-start(f32[2,16]{1,0:T(2,128)} %copy-done.60) | copy-start | bytes 388
  152.3 42.8 %copy-start.63 = (f32[16]{0:T(128)S(1)}, f32[16]{0:T(128)}, u32[]{:S(2)}) copy-start(f32[16]{0:T(128)} %copy-done.62) | copy-start | bytes 196
  152.4 42.8 %copy-start.65 = (f32[16]{0:T(128)S(1)}, f32[16]{0:T(128)}, u32[]{:S(2)}) copy-start(f32[16]{0:T(128)} %copy-done.64) | copy-start | bytes 196
  152.4 42.8 %copy-start.68 = (f32[16]{0:T(128)S(1)}, f32[16]{0:T(128)}, u32[]{:S(2)}) copy-start(f32[16]{0:T(128)} %get-tuple-element.95) | copy-start | bytes 196
  152.4 42.9 %copy-start.50 = (f32[16]{0:T(128)S(1)}, f32[16]{0:T(128)}, u32[]{:S(2)}) copy-start(f32[16]{0:T(128)} %copy-done.49) | copy-start | bytes 196
  197.6 18.5 %copy-start.69 = (f32[256]{0:T(256)S(1)}, f32[256]{0:T(256)}, u32[]{:S(2)}) copy-start(f32[256]{0:T(256)} %param.16) | copy-start | bytes 3076
  197.7 96.6 %copy-start.70 = (f32[256]{0:T(256)S(1)}, f32[256]{0:T(256)}, u32[]{:S(2)}) copy-start(f32[256]{0:T(256)} %param.15) | copy-start | bytes 3076
  197.8 98.1 %copy-start.22 = (f32[16,4,16,128]{3,2,1,0:T(8,128)S(1)}, f32[16,4,16,128]{3,2,1,0:T(8,128)}, u32[]{:S(2)}) copy-start(f32[16,4,16,128]{3,2,1,0:T(8,128)} %param.11) | copy-start | bytes 1572868
  199.6 2.7 collective-permute-start.8
  202.3 3.5 %collective-permute-start.9 = (f32[16,256]{1,0:T(8,128)S(1)}, f32[16,256]{1,0:T(8,128)S(1)}, u32[]{:S(2)}, u32[]{:S(2)}) collective-permute-start(f32[16,256]{1,0:T(8,128)S(1)} %add.479), channel_id=1, source_target_pairs={{0,2},{1,3},{2,0},{3,1},{4,6},{5,7},{6,4},{7,5},{8,10},{9,11},{10,... | collective-permute-start | bytes 49160 | tf_op jit(solution)/shard_map/ppermute | solution.py:29
  205.8 6.7 %collective-permute-start.10 = (f32[16,256]{1,0:T(8,128)S(1)}, f32[16,256]{1,0:T(8,128)S(1)}, u32[]{:S(2)}, u32[]{:S(2)}) collective-permute-start(f32[16,256]{1,0:T(8,128)S(1)} %add.480), channel_id=1, source_target_pairs={{0,4},{1,5},{2,6},{3,7},{4,0},{5,1},{6,2},{7,3},{8,12},{9,13},{10,... | collective-permute-start | bytes 49160 | tf_op jit(solution)/shard_map/ppermute | solution.py:29
  212.5 2.6 collective-permute-start.11
  215.1 4.1 %collective-permute-start.12 = (f32[16,256]{1,0:T(8,128)S(1)}, f32[16,256]{1,0:T(8,128)S(1)}, u32[]{:S(2)}, u32[]{:S(2)}) collective-permute-start(f32[16,256]{1,0:T(8,128)S(1)} %add.482), channel_id=1, source_target_pairs={{0,16},{8,24},{16,0},{24,8},{1,17},{9,25},{17,1},{25,9},{2,18},{10... | collective-permute-start | bytes 49160 | tf_op jit(solution)/shard_map/ppermute | solution.py:29
  (38 other events, 120.2 us)
Sparse Core Ops, SparseCore 0:
  9.9 38.7 all-gather.2
  50.5 34.5 all-gather.4
